TPU v7x, 512 devices: a whole 4x8x8 slice. The times are simulated.
512 devices in a mesh: ctx: 64 (over x, y, core), fsdp: 8 (over z).
Axes of the slice: x: 4, y: 8, z: 8, core: 2. Of those that a mesh axis runs over, the one named last changes fastest.
Arguments:
- outer_gate: bfloat16 [2048, 16384], P('fsdp', 'ctx'), may hold values from -6 to 6
- inner_gate: bfloat16 [2048, 16384], P('fsdp', 'ctx'), may hold values from -6 to 6
- value_stream: bfloat16 [2048, 16384], P('fsdp', 'ctx'), may hold values from -6 to 6
- grad_output: bfloat16 [2048, 16384], P('fsdp', 'ctx'), may hold values from -6 to 6
- filters: float32 [128, 128], P('fsdp', 'ctx'), may hold values from -0.5 to 0.5
- feature_taps: float32 [3, 3, 2048], P(None, None, ('ctx', 'fsdp')), may hold values from -3 to 3
- skip_gain: float32 [2048], P(('ctx', 'fsdp')), may hold values from -4 to 4
Outputs:
- gated_out: bfloat16 [2048, 16384], P('fsdp', 'ctx')
- grad_outer: bfloat16 [2048, 16384], P('fsdp', 'ctx')
- grad_inner: bfloat16 [2048, 16384], P('fsdp', 'ctx')
- grad_value: bfloat16 [2048, 16384], P('fsdp', 'ctx')
- grad_filters: float32 [128, 128], P('fsdp', 'ctx')
- grad_taps: float32 [3, 3, 2048], P(None, None, ('ctx', 'fsdp'))
- grad_skip: float32 [2048], P(('ctx', 'fsdp'))
All inputs are finite; a program needn't handle non-finite values.
Results may differ from a plain program's by a relative error of at most 0.03.
Values may be sent and summed in bfloat16 or wider, within the bound.
No kernel may reach another device: no remote copies, remote signals or barrier semaphores. Data moves between devices by JAX's collectives and lax.ppermute only.
A program may use at most 64 MiB of HBM per device.

v0:
```python
import math

import jax
import jax.numpy as jnp
from jax import lax
from jax.sharding import PartitionSpec as P


def passed_along(shard, axis, by):
    devices = lax.axis_size(axis)
    pairs = [(i, i + by) for i in range(devices) if 0 <= i + by < devices]
    return lax.ppermute(shard, axis, pairs)


def featurize(extended, tap_gains):
    out_len = extended.shape[1] - 2
    result = tap_gains[0][:, None] * extended[:, 2:]
    result = result + tap_gains[1][:, None] * extended[:, 1 : out_len + 1]
    return result + tap_gains[2][:, None] * extended[:, :out_len]


def carry_back(extended, tap_gains):
    out_len = extended.shape[1] - 2
    result = tap_gains[0][:, None] * extended[:, :out_len]
    result = result + tap_gains[1][:, None] * extended[:, 1 : out_len + 1]
    return result + tap_gains[2][:, None] * extended[:, 2:]


def tap_sums(grad_rows, extended):
    block_len = grad_rows.shape[1]
    weighted = grad_rows.astype(jnp.float32)
    return jnp.stack(
        [
            jnp.sum(
                weighted * extended[:, 2 - shift_by : 2 - shift_by + block_len].astype(jnp.float32),
                axis=1,
            )
            for shift_by in range(3)
        ]
    )


def toeplitz_rows(filters_low, out_len):
    groups, taps_count = filters_low.shape
    window = out_len + taps_count - 1
    filter_row = jnp.concatenate(
        [filters_low[:, ::-1], jnp.zeros((groups, window + 1 - taps_count), filters_low.dtype)],
        axis=1,
    )
    flattened = jnp.tile(filter_row, (1, out_len))[:, : out_len * window]
    return flattened.reshape(groups, out_len, window)


def skew_sum(cross_terms, taps_count):
    groups, block_len, window = cross_terms.shape
    flattened = jnp.pad(cross_terms.reshape(groups, block_len * window), ((0, 0), (0, block_len)))
    return jnp.sum(flattened.reshape(groups, block_len, window + 1)[:, :, :taps_count], axis=1)[
        :, ::-1
    ]


def regroup_target(lin, fsdp_size):
    i, j = divmod(lin, fsdp_size)
    return (fsdp_size * (i % fsdp_size) + j) * fsdp_size + i // fsdp_size


def shards(outer_gate, inner_gate, value_stream, grad_output, filters, feature_taps, skip_gain):
    channels, block_len = outer_gate.shape
    ctx_size = lax.axis_size("ctx")
    fsdp_size = lax.axis_size("fsdp")
    n_dev = ctx_size * fsdp_size
    groups, taps_here = filters.shape
    taps_count = taps_here * ctx_size
    reach_cols = taps_count - 1
    group_size = channels // groups
    chunk = feature_taps.shape[2]

    param_pack = jnp.concatenate([feature_taps.reshape(-1), skip_gain])
    regrouped = lax.ppermute(
        param_pack,
        ("ctx", "fsdp"),
        [(k, regroup_target(k, fsdp_size)) for k in range(n_dev)],
    )
    row = jnp.concatenate([filters.reshape(-1), regrouped])
    gathered = lax.all_to_all(
        jnp.broadcast_to(row[None], (ctx_size, row.shape[0])), "ctx", 0, 0, tiled=True
    )
    n_filt = groups * taps_here
    filters_all = (
        gathered[:, :n_filt]
        .reshape(ctx_size, groups, taps_here)
        .transpose(1, 0, 2)
        .reshape(groups, taps_count)
    )
    taps_all = (
        gathered[:, n_filt : n_filt + 9 * chunk]
        .reshape(ctx_size, 3, 3, chunk)
        .transpose(1, 2, 0, 3)
        .reshape(3, 3, channels)
    )
    skip_all = gathered[:, n_filt + 9 * chunk :].reshape(channels)

    rim = reach_cols + 2
    prev_rim = passed_along(
        jnp.concatenate(
            [outer_gate[:, block_len - 2 :], inner_gate[:, block_len - rim :], value_stream[:, block_len - rim :]],
            axis=1,
        ),
        "ctx",
        1,
    )
    next_rim = passed_along(
        jnp.concatenate(
            [grad_output[:, :rim], outer_gate[:, :rim], inner_gate[:, :2], value_stream[:, :2]], axis=1
        ),
        "ctx",
        -1,
    )
    outer_ext = jnp.concatenate([prev_rim[:, :2], outer_gate, next_rim[:, rim : 2 * rim]], axis=1)
    inner_ext = jnp.concatenate(
        [prev_rim[:, 2 : 2 + rim], inner_gate, next_rim[:, 2 * rim : 2 * rim + 2]], axis=1
    )
    value_ext = jnp.concatenate([prev_rim[:, 2 + rim :], value_stream, next_rim[:, 2 * rim + 2 :]], axis=1)
    upstream = jnp.concatenate([grad_output, next_rim[:, :rim]], axis=1).astype(jnp.float32)

    outer_feat = featurize(outer_ext.astype(jnp.float32), taps_all[0])
    inner_feat = featurize(inner_ext.astype(jnp.float32), taps_all[1])
    value_feat = featurize(value_ext.astype(jnp.float32), taps_all[2])
    product = (inner_feat * value_feat).astype(jnp.bfloat16)

    out_len = block_len + 2
    toeplitz = toeplitz_rows(filters_all.astype(jnp.bfloat16), out_len)
    windows = product.reshape(groups, group_size, out_len + reach_cols)
    convolved = jnp.einsum(
        "gcs,gts->gct", windows, toeplitz, preferred_element_type=jnp.float32
    ).reshape(channels, out_len)
    product_here = product[:, reach_cols:].astype(jnp.float32)
    mixed = convolved + skip_all[:, None] * product_here
    gated_out = (outer_feat[:, :block_len] * mixed[:, :block_len]).astype(jnp.bfloat16)

    grad_mixed = (upstream * outer_feat).astype(jnp.bfloat16)
    grad_outer_feat = (upstream[:, :out_len] * mixed).astype(jnp.bfloat16)
    gm_windows = grad_mixed[:, ::-1].reshape(groups, group_size, out_len + reach_cols)
    ahead = jnp.einsum(
        "gcs,gts->gct", gm_windows, toeplitz, preferred_element_type=jnp.float32
    ).reshape(channels, out_len)[:, ::-1]
    grad_product = ahead + skip_all[:, None] * grad_mixed[:, :out_len].astype(jnp.float32)
    grad_inner_feat = (grad_product * value_feat[:, reach_cols:]).astype(jnp.bfloat16)
    grad_value_feat = (grad_product * inner_feat[:, reach_cols:]).astype(jnp.bfloat16)

    grad_outer = carry_back(grad_outer_feat.astype(jnp.float32), taps_all[0])
    grad_inner = carry_back(grad_inner_feat.astype(jnp.float32), taps_all[1])
    grad_value = carry_back(grad_value_feat.astype(jnp.float32), taps_all[2])

    grad_scale = 1.0 / math.sqrt(ctx_size * block_len)
    gm_here = grad_mixed[:, :block_len]
    cross_terms = jnp.einsum(
        "gct,gcs->gts",
        gm_here.reshape(groups, group_size, block_len),
        product[:, : block_len + reach_cols].reshape(groups, group_size, block_len + reach_cols),
        preferred_element_type=jnp.float32,
    )
    filter_part = grad_scale * skew_sum(cross_terms, taps_count)
    skip_part = grad_scale * jnp.sum(
        gm_here.astype(jnp.float32) * product_here[:, :block_len], axis=1
    )
    taps_part = grad_scale * jnp.stack(
        [
            tap_sums(grad_outer_feat[:, :block_len], outer_ext[:, : block_len + 2]),
            tap_sums(grad_inner_feat[:, :block_len], inner_ext[:, reach_cols : reach_cols + block_len + 2]),
            tap_sums(grad_value_feat[:, :block_len], value_ext[:, reach_cols : reach_cols + block_len + 2]),
        ]
    )

    send = jnp.concatenate(
        [
            filter_part.reshape(groups, ctx_size, taps_here).transpose(1, 0, 2).reshape(ctx_size, -1),
            taps_part.reshape(3, 3, ctx_size, chunk).transpose(2, 0, 1, 3).reshape(ctx_size, -1),
            skip_part.reshape(ctx_size, chunk),
        ],
        axis=1,
    )
    reduced = jnp.sum(lax.all_to_all(send, "ctx", 0, 0, tiled=True), axis=0)
    filter_share = reduced[:n_filt].reshape(groups, taps_here)
    back = lax.ppermute(
        reduced[n_filt:],
        ("ctx", "fsdp"),
        [(regroup_target(k, fsdp_size), k) for k in range(n_dev)],
    )
    taps_share = back[: 9 * chunk].reshape(3, 3, chunk)
    skip_share = back[9 * chunk :]
    return (
        gated_out,
        grad_outer.astype(jnp.bfloat16),
        grad_inner.astype(jnp.bfloat16),
        grad_value.astype(jnp.bfloat16),
        filter_share,
        taps_share,
        skip_share,
    )


def solution(mesh):
    return jax.shard_map(
        shards,
        mesh=mesh,
        in_specs=(
            P("fsdp", "ctx"),
            P("fsdp", "ctx"),
            P("fsdp", "ctx"),
            P("fsdp", "ctx"),
            P("fsdp", "ctx"),
            P(None, None, ("ctx", "fsdp")),
            P(("ctx", "fsdp")),
        ),
        out_specs=(
            P("fsdp", "ctx"),
            P("fsdp", "ctx"),
            P("fsdp", "ctx"),
            P("fsdp", "ctx"),
            P("fsdp", "ctx"),
            P(None, None, ("ctx", "fsdp")),
            P(("ctx", "fsdp")),
        ),
        check_vma=False,
    )
```

profile of v0, /device:TPU:5, one launch (start us, length us, event | category | flops | bytes accessed | tf_op | source)
XLA Modules:
  0.0 144.9 jit_solution(2409700622174463150)
XLA Ops:
  0.6 0.8 reshape.154
  1.4 0.7 pad_maximum_fusion.5
  2.1 16.4 %collective-permute-start = (f32[40]{0:T(128)S(1)}, f32[40]{0:T(128)S(1)}, u32[]{:S(2)}, u32[]{:S(2)}) collective-permute-start(f32[40]{0:T(128)S(1)} %pad_maximum_fusion.5), channel_id=1, source_target_pairs={{0,0},{1,8},{2,16},{3,24},{4,32},{5,40},{6,48},{7,56},{8,64},{9,72... | collective-permute-start | bytes 488 | tf_op jit(solution)/shard_map/ppermute | solution.py:79
  18.5 0.9 slice.270
  19.5 1.0 slice.271
  20.5 1.0 slice.272
  21.5 0.8 pad_maximum_fusion
  22.3 1.9 %collective-permute-start.1 = (bf16[256,260]{1,0:T(8,128)(2,1)}, bf16[256,260]{1,0:T(8,128)(2,1)S(1)}, u32[]{:S(2)}, u32[]{:S(2)}) collective-permute-start(bf16[256,260]{1,0:T(8,128)(2,1)} %pad_maximum_fusion), channel_id=1, source_target_pairs={{0,8},{8,16},{16,24},{24,32},{32,40},{40,48},{48,56},{56,64},{64,7... | collective-permute-start | bytes 399368 | tf_op jit(solution)/shard_map/ppermute | solution.py:12
  24.3 0.8 slice.276
  25.1 0.8 slice.277
  25.9 0.8 copy.33
  27.5 6.3 %all-to-all-start = ((f32[64,1,72]{2,1,0:T(1,128)}), f32[64,1,72]{2,1,0:T(1,128)S(1)}, u32[]{:S(2)}, u32[]{:S(2)}) async-start(f32[64,1,72]{2,1,0:T(1,128)} %broadcast_in_dim.2), calls=%async_computation | async-start | bytes 65536 | tf_op jit(solution)/shard_map/all_to_all | solution.py:85
  33.8 1.8 %pad_maximum_fusion.1 = bf16[256,262]{1,0:T(8,128)(2,1)} fusion(bf16[256,2]{1,0:T(8,128)(2,1)S(1)} %slice.277, bf16[256,2]{1,0:T(8,128)(2,1)S(1)} %slice.276, bf16[256,129]{1,0:T(8,128)(2,1)} %bitcast.62, bf16[256,129]{1,0:T(8,128)(2,1)} %bitcast.64), kind=kLoop, calls=%fused_computation.76 | loop fusion | flops 536576 | bytes 268288 | tf_op jit(solution)/shard_map/concatenate | solution.py:113
  35.6 2.3 %collective-permute-start.2 = (bf16[256,262]{1,0:T(8,128)(2,1)}, bf16[256,262]{1,0:T(8,128)(2,1)}, u32[]{:S(2)}, u32[]{:S(2)}) collective-permute-start(bf16[256,262]{1,0:T(8,128)(2,1)} %pad_maximum_fusion.1), channel_id=1, source_target_pairs={{8,0},{16,8},{24,16},{32,24},{40,32},{48,40},{56,48},{64,56},{72,6... | collective-permute-start | bytes 402440 | tf_op jit(solution)/shard_map/ppermute | solution.py:12
  37.9 3.3 %all-to-all-done = f32[64,1,72]{2,1,0:T(1,128)S(1)} async-done(((f32[64,1,72]{2,1,0:T(1,128)}), f32[64,1,72]{2,1,0:T(1,128)S(1)}, u32[]{:S(2)}, u32[]{:S(2)}) %all-to-all-start) | async-done | bytes 18464 | tf_op jit(solution)/shard_map/all_to_all | solution.py:85
  44.3 0.7 mul.264
  45.1 0.7 mul.261
  45.9 0.7 mul.258
  47.0 2.3 %tile.4 = bf16[16,258,386]{2,1,0:T(8,128)(2,1)} broadcast(bf16[16,386]{1,0:T(8,128)(2,1)S(1)} %concatenate.50.clone), dimensions={0,2} | broadcast | bytes 3199168 | tf_op jit(solution)/shard_map/tile | solution.py:50
  49.3 6.8 %tile.10 = bf16[16,99588]{1,0:T(8,128)(2,1)S(1)} reshape(bf16[16,258,386]{2,1,0:T(8,128)(2,1)} %tile.4) | data formatting | bytes 6373632 | tf_op jit(solution)/shard_map/tile | solution.py:50
  56.1 1.9 %slice.364 = bf16[16,99330]{1,0:T(8,128)(2,1)} slice(bf16[16,99588]{1,0:T(8,128)(2,1)S(1)} %tile.10), slice={[0:16], [0:99330]} | slice | bytes 6357120 | tf_op jit(solution)/shard_map/slice | solution.py:50
  58.0 11.1 %reshape.157 = bf16[16,258,385]{2,1,0:T(8,128)(2,1)} reshape(bf16[16,99330]{1,0:T(8,128)(2,1)} %slice.364) | data formatting | bytes 6357120 | tf_op jit(solution)/shard_map/reshape | solution.py:51
  69.7 1.2 fusion.43
  70.9 1.0 fusion.44
  72.3 0.9 multiply_convert_fusion.1
  73.2 0.7 slice.383
  74.0 1.1 fusion.42
  75.4 1.3 multiply_convert_fusion
  77.3 0.8 reverse
  78.2 0.8 slice.524
  79.9 3.6 %fusion.47 = f32[16,16,258]{2,1,0:T(8,128)S(1)} fusion(bf16[16,16,385]{2,1,0:T(8,128)(2,1)} %bitcast.65, bf16[16,258,385]{2,1,0:T(8,128)(2,1)} %reshape.157), kind=kOutput, calls=%fused_computation.101 | convolution fusion | flops 50856960 | bytes 3639872 | tf_op jit(solution)/shard_map/gcs,gts->gct/dot_general | solution.py:144
  83.5 4.3 %fusion.46 = f32[16,16,258]{2,1,0:T(8,128)} fusion(bf16[16,16,385]{2,1,0:T(8,128)(2,1)S(1)} %bitcast.61, bf16[16,258,385]{2,1,0:T(8,128)(2,1)} %reshape.157), kind=kOutput, calls=%fused_computation.100 | convolution fusion | flops 50856960 | bytes 3639872 | tf_op jit(solution)/shard_map/gcs,gts->gct/dot_general | solution.py:134
  88.5 1.0 fusion.33
  89.6 1.3 fusion.35
  91.2 1.6 %fusion.23 = bf16[256,256]{1,0:T(8,128)(2,1)} fusion(f32[256,258]{1,0:T(8,128)S(1)} %get-tuple-element.40, f32[256]{0:T(256)} %mul.264, f32[256]{0:T(256)} %mul.261, f32[256]{0:T(256)} %mul.258), kind=kLoop, calls=%fused_computation.54 | loop fusion | flops 393216 | bytes 920576 | tf_op jit(solution)/shard_map/convert_element_type | solution.py:195
  93.2 1.7 %fusion.20 = bf16[256,256]{1,0:T(8,128)(2,1)} fusion(f32[256,258]{1,0:T(8,128)S(1)} %get-tuple-element.37, f32[256]{0:T(256)S(1)} %mul.273, f32[256]{0:T(256)} %mul.270, f32[256]{0:T(256)} %mul.267), kind=kLoop, calls=%fused_computation.48 | loop fusion | flops 393216 | bytes 920576 | tf_op jit(solution)/shard_map/convert_element_type | solution.py:196
  97.0 3.7 %fusion.48 = f32[16,256,383]{2,1,0:T(8,128)} fusion(bf16[16,16,256]{2,1,0:T(8,128)(2,1)S(1)} %bitcast.67, bf16[16,16,383]{2,1,0:T(8,128)(2,1)S(1)} %bitcast.66), kind=kOutput, calls=%fused_computation.102 | convolution fusion | flops 50200576 | bytes 6602240 | tf_op jit(solution)/shard_map/gct,gcs->gts/dot_general | solution.py:157
  100.7 6.9 %reshape.163 = f32[16,98048]{1,0:T(8,128)} reshape(f32[16,256,383]{2,1,0:T(8,128)} %fusion.48) | data formatting | bytes 12550144 | tf_op jit(solution)/shard_map/reshape | solution.py:56
  107.6 3.2 %pad.5 = f32[16,98304]{1,0:T(8,128)S(1)} pad(f32[16,98048]{1,0:T(8,128)} %reshape.163, f32[]{:T(128)} %constant.4.clone.1), padding=0_0x0_256 | pad | bytes 12566532 | tf_op jit(solution)/shard_map/jit(_pad)/pad | solution.py:56
  110.8 1.2 copy.62
  112.4 0.7 copy.59
  113.1 7.0 %all-to-all-start.1 = ((f32[64,1,72]{2,1,0:T(1,128)}), f32[64,1,72]{2,1,0:T(1,128)S(1)}, u32[]{:S(2)}, u32[]{:S(2)}) async-start(f32[64,1,72]{2,1,0:T(1,128)} %copy.59), calls=%async_computation.1 | async-start | bytes 65536 | tf_op jit(solution)/shard_map/all_to_all | solution.py:183
  120.1 0.7 fusion.28
  120.8 1.0 fusion.26
  121.8 5.7 %all-to-all-done.1 = f32[64,1,72]{2,1,0:T(1,128)S(1)} async-done(((f32[64,1,72]{2,1,0:T(1,128)}), f32[64,1,72]{2,1,0:T(1,128)S(1)}, u32[]{:S(2)}, u32[]{:S(2)}) %all-to-all-start.1) | async-done | bytes 18464 | tf_op jit(solution)/shard_map/all_to_all | solution.py:183
  127.7 4.8 %collective-permute-start.3 = (f32[40]{0:T(128)S(1)}, f32[40]{0:T(128)S(1)}, u32[]{:S(2)}, u32[]{:S(2)}) collective-permute-start(f32[40]{0:T(128)S(1)} %slice.334), channel_id=1, source_target_pairs={{0,0},{8,1},{16,2},{24,3},{32,4},{40,5},{48,6},{56,7},{64,8},{72,9... | collective-permute-start | bytes 488 | tf_op jit(solution)/shard_map/ppermute | solution.py:185
  133.2 10.4 %collective-permute-done.3 = f32[40]{0:T(128)S(1)} collective-permute-done((f32[40]{0:T(128)S(1)}, f32[40]{0:T(128)S(1)}, u32[]{:S(2)}, u32[]{:S(2)}) %collective-permute-start.3) | collective-permute-done | bytes 192 | tf_op jit(solution)/shard_map/ppermute | solution.py:185
  143.7 0.7 reshape.169
  (110 shorter events, 12.6 us)
Async XLA Ops:
  2.1 24.7 %collective-permute-start = (f32[40]{0:T(128)S(1)}, f32[40]{0:T(128)S(1)}, u32[]{:S(2)}, u32[]{:S(2)}) collective-permute-start(f32[40]{0:T(128)S(1)} %pad_maximum_fusion.5), channel_id=1, source_target_pairs={{0,0},{1,8},{2,16},{3,24},{4,32},{5,40},{6,48},{7,56},{8,64},{9,72... | collective-permute-start | bytes 488 | tf_op jit(solution)/shard_map/ppermute | solution.py:79
  22.3 46.7 %collective-permute-start.1 = (bf16[256,260]{1,0:T(8,128)(2,1)}, bf16[256,260]{1,0:T(8,128)(2,1)S(1)}, u32[]{:S(2)}, u32[]{:S(2)}) collective-permute-start(bf16[256,260]{1,0:T(8,128)(2,1)} %pad_maximum_fusion), channel_id=1, source_target_pairs={{0,8},{8,16},{16,24},{24,32},{32,40},{40,48},{48,56},{56,64},{64,7... | collective-permute-start | bytes 399368 | tf_op jit(solution)/shard_map/ppermute | solution.py:12
  27.5 13.6 %all-to-all-start = ((f32[64,1,72]{2,1,0:T(1,128)}), f32[64,1,72]{2,1,0:T(1,128)S(1)}, u32[]{:S(2)}, u32[]{:S(2)}) async-start(f32[64,1,72]{2,1,0:T(1,128)} %broadcast_in_dim.2), calls=%async_computation | async-start | bytes 65536 | tf_op jit(solution)/shard_map/all_to_all | solution.py:85
  35.6 35.3 %collective-permute-start.2 = (bf16[256,262]{1,0:T(8,128)(2,1)}, bf16[256,262]{1,0:T(8,128)(2,1)}, u32[]{:S(2)}, u32[]{:S(2)}) collective-permute-start(bf16[256,262]{1,0:T(8,128)(2,1)} %pad_maximum_fusion.1), channel_id=1, source_target_pairs={{8,0},{16,8},{24,16},{32,24},{40,32},{48,40},{56,48},{64,56},{72,6... | collective-permute-start | bytes 402440 | tf_op jit(solution)/shard_map/ppermute | solution.py:12
  57.9 14.0 %copy-start.1 = (bf16[256,256]{1,0:T(8,128)(2,1)S(1)}, bf16[256,256]{1,0:T(8,128)(2,1)}, u32[]{:S(2)}) copy-start(bf16[256,256]{1,0:T(8,128)(2,1)} %param.8) | copy-start | bytes 393220
  57.9 14.0 %copy-start.2 = (bf16[256,256]{1,0:T(8,128)(2,1)S(1)}, bf16[256,256]{1,0:T(8,128)(2,1)}, u32[]{:S(2)}) copy-start(bf16[256,256]{1,0:T(8,128)(2,1)} %param.9) | copy-start | bytes 393220
  57.9 14.3 %copy-start.10 = (f32[256]{0:T(256)S(1)}, f32[256]{0:T(256)}, u32[]{:S(2)}) copy-start(f32[256]{0:T(256)} %mul.270) | copy-start | bytes 3076
  57.9 14.3 %copy-start.11 = (f32[256]{0:T(256)S(1)}, f32[256]{0:T(256)}, u32[]{:S(2)}) copy-start(f32[256]{0:T(256)} %mul.267) | copy-start | bytes 3076
  58.0 14.3 %copy-start.12 = (f32[256]{0:T(256)S(1)}, f32[256]{0:T(256)}, u32[]{:S(2)}) copy-start(f32[256]{0:T(256)} %mul.264) | copy-start | bytes 3076
  58.0 14.3 %copy-start.13 = (f32[256]{0:T(256)S(1)}, f32[256]{0:T(256)}, u32[]{:S(2)}) copy-start(f32[256]{0:T(256)} %mul.261) | copy-start | bytes 3076
  58.0 14.3 %copy-start.14 = (f32[256]{0:T(256)S(1)}, f32[256]{0:T(256)}, u32[]{:S(2)}) copy-start(f32[256]{0:T(256)} %mul.258) | copy-start | bytes 3076
  69.0 6.1 %copy-start.3 = (bf16[256,256]{1,0:T(8,128)(2,1)S(1)}, bf16[256,256]{1,0:T(8,128)(2,1)}, u32[]{:S(2)}) copy-start(bf16[256,256]{1,0:T(8,128)(2,1)} %param.10) | copy-start | bytes 393220
  69.1 0.7 copy-start.8
  69.7 7.6 %copy-start.6 = (bf16[256,2]{1,0:T(8,128)(2,1)}, bf16[256,2]{1,0:T(8,128)(2,1)S(1)}, u32[]{:S(2)}) copy-start(bf16[256,2]{1,0:T(8,128)(2,1)S(1)} %slice.339) | copy-start | bytes 3076
  70.9 4.3 %copy-start = (bf16[256,256]{1,0:T(8,128)(2,1)S(1)}, bf16[256,256]{1,0:T(8,128)(2,1)}, u32[]{:S(2)}) copy-start(bf16[256,256]{1,0:T(8,128)(2,1)} %param.7) | copy-start | bytes 393220
  88.5 2.4 %copy-start.7 = (bf16[256,2]{1,0:T(8,128)(2,1)S(1)}, bf16[256,2]{1,0:T(8,128)(2,1)}, u32[]{:S(2)}) copy-start(bf16[256,2]{1,0:T(8,128)(2,1)} %copy-done.6) | copy-start | bytes 3076
  88.5 8.5 %copy-start.5 = (bf16[256,383]{1,0:T(8,128)(2,1)S(1)}, bf16[256,383]{1,0:T(8,128)(2,1)}, u32[]{:S(2)}) copy-start(bf16[256,383]{1,0:T(8,128)(2,1)} %slice.383) | copy-start | bytes 588292
  88.5 8.5 %copy-start.9 = (bf16[256,256]{1,0:T(8,128)(2,1)S(1)}, bf16[256,256]{1,0:T(8,128)(2,1)}, u32[]{:S(2)}) copy-start(bf16[256,256]{1,0:T(8,128)(2,1)} %slice.382) | copy-start | bytes 393220
  110.8 1.6 %copy-start.15 = (f32[64,4]{0,1:T(4,128)S(1)}, f32[64,4]{0,1:T(4,128)}, u32[]{:S(2)}) copy-start(f32[64,4]{0,1:T(4,128)} %copy.58) | copy-start | bytes 3076
  110.8 9.4 %copy-start.4 = (f32[256,385]{1,0:T(8,128)S(1)}, f32[256,385]{1,0:T(8,128)}, u32[]{:S(2)}) copy-start(f32[256,385]{1,0:T(8,128)} %get-tuple-element.43) | copy-start | bytes 1182724
  113.1 14.4 %all-to-all-start.1 = ((f32[64,1,72]{2,1,0:T(1,128)}), f32[64,1,72]{2,1,0:T(1,128)S(1)}, u32[]{:S(2)}, u32[]{:S(2)}) async-start(f32[64,1,72]{2,1,0:T(1,128)} %copy.59), calls=%async_computation.1 | async-start | bytes 65536 | tf_op jit(solution)/shard_map/all_to_all | solution.py:183
  127.7 16.0 %collective-permute-start.3 = (f32[40]{0:T(128)S(1)}, f32[40]{0:T(128)S(1)}, u32[]{:S(2)}, u32[]{:S(2)}) collective-permute-start(f32[40]{0:T(128)S(1)} %slice.334), channel_id=1, source_target_pairs={{0,0},{8,1},{16,2},{24,3},{32,4},{40,5},{48,6},{56,7},{64,8},{72,9... | collective-permute-start | bytes 488 | tf_op jit(solution)/shard_map/ppermute | solution.py:185
where the time goes:
time: 146 us; the launch traced here: 145 us
  local copies, waits for them, and re-layouts  59.1 us (40%)
  starting transfers between devices  38.6 us (26%)
  waiting for transfers between devices  19.5 us (13%)
  other arithmetic  14.9 us (10%)
  matrix products  11.6 us (8%)
    ppermute x1, starting transfers between devices, shards(): lax.ppermute(param_pack, ('ctx', 'fsdp'), [(k, regroup_target(k, fsdp_siz...  16.4 us
    reshape x1, local copies, waits for them, and re-layouts, toeplitz_rows(): return flattened.reshape(groups, out_len, window)  11.1 us
    ppermute x1, waiting for transfers between devices, shards(): lax.ppermute(reduced[n_filt:], ('ctx', 'fsdp'), [(regroup_target(k, fsdp_...  10.4 us
    another operation x2, local copies, waits for them, and re-layouts, toeplitz_rows(): flattened = jnp.tile(filter_row, (1, out_len))[:, :out_len * window]  9.05 us
    all_to_all x1, starting transfers between devices, shards(): reduced = jnp.sum(lax.all_to_all(send, 'ctx', 0, 0, tiled=True), axis=0)  7.01 us
    reshape x1, local copies, waits for them, and re-layouts, skew_sum(): cross_terms.reshape(groups, block_len * window)  6.88 us
    all_to_all x1, starting transfers between devices, shards(): lax.all_to_all(jnp.broadcast_to(row[None], (ctx_size, row.shape[0])), 'ct...  6.3 us
    unnamed x39, local copies, waits for them, and re-layouts  5.77 us
  transfers between devices with their start and end apart: 6, of which 3 were waited for; matrix products, arithmetic and copies ran while one was open for 28% of the time, Pallas kernels for 0%

commit v1 on v0

--- a/solution.py
+++ b/solution.py
@@ -59,6 +59,19 @@
     ]
 
 
+def depthwise(values, kernel):
+    channels = values.shape[0]
+    return lax.conv_general_dilated(
+        values[None],
+        kernel[:, None, :],
+        window_strides=(1,),
+        padding="VALID",
+        dimension_numbers=("NCH", "OIH", "NCH"),
+        feature_group_count=channels,
+        preferred_element_type=jnp.float32,
+    )[0]
+
+
 def regroup_target(lin, fsdp_size):
     i, j = divmod(lin, fsdp_size)
     return (fsdp_size * (i % fsdp_size) + j) * fsdp_size + i // fsdp_size
@@ -129,21 +142,16 @@
     product = (inner_feat * value_feat).astype(jnp.bfloat16)
 
     out_len = block_len + 2
-    toeplitz = toeplitz_rows(filters_all.astype(jnp.bfloat16), out_len)
-    windows = product.reshape(groups, group_size, out_len + reach_cols)
-    convolved = jnp.einsum(
-        "gcs,gts->gct", windows, toeplitz, preferred_element_type=jnp.float32
-    ).reshape(channels, out_len)
+    filters_low = filters_all.astype(jnp.bfloat16)
+    per_channel = jnp.repeat(filters_low, group_size, axis=0)
+    convolved = depthwise(product, per_channel[:, ::-1])
     product_here = product[:, reach_cols:].astype(jnp.float32)
     mixed = convolved + skip_all[:, None] * product_here
     gated_out = (outer_feat[:, :block_len] * mixed[:, :block_len]).astype(jnp.bfloat16)
 
     grad_mixed = (upstream * outer_feat).astype(jnp.bfloat16)
     grad_outer_feat = (upstream[:, :out_len] * mixed).astype(jnp.bfloat16)
-    gm_windows = grad_mixed[:, ::-1].reshape(groups, group_size, out_len + reach_cols)
-    ahead = jnp.einsum(
-        "gcs,gts->gct", gm_windows, toeplitz, preferred_element_type=jnp.float32
-    ).reshape(channels, out_len)[:, ::-1]
+    ahead = depthwise(grad_mixed, per_channel)
     grad_product = ahead + skip_all[:, None] * grad_mixed[:, :out_len].astype(jnp.float32)
     grad_inner_feat = (grad_product * value_feat[:, reach_cols:]).astype(jnp.bfloat16)
     grad_value_feat = (grad_product * inner_feat[:, reach_cols:]).astype(jnp.bfloat16)
@@ -154,13 +162,10 @@
 
     grad_scale = 1.0 / math.sqrt(ctx_size * block_len)
     gm_here = grad_mixed[:, :block_len]
-    cross_terms = jnp.einsum(
-        "gct,gcs->gts",
-        gm_here.reshape(groups, group_size, block_len),
-        product[:, : block_len + reach_cols].reshape(groups, group_size, block_len + reach_cols),
-        preferred_element_type=jnp.float32,
-    )
-    filter_part = grad_scale * skew_sum(cross_terms, taps_count)
+    filter_rev = depthwise(product[:, : block_len + reach_cols], gm_here)
+    filter_part = grad_scale * jnp.sum(
+        filter_rev.reshape(groups, group_size, taps_count), axis=1
+    )[:, ::-1]
     skip_part = grad_scale * jnp.sum(
         gm_here.astype(jnp.float32) * product_here[:, :block_len], axis=1
     )

time: 146 us -> 99.8 us (0.68)
  local copies, waits for them, and re-layouts: 59.1 us -> 17.2 us
  other arithmetic: 14.9 us -> 1.94 us
  matrix products: 11.6 us -> 17.5 us
  starting transfers between devices: 38.6 us -> 42.2 us
    reshape x2 -> x0, local copies, waits for them, and re-layouts: 17.9 us -> none  [the longest x1 11.1 us: toeplitz_rows(): return flattened.reshape(groups, out_len, window)]
    conv_general_dilated x0 -> x3, matrix products: none -> 17.5 us  [depthwise(): lax.conv_general_dilated(values[None], kernel[:, None, :], window_strides...]
    dot_general x3 -> x0, matrix products: 11.6 us -> none  [the longest x1 4.29 us: shards(): jnp.einsum('gcs,gts->gct', windows, toeplitz, preferred_element_type=jnp....]
    another operation x2 -> x1, local copies, waits for them, and re-layouts: 9.05 us -> 0.14 us  [depthwise(): kernel[:, None, :]]
    pad x1 -> x0, local copies, waits for them, and re-layouts: 3.18 us -> none  [skew_sum(): jnp.pad(cross_terms.reshape(groups, block_len * window), ((0, 0), (0, blo...]
    all_to_all x1, starting transfers between devices: 6.3 us -> 8.88 us  [shards(): lax.all_to_all(jnp.broadcast_to(row[None], (ctx_size, row.shape[0])), 'ct...]
    unnamed x39 -> x26, local copies, waits for them, and re-layouts: 5.77 us -> 8.26 us
    slice x3, local copies, waits for them, and re-layouts: 3.25 us -> 0.87 us  [the longest x2 0.86 us: shards(): outer_gate[:, :rim]]
  transfers between devices with their start and end apart: 6 -> 6, of which waited for: 3 -> 3; matrix products, arithmetic and copies ran while one was open for 28% -> 8% of each run, Pallas kernels for 0% -> 0%
where the time goes in v1:
time: 99.8 us; the launch traced here: 99.3 us
  starting transfers between devices  42.2 us (42%)
  waiting for transfers between devices  19.3 us (19%)
  matrix products  17.5 us (18%)
  local copies, waits for them, and re-layouts  17.2 us (17%)
  other arithmetic  1.94 us (2%)
  between operations  1.23 us (1%)
    conv_general_dilated x3, matrix products, depthwise(): lax.conv_general_dilated(values[None], kernel[:, None, :], window_strides...  17.5 us
    ppermute x1, starting transfers between devices, shards(): lax.ppermute(param_pack, ('ctx', 'fsdp'), [(k, regroup_target(k, fsdp_siz...  15.9 us
    ppermute x1, waiting for transfers between devices, shards(): lax.ppermute(reduced[n_filt:], ('ctx', 'fsdp'), [(regroup_target(k, fsdp_...  11.3 us
    all_to_all x1, starting transfers between devices, shards(): lax.all_to_all(jnp.broadcast_to(row[None], (ctx_size, row.shape[0])), 'ct...  8.88 us
    unnamed x26, local copies, waits for them, and re-layouts  8.26 us
    all_to_all x1, starting transfers between devices, shards(): reduced = jnp.sum(lax.all_to_all(send, 'ctx', 0, 0, tiled=True), axis=0)  7.63 us
    ppermute x2, starting transfers between devices, passed_along(): return lax.ppermute(shard, axis, pairs)  5.93 us
    all_to_all x1, waiting for transfers between devices, shards(): reduced = jnp.sum(lax.all_to_all(send, 'ctx', 0, 0, tiled=True), axis=0)  4.03 us
  transfers between devices with their start and end apart: 6, of which 3 were waited for; matrix products, arithmetic and copies ran while one was open for 8% of the time, Pallas kernels for 0%

profile of v1, /device:TPU:5, one launch (start us, length us, event | category | flops | bytes accessed | tf_op | source)
XLA Modules:
  0.0 99.3 jit_solution(11536818780679641481)
XLA Ops:
  0.6 1.0 %copy.132 = bf16[256,256]{0,1:T(8,128)(2,1)S(1)} copy(bf16[256,256]{1,0:T(8,128)(2,1)} %param.7) | data formatting | bytes 262144 | tf_op args[0]
  1.7 0.6 copy-done
  2.3 0.3 copy-done.2
  2.7 0.8 copy-done.3
  3.6 0.8 copy-done.4
  4.5 0.9 slice-done
  5.5 2.6 %collective-permute-start.2 = (bf16[256,262]{0,1:T(8,128)(2,1)S(1)}, bf16[256,262]{0,1:T(8,128)(2,1)S(1)}, u32[]{:S(2)}, u32[]{:S(2)}) collective-permute-start(bf16[256,262]{0,1:T(8,128)(2,1)S(1)} %pad_maximum_fusion.1), channel_id=1, source_target_pairs={{8,0},{16,8},{24,16},{32,24},{40,32},{48,40},{56,48},{64,56},{72,6... | collective-permute-start | bytes 402440 | tf_op jit(solution)/shard_map/ppermute | solution.py:12
  8.2 15.9 %collective-permute-start = (f32[40]{0:T(128)S(1)}, f32[40]{0:T(128)S(1)}, u32[]{:S(2)}, u32[]{:S(2)}) collective-permute-start(f32[40]{0:T(128)S(1)} %pad_maximum_fusion.5), channel_id=1, source_target_pairs={{0,0},{1,8},{2,16},{3,24},{4,32},{5,40},{6,48},{7,56},{8,64},{9,72... | collective-permute-start | bytes 488 | tf_op jit(solution)/shard_map/ppermute | solution.py:92
  24.2 0.7 copy-done.6
  25.1 0.6 broadcast_in_dim.24
  25.7 8.9 %all-to-all-start = ((f32[64,1,72]{2,1,0:T(1,128)}), f32[64,1,72]{2,1,0:T(1,128)S(1)}, u32[]{:S(2)}, u32[]{:S(2)}) async-start(f32[64,1,72]{2,1,0:T(1,128)} %broadcast_in_dim.24), calls=%async_computation | async-start | bytes 65536 | tf_op jit(solution)/shard_map/all_to_all | solution.py:98
  34.7 3.4 %collective-permute-start.1 = (bf16[256,260]{0,1:T(8,128)(2,1)S(1)}, bf16[256,260]{0,1:T(8,128)(2,1)S(1)}, u32[]{:S(2)}, u32[]{:S(2)}) collective-permute-start(bf16[256,260]{0,1:T(8,128)(2,1)S(1)} %pad_maximum_fusion), channel_id=1, source_target_pairs={{0,8},{8,16},{16,24},{24,32},{32,40},{40,48},{48,56},{56,64},{64,7... | collective-permute-start | bytes 399368 | tf_op jit(solution)/shard_map/ppermute | solution.py:12
  38.0 3.9 %all-to-all-done = f32[64,1,72]{2,1,0:T(1,128)S(1)} async-done(((f32[64,1,72]{2,1,0:T(1,128)}), f32[64,1,72]{2,1,0:T(1,128)S(1)}, u32[]{:S(2)}, u32[]{:S(2)}) %all-to-all-start) | async-done | bytes 18464 | tf_op jit(solution)/shard_map/all_to_all | solution.py:98
  42.4 0.1 mul.261
  42.6 0.1 mul.264
  42.8 0.1 mul.267
  43.0 0.1 mul.270
  43.2 0.1 mul.273
  43.5 0.2 rev.6
  43.8 0.1 copy.153
  44.5 0.1 copy.157
  45.0 0.3 multiply_convert_fusion.1
  45.5 0.2 multiply_convert_fusion
  45.7 7.0 %fusion.8 = f32[1,256,258]{1,0,2:T(1,128)S(1)} fusion(bf16[256,1,128]{0,1,2:T(2,128)(2,1)S(1)} %copy.153, bf16[1,256,385]{1,2,0:T(8,128)(2,1)S(1)} %bitcast.61), kind=kOutput, calls=%fused_computation.19 | convolution fusion | flops 16908288 | bytes 526848 | tf_op jit(solution)/shard_map/conv_general_dilated | solution.py:64
  52.7 7.0 %fusion.6 = f32[1,256,258]{1,0,2:T(1,128)S(1)} fusion(bf16[256,1,128]{0,1,2:T(2,128)(2,1)S(1)} %copy.157, bf16[1,256,385]{1,2,0:T(8,128)(2,1)S(1)} %bitcast.62), kind=kOutput, calls=%fused_computation.17 | convolution fusion | flops 16908288 | bytes 526848 | tf_op jit(solution)/shard_map/conv_general_dilated | solution.py:64
  59.7 0.2 fusion.40
  59.9 0.1 fusion.19
  60.2 0.1 stack.47
  60.4 0.1 stack.48
  60.6 0.1 fusion.22
  60.9 0.1 stack.51
  61.1 0.1 stack.52
  61.3 0.1 fusion.16
  61.6 0.1 stack.43
  61.8 0.1 stack.44
  62.1 3.5 %fusion.10 = f32[1,256,128]{1,0,2:T(1,128)S(1)} fusion(bf16[1,256,383]{1,2,0:T(8,128)(2,1)S(1)} %slice_bitcast_fusion, bf16[256,1,256]{0,2,1:T(8,128)(2,1)S(1)} %slice_bitcast_fusion.1), kind=kOutput, calls=%fused_computation.30 | convolution fusion | flops 16777216 | bytes 458240 | tf_op jit(solution)/shard_map/conv_general_dilated | solution.py:64
  66.2 0.7 copy.179
  66.9 7.6 %all-to-all-start.1 = ((f32[64,1,72]{2,1,0:T(1,128)}), f32[64,1,72]{2,1,0:T(1,128)S(1)}, u32[]{:S(2)}, u32[]{:S(2)}) async-start(f32[64,1,72]{2,1,0:T(1,128)} %copy.179), calls=%async_computation.1 | async-start | bytes 65536 | tf_op jit(solution)/shard_map/all_to_all | solution.py:188
  74.9 0.8 copy.183
  75.6 0.8 copy.182
  76.4 0.8 copy.181
  77.2 0.8 copy.180
  77.9 4.0 %all-to-all-done.1 = f32[64,1,72]{2,1,0:T(1,128)S(1)} async-done(((f32[64,1,72]{2,1,0:T(1,128)}), f32[64,1,72]{2,1,0:T(1,128)S(1)}, u32[]{:S(2)}, u32[]{:S(2)}) %all-to-all-start.1) | async-done | bytes 18464 | tf_op jit(solution)/shard_map/all_to_all | solution.py:188
  82.1 3.9 %collective-permute-start.3 = (f32[40]{0:T(128)S(1)}, f32[40]{0:T(128)S(1)}, u32[]{:S(2)}, u32[]{:S(2)}) collective-permute-start(f32[40]{0:T(128)S(1)} %slice.326), channel_id=1, source_target_pairs={{0,0},{8,1},{16,2},{24,3},{32,4},{40,5},{48,6},{56,7},{64,8},{72,9... | collective-permute-start | bytes 488 | tf_op jit(solution)/shard_map/ppermute | solution.py:190
  86.1 0.7 copy.184
  86.8 11.3 %collective-permute-done.3 = f32[40]{0:T(128)S(1)} collective-permute-done((f32[40]{0:T(128)S(1)}, f32[40]{0:T(128)S(1)}, u32[]{:S(2)}, u32[]{:S(2)}) %collective-permute-start.3) | collective-permute-done | bytes 192 | tf_op jit(solution)/shard_map/ppermute | solution.py:190
  98.1 0.7 reshape.133
  98.8 0.6 slice.328
  (97 shorter events, 5.1 us)
Async XLA Ops:
  1.6 0.7 copy-start
  1.7 1.0 copy-start.2
  2.6 0.9 copy-start.3
  3.5 0.9 copy-start.4
  4.5 0.9 slice-start
  5.4 2.6 %copy-start.5 = (f32[3,3,4]{2,1,0:T(4,128)S(1)}, f32[3,3,4]{2,1,0:T(4,128)}, u32[]{:S(2)}) copy-start(f32[3,3,4]{2,1,0:T(4,128)} %param.12) | copy-start | bytes 436
  5.4 2.7 %copy-start.7 = (f32[4]{0:T(128)S(1)}, f32[4]{0:T(128)}, u32[]{:S(2)}) copy-start(f32[4]{0:T(128)} %param.13) | copy-start | bytes 52
  5.5 39.5 %collective-permute-start.2 = (bf16[256,262]{0,1:T(8,128)(2,1)S(1)}, bf16[256,262]{0,1:T(8,128)(2,1)S(1)}, u32[]{:S(2)}, u32[]{:S(2)}) collective-permute-start(bf16[256,262]{0,1:T(8,128)(2,1)S(1)} %pad_maximum_fusion.1), channel_id=1, source_target_pairs={{8,0},{16,8},{24,16},{32,24},{40,32},{48,40},{56,48},{64,56},{72,6... | collective-permute-start | bytes 402440 | tf_op jit(solution)/shard_map/ppermute | solution.py:12
  8.2 15.9 %copy-start.1 = (bf16[256,256]{0,1:T(8,128)(2,1)S(1)}, bf16[256,256]{0,1:T(8,128)(2,1)}, u32[]{:S(2)}) copy-start(bf16[256,256]{0,1:T(8,128)(2,1)} %copy-done) | copy-start | bytes 393220
  8.2 16.8 %collective-permute-start = (f32[40]{0:T(128)S(1)}, f32[40]{0:T(128)S(1)}, u32[]{:S(2)}, u32[]{:S(2)}) collective-permute-start(f32[40]{0:T(128)S(1)} %pad_maximum_fusion.5), channel_id=1, source_target_pairs={{0,0},{1,8},{2,16},{3,24},{4,32},{5,40},{6,48},{7,56},{8,64},{9,72... | collective-permute-start | bytes 488 | tf_op jit(solution)/shard_map/ppermute | solution.py:92
  24.2 0.7 copy-start.6
  25.7 16.2 %all-to-all-start = ((f32[64,1,72]{2,1,0:T(1,128)}), f32[64,1,72]{2,1,0:T(1,128)S(1)}, u32[]{:S(2)}, u32[]{:S(2)}) async-start(f32[64,1,72]{2,1,0:T(1,128)} %broadcast_in_dim.24), calls=%async_computation | async-start | bytes 65536 | tf_op jit(solution)/shard_map/all_to_all | solution.py:98
  34.7 10.2 %collective-permute-start.1 = (bf16[256,260]{0,1:T(8,128)(2,1)S(1)}, bf16[256,260]{0,1:T(8,128)(2,1)S(1)}, u32[]{:S(2)}, u32[]{:S(2)}) collective-permute-start(bf16[256,260]{0,1:T(8,128)(2,1)S(1)} %pad_maximum_fusion), channel_id=1, source_target_pairs={{0,8},{8,16},{16,24},{24,32},{32,40},{40,48},{48,56},{56,64},{64,7... | collective-permute-start | bytes 399368 | tf_op jit(solution)/shard_map/ppermute | solution.py:12
  66.9 15.0 %all-to-all-start.1 = ((f32[64,1,72]{2,1,0:T(1,128)}), f32[64,1,72]{2,1,0:T(1,128)S(1)}, u32[]{:S(2)}, u32[]{:S(2)}) async-start(f32[64,1,72]{2,1,0:T(1,128)} %copy.179), calls=%async_computation.1 | async-start | bytes 65536 | tf_op jit(solution)/shard_map/all_to_all | solution.py:188
  82.1 16.0 %collective-permute-start.3 = (f32[40]{0:T(128)S(1)}, f32[40]{0:T(128)S(1)}, u32[]{:S(2)}, u32[]{:S(2)}) collective-permute-start(f32[40]{0:T(128)S(1)} %slice.326), channel_id=1, source_target_pairs={{0,0},{8,1},{16,2},{24,3},{32,4},{40,5},{48,6},{56,7},{64,8},{72,9... | collective-permute-start | bytes 488 | tf_op jit(solution)/shard_map/ppermute | solution.py:190

commit v2 on v1

--- a/solution.py
+++ b/solution.py
@@ -72,11 +72,6 @@
     )[0]
 
 
-def regroup_target(lin, fsdp_size):
-    i, j = divmod(lin, fsdp_size)
-    return (fsdp_size * (i % fsdp_size) + j) * fsdp_size + i // fsdp_size
-
-
 def shards(outer_gate, inner_gate, value_stream, grad_output, filters, feature_taps, skip_gain):
     channels, block_len = outer_gate.shape
     ctx_size = lax.axis_size("ctx")
@@ -88,30 +83,27 @@
     group_size = channels // groups
     chunk = feature_taps.shape[2]
 
-    param_pack = jnp.concatenate([feature_taps.reshape(-1), skip_gain])
-    regrouped = lax.ppermute(
-        param_pack,
-        ("ctx", "fsdp"),
-        [(k, regroup_target(k, fsdp_size)) for k in range(n_dev)],
-    )
-    row = jnp.concatenate([filters.reshape(-1), regrouped])
+    row = jnp.concatenate([filters.reshape(-1), feature_taps.reshape(-1), skip_gain])
     gathered = lax.all_to_all(
         jnp.broadcast_to(row[None], (ctx_size, row.shape[0])), "ctx", 0, 0, tiled=True
     )
     n_filt = groups * taps_here
+    n_chunk = row.shape[0] - n_filt
+    per_block = ctx_size // fsdp_size
     filters_all = (
         gathered[:, :n_filt]
         .reshape(ctx_size, groups, taps_here)
         .transpose(1, 0, 2)
         .reshape(groups, taps_count)
     )
+    moved = lax.all_to_all(gathered[:, n_filt:], "fsdp", 0, 0, tiled=True)
+    local = (
+        moved.reshape(fsdp_size, per_block, n_chunk).transpose(1, 0, 2).reshape(ctx_size, n_chunk)
+    )
     taps_all = (
-        gathered[:, n_filt : n_filt + 9 * chunk]
-        .reshape(ctx_size, 3, 3, chunk)
-        .transpose(1, 2, 0, 3)
-        .reshape(3, 3, channels)
-    )
-    skip_all = gathered[:, n_filt + 9 * chunk :].reshape(channels)
+        local[:, : 9 * chunk].reshape(ctx_size, 3, 3, chunk).transpose(1, 2, 0, 3).reshape(3, 3, channels)
+    )
+    skip_all = local[:, 9 * chunk :].reshape(channels)
 
     rim = reach_cols + 2
     prev_rim = passed_along(
@@ -177,23 +169,26 @@
         ]
     )
 
-    send = jnp.concatenate(
-        [
-            filter_part.reshape(groups, ctx_size, taps_here).transpose(1, 0, 2).reshape(ctx_size, -1),
+    chunk_parts = jnp.concatenate(
+        [
             taps_part.reshape(3, 3, ctx_size, chunk).transpose(2, 0, 1, 3).reshape(ctx_size, -1),
             skip_part.reshape(ctx_size, chunk),
         ],
         axis=1,
     )
+    to_fsdp = chunk_parts.reshape(per_block, fsdp_size, n_chunk).transpose(1, 0, 2).reshape(ctx_size, n_chunk)
+    by_owner = lax.all_to_all(to_fsdp, "fsdp", 0, 0, tiled=True)
+    send = jnp.concatenate(
+        [
+            filter_part.reshape(groups, ctx_size, taps_here).transpose(1, 0, 2).reshape(ctx_size, -1),
+            by_owner,
+        ],
+        axis=1,
+    )
     reduced = jnp.sum(lax.all_to_all(send, "ctx", 0, 0, tiled=True), axis=0)
     filter_share = reduced[:n_filt].reshape(groups, taps_here)
-    back = lax.ppermute(
-        reduced[n_filt:],
-        ("ctx", "fsdp"),
-        [(regroup_target(k, fsdp_size), k) for k in range(n_dev)],
-    )
-    taps_share = back[: 9 * chunk].reshape(3, 3, chunk)
-    skip_share = back[9 * chunk :]
+    taps_share = reduced[n_filt : n_filt + 9 * chunk].reshape(3, 3, chunk)
+    skip_share = reduced[n_filt + 9 * chunk :]
     return (
         gated_out,
         grad_outer.astype(jnp.bfloat16),

time: 99.8 us -> 98.1 us (0.983)
  the two profiles are of different devices: /device:TPU:5 before, /device:TPU:1 now
where the time goes in v2:
time: 98.1 us; the launch traced here: 97.6 us
  starting transfers between devices  41.8 us (43%)
  local copies, waits for them, and re-layouts  20.2 us (21%)
  matrix products  17.5 us (18%)
  waiting for transfers between devices  13 us (13%)
  other arithmetic  3.9 us (4%)
  between operations  1.2 us (1%)
    conv_general_dilated x3, matrix products, depthwise(): lax.conv_general_dilated(values[None], kernel[:, None, :], window_strides...  17.5 us
    all_to_all x1, starting transfers between devices, shards(): lax.all_to_all(jnp.broadcast_to(row[None], (ctx_size, row.shape[0])), 'ct...  11.6 us
    unnamed x28, local copies, waits for them, and re-layouts  11 us
    all_to_all x1, starting transfers between devices, shards(): reduced = jnp.sum(lax.all_to_all(send, 'ctx', 0, 0, tiled=True), axis=0)  10.2 us
    all_to_all x1, starting transfers between devices, shards(): moved = lax.all_to_all(gathered[:, n_filt:], 'fsdp', 0, 0, tiled=True)  10 us
    all_to_all x1, waiting for transfers between devices, shards(): reduced = jnp.sum(lax.all_to_all(send, 'ctx', 0, 0, tiled=True), axis=0)  6.15 us
    ppermute x2, starting transfers between devices, passed_along(): return lax.ppermute(shard, axis, pairs)  5.58 us
    all_to_all x1, starting transfers between devices, shards(): by_owner = lax.all_to_all(to_fsdp, 'fsdp', 0, 0, tiled=True)  4.3 us
  transfers between devices with their start and end apart: 6, of which 4 were waited for; matrix products, arithmetic and copies ran while one was open for 14% of the time, Pallas kernels for 0%

profile of v2, /device:TPU:1, one launch (start us, length us, event | category | flops | bytes accessed | tf_op | source)
XLA Modules:
  0.0 97.6 jit_solution(17677990868881081103)
XLA Ops:
  0.6 0.8 copy.195
  1.5 0.6 copy-done.5
  2.2 0.6 copy-done.6
  2.8 0.6 broadcast_in_dim.24
  3.4 11.6 %all-to-all-start = ((f32[64,1,72]{2,1,0:T(1,128)}), f32[64,1,72]{2,1,0:T(1,128)S(1)}, u32[]{:S(2)}, u32[]{:S(2)}) async-start(f32[64,1,72]{2,1,0:T(1,128)} %broadcast_in_dim.24), calls=%async_computation | async-start | bytes 65536 | tf_op jit(solution)/shard_map/all_to_all | solution.py:87
  15.1 1.0 %copy.199 = bf16[256,256]{0,1:T(8,128)(2,1)S(1)} copy(bf16[256,256]{1,0:T(8,128)(2,1)} %param.7) | data formatting | bytes 262144 | tf_op args[0]
  16.1 0.6 copy-done
  16.7 0.3 copy-done.2
  17.2 0.8 copy-done.3
  18.1 0.8 copy-done.4
  19.0 0.9 slice-done
  19.9 2.5 %collective-permute-start.1 = (bf16[256,262]{0,1:T(8,128)(2,1)S(1)}, bf16[256,262]{0,1:T(8,128)(2,1)S(1)}, u32[]{:S(2)}, u32[]{:S(2)}) collective-permute-start(bf16[256,262]{0,1:T(8,128)(2,1)S(1)} %pad_maximum_fusion.1), channel_id=1, source_target_pairs={{8,0},{16,8},{24,16},{32,24},{40,32},{48,40},{56,48},{64,56},{72,6... | collective-permute-start | bytes 402440 | tf_op jit(solution)/shard_map/ppermute | solution.py:12
  22.5 1.8 %all-to-all-done = f32[64,1,72]{2,1,0:T(1,128)S(1)} async-done(((f32[64,1,72]{2,1,0:T(1,128)}), f32[64,1,72]{2,1,0:T(1,128)S(1)}, u32[]{:S(2)}, u32[]{:S(2)}) %all-to-all-start) | async-done | bytes 18464 | tf_op jit(solution)/shard_map/all_to_all | solution.py:87
  24.4 0.7 reshape.148
  25.1 10.0 %all-to-all-start.1 = ((f32[8,1,320]{2,1,0:T(1,128)}), f32[8,1,320]{2,1,0:T(1,128)S(1)}, u32[]{:S(2)}, u32[]{:S(2)}) async-start(f32[8,1,320]{2,1,0:T(1,128)} %reshape.148), calls=%async_computation.1 | async-start | bytes 24576 | tf_op jit(solution)/shard_map/all_to_all | solution.py:99
  35.1 3.1 %collective-permute-start = (bf16[256,260]{0,1:T(8,128)(2,1)S(1)}, bf16[256,260]{0,1:T(8,128)(2,1)S(1)}, u32[]{:S(2)}, u32[]{:S(2)}) collective-permute-start(bf16[256,260]{0,1:T(8,128)(2,1)S(1)} %pad_maximum_fusion), channel_id=1, source_target_pairs={{0,8},{8,16},{16,24},{24,32},{32,40},{40,48},{48,56},{56,64},{64,7... | collective-permute-start | bytes 399368 | tf_op jit(solution)/shard_map/ppermute | solution.py:12
  38.3 0.1 copy.218
  38.6 0.2 rev.6
  38.8 0.1 copy.221
  38.9 0.1 copy.224
  39.1 2.6 %all-to-all-done.1 = f32[8,1,320]{2,1,0:T(1,128)S(1)} async-done(((f32[8,1,320]{2,1,0:T(1,128)}), f32[8,1,320]{2,1,0:T(1,128)S(1)}, u32[]{:S(2)}, u32[]{:S(2)}) %all-to-all-start.1) | async-done | bytes 10272 | tf_op jit(solution)/shard_map/all_to_all | solution.py:99
  41.7 0.5 broadcast.14
  42.2 0.7 reduce.1
  45.3 0.3 multiply_convert_fusion.1
  45.8 0.2 multiply_convert_fusion
  46.0 7.0 %fusion.8 = f32[1,256,258]{1,0,2:T(1,128)S(1)} fusion(bf16[256,1,128]{0,1,2:T(2,128)(2,1)S(1)} %copy.221, bf16[1,256,385]{1,2,0:T(8,128)(2,1)S(1)} %bitcast.71), kind=kOutput, calls=%fused_computation.19 | convolution fusion | flops 16908288 | bytes 526848 | tf_op jit(solution)/shard_map/conv_general_dilated | solution.py:64
  53.0 7.0 %fusion.6 = f32[1,256,258]{1,0,2:T(1,128)S(1)} fusion(bf16[256,1,128]{0,1,2:T(2,128)(2,1)S(1)} %copy.224, bf16[1,256,385]{1,2,0:T(8,128)(2,1)S(1)} %bitcast.72), kind=kOutput, calls=%fused_computation.17 | convolution fusion | flops 16908288 | bytes 526848 | tf_op jit(solution)/shard_map/conv_general_dilated | solution.py:64
  60.0 0.2 fusion.40
  60.2 0.1 fusion.19
  60.9 0.1 fusion.22
  61.6 0.1 fusion.16
  62.1 0.1 stack.44
  62.6 0.1 copy.245
  62.9 0.7 reshape.150
  63.6 4.3 %all-to-all-start.2 = ((f32[8,1,320]{2,1,0:T(1,128)}), f32[8,1,320]{2,1,0:T(1,128)S(1)}, u32[]{:S(2)}, u32[]{:S(2)}) async-start(f32[8,1,320]{2,1,0:T(1,128)} %reshape.150), calls=%async_computation.2 | async-start | bytes 24576 | tf_op jit(solution)/shard_map/all_to_all | solution.py:180
  67.9 3.4 %fusion.10 = f32[1,256,128]{1,0,2:T(1,128)S(1)} fusion(bf16[1,256,383]{1,2,0:T(8,128)(2,1)S(1)} %slice_bitcast_fusion, bf16[256,1,256]{0,2,1:T(8,128)(2,1)S(1)} %slice_bitcast_fusion.1), kind=kOutput, calls=%fused_computation.30 | convolution fusion | flops 16777216 | bytes 458240 | tf_op jit(solution)/shard_map/conv_general_dilated | solution.py:64
  72.1 2.4 %all-to-all-done.2 = f32[8,1,320]{2,1,0:T(1,128)S(1)} async-done(((f32[8,1,320]{2,1,0:T(1,128)}), f32[8,1,320]{2,1,0:T(1,128)S(1)}, u32[]{:S(2)}, u32[]{:S(2)}) %all-to-all-start.2) | async-done | bytes 10272 | tf_op jit(solution)/shard_map/all_to_all | solution.py:180
  74.5 0.7 reduce.2
  75.2 0.7 pad_maximum_fusion.5
  75.9 10.2 %all-to-all-start.3 = ((f32[64,1,72]{2,1,0:T(1,128)}), f32[64,1,72]{2,1,0:T(1,128)S(1)}, u32[]{:S(2)}, u32[]{:S(2)}) async-start(f32[64,1,72]{2,1,0:T(1,128)} %bitcast.23), calls=%async_computation.3 | async-start | bytes 65536 | tf_op jit(solution)/shard_map/all_to_all | solution.py:188
  86.3 0.8 copy.252
  87.0 0.8 copy.251
  87.8 0.8 copy.250
  88.5 0.8 copy.249
  89.3 6.2 %all-to-all-done.3 = f32[64,1,72]{2,1,0:T(1,128)S(1)} async-done(((f32[64,1,72]{2,1,0:T(1,128)}), f32[64,1,72]{2,1,0:T(1,128)S(1)}, u32[]{:S(2)}, u32[]{:S(2)}) %all-to-all-start.3) | async-done | bytes 18464 | tf_op jit(solution)/shard_map/all_to_all | solution.py:188
  95.6 0.6 slice.328
  96.3 0.6 copy.253
  96.9 0.7 reshape.147
  (104 shorter events, 6.4 us)
Async XLA Ops:
  1.4 0.7 copy-start.5
  2.1 0.7 copy-start.6
  3.4 20.8 %all-to-all-start = ((f32[64,1,72]{2,1,0:T(1,128)}), f32[64,1,72]{2,1,0:T(1,128)S(1)}, u32[]{:S(2)}, u32[]{:S(2)}) async-start(f32[64,1,72]{2,1,0:T(1,128)} %broadcast_in_dim.24), calls=%async_computation | async-start | bytes 65536 | tf_op jit(solution)/shard_map/all_to_all | solution.py:87
  16.1 0.7 copy-start
  16.1 1.0 copy-start.2
  17.1 0.9 copy-start.3
  18.0 0.9 copy-start.4
  19.0 0.9 slice-start
  19.9 2.6 %copy-start.1 = (bf16[256,256]{0,1:T(8,128)(2,1)S(1)}, bf16[256,256]{0,1:T(8,128)(2,1)}, u32[]{:S(2)}) copy-start(bf16[256,256]{0,1:T(8,128)(2,1)} %copy-done) | copy-start | bytes 393220
  19.9 25.3 %collective-permute-start.1 = (bf16[256,262]{0,1:T(8,128)(2,1)S(1)}, bf16[256,262]{0,1:T(8,128)(2,1)S(1)}, u32[]{:S(2)}, u32[]{:S(2)}) collective-permute-start(bf16[256,262]{0,1:T(8,128)(2,1)S(1)} %pad_maximum_fusion.1), channel_id=1, source_target_pairs={{8,0},{16,8},{24,16},{32,24},{40,32},{48,40},{56,48},{64,56},{72,6... | collective-permute-start | bytes 402440 | tf_op jit(solution)/shard_map/ppermute | solution.py:12
  25.1 16.6 %all-to-all-start.1 = ((f32[8,1,320]{2,1,0:T(1,128)}), f32[8,1,320]{2,1,0:T(1,128)S(1)}, u32[]{:S(2)}, u32[]{:S(2)}) async-start(f32[8,1,320]{2,1,0:T(1,128)} %reshape.148), calls=%async_computation.1 | async-start | bytes 24576 | tf_op jit(solution)/shard_map/all_to_all | solution.py:99
  35.1 10.0 %collective-permute-start = (bf16[256,260]{0,1:T(8,128)(2,1)S(1)}, bf16[256,260]{0,1:T(8,128)(2,1)S(1)}, u32[]{:S(2)}, u32[]{:S(2)}) collective-permute-start(bf16[256,260]{0,1:T(8,128)(2,1)S(1)} %pad_maximum_fusion), channel_id=1, source_target_pairs={{0,8},{8,16},{16,24},{24,32},{32,40},{40,48},{48,56},{56,64},{64,7... | collective-permute-start | bytes 399368 | tf_op jit(solution)/shard_map/ppermute | solution.py:12
  63.6 10.9 %all-to-all-start.2 = ((f32[8,1,320]{2,1,0:T(1,128)}), f32[8,1,320]{2,1,0:T(1,128)S(1)}, u32[]{:S(2)}, u32[]{:S(2)}) async-start(f32[8,1,320]{2,1,0:T(1,128)} %reshape.150), calls=%async_computation.2 | async-start | bytes 24576 | tf_op jit(solution)/shard_map/all_to_all | solution.py:180
  75.9 19.5 %all-to-all-start.3 = ((f32[64,1,72]{2,1,0:T(1,128)}), f32[64,1,72]{2,1,0:T(1,128)S(1)}, u32[]{:S(2)}, u32[]{:S(2)}) async-start(f32[64,1,72]{2,1,0:T(1,128)} %bitcast.23), calls=%async_computation.3 | async-start | bytes 65536 | tf_op jit(solution)/shard_map/all_to_all | solution.py:188

commit v3 on v2

--- a/solution.py
+++ b/solution.py
@@ -3,6 +3,8 @@
 import jax
 import jax.numpy as jnp
 from jax import lax
+from jax.experimental import pallas as pl
+from jax.experimental.pallas import tpu as pltpu
 from jax.sharding import PartitionSpec as P
 
 
@@ -72,6 +74,44 @@
     )[0]
 
 
+def banded_kernel(ahead_ref, behind_ref, pw_ref, gw_ref, fo_ref, bo_ref):
+    rows = fo_ref.shape[2]
+    lanes = ahead_ref.shape[1]
+    dims = (((1,), (1,)), ((), ()))
+    for group in range(ahead_ref.shape[0]):
+        for row_ref, data_ref, out_ref in ((ahead_ref, pw_ref, fo_ref), (behind_ref, gw_ref, bo_ref)):
+            band = pltpu.roll(
+                jnp.broadcast_to(row_ref[group : group + 1, :], (rows, lanes)), 0, 1, stride=1, stride_axis=0
+            ).astype(jnp.bfloat16)
+            out_ref[group] = lax.dot_general(
+                data_ref[group], band, dims, preferred_element_type=jnp.float32
+            )
+
+
+def both_convs(product, grad_mixed, filters_low):
+    channels, win = product.shape
+    groups, taps = filters_low.shape
+    out_len = win - taps + 1
+    rows = -(-out_len // 16) * 16
+    lanes = -(-max(win, rows + taps - 1) // 128) * 128
+    as_rows = filters_low.astype(jnp.float32)
+    ahead = jnp.pad(as_rows[:, ::-1], ((0, 0), (0, lanes - taps)))
+    behind = jnp.pad(as_rows, ((0, 0), (0, lanes - taps)))
+    pw = jnp.pad(product, ((0, 0), (0, lanes - win))).reshape(groups, channels // groups, lanes)
+    gw = jnp.pad(grad_mixed, ((0, 0), (0, lanes - win))).reshape(groups, channels // groups, lanes)
+    spec = pl.BlockSpec(memory_space=pltpu.VMEM)
+    fo, bo = pl.pallas_call(
+        banded_kernel,
+        out_shape=(jax.ShapeDtypeStruct((groups, channels // groups, rows), jnp.float32),) * 2,
+        in_specs=[spec] * 4,
+        out_specs=(spec, spec),
+        cost_estimate=pl.CostEstimate(
+            flops=4 * channels * lanes * rows, transcendentals=0, bytes_accessed=4 * channels * (lanes + 2 * rows)
+        ),
+    )(ahead, behind, pw, gw)
+    return fo.reshape(channels, rows)[:, :out_len], bo.reshape(channels, rows)[:, :out_len]
+
+
 def shards(outer_gate, inner_gate, value_stream, grad_output, filters, feature_taps, skip_gain):
     channels, block_len = outer_gate.shape
     ctx_size = lax.axis_size("ctx")
@@ -135,15 +175,13 @@
 
     out_len = block_len + 2
     filters_low = filters_all.astype(jnp.bfloat16)
-    per_channel = jnp.repeat(filters_low, group_size, axis=0)
-    convolved = depthwise(product, per_channel[:, ::-1])
     product_here = product[:, reach_cols:].astype(jnp.float32)
+    grad_mixed = (upstream * outer_feat).astype(jnp.bfloat16)
+    convolved, ahead = both_convs(product, grad_mixed, filters_low)
     mixed = convolved + skip_all[:, None] * product_here
     gated_out = (outer_feat[:, :block_len] * mixed[:, :block_len]).astype(jnp.bfloat16)
 
-    grad_mixed = (upstream * outer_feat).astype(jnp.bfloat16)
     grad_outer_feat = (upstream[:, :out_len] * mixed).astype(jnp.bfloat16)
-    ahead = depthwise(grad_mixed, per_channel)
     grad_product = ahead + skip_all[:, None] * grad_mixed[:, :out_len].astype(jnp.float32)
     grad_inner_feat = (grad_product * value_feat[:, reach_cols:]).astype(jnp.bfloat16)
     grad_value_feat = (grad_product * inner_feat[:, reach_cols:]).astype(jnp.bfloat16)

time: 98.1 us -> 108 us (1.10)
  matrix products: 17.5 us -> 7.06 us
  other arithmetic: 3.9 us -> 13.2 us
  Pallas kernels: 0 us -> 4.59 us
  local copies, waits for them, and re-layouts: 20.2 us -> 24.1 us
  starting transfers between devices: 41.8 us -> 43.3 us
    conv_general_dilated x3 -> x1, matrix products: 17.5 us -> 7.06 us  [depthwise(): lax.conv_general_dilated(values[None], kernel[:, None, :], window_strides...]
    pallas_call x0 -> x1, Pallas kernels: none -> 4.59 us  [both_convs(): pl.pallas_call(banded_kernel, out_shape=(jax.ShapeDtypeStruct((groups, ch...]
    pad x0 -> x4, local copies, waits for them, and re-layouts: none -> 2.69 us  [the longest x1 0.73 us: both_convs(): jnp.pad(grad_mixed, ((0, 0), (0, lanes - win)))]
    all_to_all x1, starting transfers between devices: 10.2 us -> 12.7 us  [shards(): reduced = jnp.sum(lax.all_to_all(send, 'ctx', 0, 0, tiled=True), axis=0)]
    all_to_all x1, waiting for transfers between devices: 2.63 us -> 5.13 us  [shards(): moved = lax.all_to_all(gathered[:, n_filt:], 'fsdp', 0, 0, tiled=True)]
    unnamed x28 -> x68, local copies, waits for them, and re-layouts: 11 us -> 8.57 us
    all_to_all x1, waiting for transfers between devices: 2.44 us -> 0.01 us  [shards(): by_owner = lax.all_to_all(to_fsdp, 'fsdp', 0, 0, tiled=True)]
    convert_element_type x1, other arithmetic: 0.21 us -> 2.41 us  [shards(): grad_value = carry_back(grad_value_feat.astype(jnp.float32), taps_all[2])]
  transfers between devices with their start and end apart: 6 -> 6, of which waited for: 4 -> 3; matrix products, arithmetic and copies ran while one was open for 14% -> 18% of each run, Pallas kernels for 0% -> 0%
where the time goes in v3:
time: 108 us; the launch traced here: 107 us
  starting transfers between devices  43.3 us (40%)
  local copies, waits for them, and re-layouts  24.1 us (22%)
  waiting for transfers between devices  13.8 us (13%)
  other arithmetic  13.2 us (12%)
  matrix products  7.06 us (7%)
  Pallas kernels  4.59 us (4%)
  between operations  1.27 us (1%)
    all_to_all x1, starting transfers between devices, shards(): reduced = jnp.sum(lax.all_to_all(send, 'ctx', 0, 0, tiled=True), axis=0)  12.7 us
    all_to_all x1, starting transfers between devices, shards(): lax.all_to_all(jnp.broadcast_to(row[None], (ctx_size, row.shape[0])), 'ct...  11.6 us
    all_to_all x1, starting transfers between devices, shards(): moved = lax.all_to_all(gathered[:, n_filt:], 'fsdp', 0, 0, tiled=True)  10 us
    unnamed x68, local copies, waits for them, and re-layouts  8.57 us
    all_to_all x1, waiting for transfers between devices, shards(): reduced = jnp.sum(lax.all_to_all(send, 'ctx', 0, 0, tiled=True), axis=0)  8.32 us
    conv_general_dilated x1, matrix products, depthwise(): lax.conv_general_dilated(values[None], kernel[:, None, :], window_strides...  7.06 us
    ppermute x2, starting transfers between devices, passed_along(): return lax.ppermute(shard, axis, pairs)  5.59 us
    all_to_all x1, waiting for transfers between devices, shards(): moved = lax.all_to_all(gathered[:, n_filt:], 'fsdp', 0, 0, tiled=True)  5.13 us
  transfers between devices with their start and end apart: 6, of which 3 were waited for; matrix products, arithmetic and copies ran while one was open for 18% of the time, Pallas kernels for 0%

profile of v3, /device:TPU:1, one launch (start us, length us, event | category | flops | bytes accessed | tf_op | source)
XLA Modules:
  0.0 107.4 jit_solution(10301409387951238164)
XLA Ops:
  0.6 0.8 copy.186
  1.5 0.6 copy-done.28
  2.2 0.6 copy-done.30
  2.8 0.6 broadcast_in_dim.12
  3.4 11.6 %all-to-all-start = ((f32[64,1,72]{2,1,0:T(1,128)}), f32[64,1,72]{2,1,0:T(1,128)S(1)}, u32[]{:S(2)}, u32[]{:S(2)}) async-start(f32[64,1,72]{2,1,0:T(1,128)} %broadcast_in_dim.12), calls=%async_computation | async-start | bytes 65536 | tf_op jit(solution)/shard_map/all_to_all | solution.py:127
  15.1 1.0 slice.272
  16.3 0.8 copy-done.2
  17.3 3.7 %collective-permute-start = (bf16[256,260]{1,0:T(8,128)(2,1)S(1)}, bf16[256,260]{1,0:T(8,128)(2,1)S(1)}, u32[]{:S(2)}, u32[]{:S(2)}) collective-permute-start(bf16[256,260]{1,0:T(8,128)(2,1)S(1)} %pad_maximum_fusion), channel_id=1, source_target_pairs={{0,8},{8,16},{16,24},{24,32},{32,40},{40,48},{48,56},{56,64},{64,7... | collective-permute-start | bytes 399368 | tf_op jit(solution)/shard_map/ppermute | solution.py:14
  21.0 0.8 slice-done
  22.0 1.9 %collective-permute-start.1 = (bf16[256,262]{1,0:T(8,128)(2,1)S(1)}, bf16[256,262]{1,0:T(8,128)(2,1)S(1)}, u32[]{:S(2)}, u32[]{:S(2)}) collective-permute-start(bf16[256,262]{1,0:T(8,128)(2,1)S(1)} %pad_maximum_fusion.1), channel_id=1, source_target_pairs={{8,0},{16,8},{24,16},{32,24},{40,32},{48,40},{56,48},{64,56},{72,6... | collective-permute-start | bytes 402440 | tf_op jit(solution)/shard_map/ppermute | solution.py:14
  24.5 0.7 reshape.166
  25.2 10.0 %all-to-all-start.1 = ((f32[8,1,320]{2,1,0:T(1,128)}), f32[8,1,320]{2,1,0:T(1,128)S(1)}, u32[]{:S(2)}, u32[]{:S(2)}) async-start(f32[8,1,320]{2,1,0:T(1,128)} %reshape.166), calls=%async_computation.1 | async-start | bytes 24576 | tf_op jit(solution)/shard_map/all_to_all | solution.py:139
  35.4 0.6 pad.15.behind_ref
  36.1 0.6 pad.14.ahead_ref
  36.7 5.1 %all-to-all-done.1 = f32[8,1,320]{2,1,0:T(1,128)S(1)} async-done(((f32[8,1,320]{2,1,0:T(1,128)}), f32[8,1,320]{2,1,0:T(1,128)S(1)}, u32[]{:S(2)}, u32[]{:S(2)}) %all-to-all-start.1) | async-done | bytes 10272 | tf_op jit(solution)/shard_map/all_to_all | solution.py:139
  41.8 0.5 broadcast.18
  42.3 0.7 reduce.1
  45.2 0.7 mul.279
  46.2 0.5 copy-done.6
  47.4 0.9 multiply_convert_fusion.1
  48.3 0.9 slice_convert_fusion
  49.1 0.7 slice_bitcast_fusion
  49.8 0.7 pad.16
  50.9 1.3 %multiply_convert_fusion = (bf16[256,385]{1,0:T(8,128)(2,1)S(1)}, f32[256,385]{1,0:T(8,128)}) fusion(bf16[256,129]{1,0:T(8,128)(2,1)S(1)} %get-tuple-element.77, bf16[256,256]{1,0:T(8,128)(2,1)S(1)} %copy-done.4, f32[256,387]{1,0:T(8,128)S(1)} %maximum_convert_fusion, f32[256]{0:T(256)S(1)} %mul.256, f32[256]{0:T(256)S(1)} %mul.253, f32[256]{0:T(256)S(1)} %mul.250), kind=kLoop, calls=%fused_computation.15 | loop fusion | flops 1084160 | bytes 1974272 | tf_op jit(solution)/shard_map/convert_element_type | solution.py:179
  52.2 0.7 pad.17
  52.9 0.7 slice_bitcast_fusion.1
  53.6 4.6 %shard_map.126 = (f32[16,16,272]{2,1,0:T(8,128)}, f32[16,16,272]{2,1,0:T(8,128)}) custom-call(f32[16,512]{1,0:T(8,128)} %pad.14.ahead_ref, f32[16,512]{1,0:T(8,128)} %pad.15.behind_ref, bf16[16,16,512]{2,1,0:T(8,128)(2,1)} %bitcast.64, bf16[16,16,512]{2,1,0:T(8,128)(2,1)} %bitcast.65), custom_call_target="tpu_custom_call" | custom-call | flops 142606336 | bytes 1081344 | tf_op jit(solution)/shard_map/pallas_call | solution.py:103
  58.2 0.7 copy-done.29
  58.8 2.4 %fusion.34 = (f32[256,258]{1,0:T(8,128)S(1)}, bf16[256,258]{1,0:T(8,128)(2,1)}, f32[256,258]{1,0:T(8,128)S(1)}, bf16[256,258]{1,0:T(8,128)(2,1)S(1)}, f32[256,25...) fusion(f32[256,385]{1,0:T(8,128)S(1)} %get-tuple-element.73, ...), kind=kLoop, calls=%fused_computation.96 | loop fusion | flops 990720 | bytes 3039232 | tf_op jit(solution)/shard_map/convert_element_type | solution.py:191
  61.3 0.4 fusion.13
  62.2 0.4 copy-done.7
  63.5 0.3 copy-done.3
  65.5 0.7 reshape.168
  66.2 3.3 %all-to-all-start.2 = ((f32[8,1,320]{2,1,0:T(1,128)}), f32[8,1,320]{2,1,0:T(1,128)S(1)}, u32[]{:S(2)}, u32[]{:S(2)}) async-start(f32[8,1,320]{2,1,0:T(1,128)} %reshape.168), calls=%async_computation.2 | async-start | bytes 24576 | tf_op jit(solution)/shard_map/all_to_all | solution.py:218
  69.6 0.6 copy.203
  70.7 7.1 %fusion.47 = f32[1,256,128]{1,0,2:T(1,128)S(1)} fusion(bf16[1,256,383]{1,0,2:T(2,128)(2,1)S(1)} %copy.203, bf16[256,1,256]{0,1,2:T(2,128)(2,1)S(1)} %copy.204), kind=kOutput, calls=%fused_computation.103 | convolution fusion | flops 16777216 | bytes 458240 | tf_op jit(solution)/shard_map/conv_general_dilated | solution.py:66
  78.0 0.7 copy-done.23
  78.6 1.0 fusion.20
  79.6 1.0 fusion.23
  80.8 0.7 fusion.28
  81.7 0.7 reduce.2
  82.5 0.7 pad_maximum_fusion.5
  83.2 12.7 %all-to-all-start.3 = ((f32[64,1,72]{2,1,0:T(1,128)}), f32[64,1,72]{2,1,0:T(1,128)S(1)}, u32[]{:S(2)}, u32[]{:S(2)}) async-start(f32[64,1,72]{2,1,0:T(1,128)} %bitcast.22), calls=%async_computation.3 | async-start | bytes 65536 | tf_op jit(solution)/shard_map/all_to_all | solution.py:226
  95.9 1.0 fusion.26
  96.9 8.3 %all-to-all-done.3 = f32[64,1,72]{2,1,0:T(1,128)S(1)} async-done(((f32[64,1,72]{2,1,0:T(1,128)}), f32[64,1,72]{2,1,0:T(1,128)S(1)}, u32[]{:S(2)}, u32[]{:S(2)}) %all-to-all-start.3) | async-done | bytes 18464 | tf_op jit(solution)/shard_map/all_to_all | solution.py:226
  105.4 0.6 slice.336
  106.0 0.6 copy.221
  106.7 0.7 reshape.163
  (146 shorter events, 9.3 us)
Async XLA Ops:
  1.4 0.7 copy-start.28
  2.1 0.7 copy-start.30
  3.4 20.8 %all-to-all-start = ((f32[64,1,72]{2,1,0:T(1,128)}), f32[64,1,72]{2,1,0:T(1,128)S(1)}, u32[]{:S(2)}, u32[]{:S(2)}) async-start(f32[64,1,72]{2,1,0:T(1,128)} %broadcast_in_dim.12), calls=%async_computation | async-start | bytes 65536 | tf_op jit(solution)/shard_map/all_to_all | solution.py:127
  15.1 1.1 copy-start.1
  16.1 0.9 copy-start.2
  17.3 3.7 %copy-start.4 = (bf16[256,256]{1,0:T(8,128)(2,1)S(1)}, bf16[256,256]{1,0:T(8,128)(2,1)}, u32[]{:S(2)}) copy-start(bf16[256,256]{1,0:T(8,128)(2,1)} %param.10) | copy-start | bytes 393220
  17.3 28.5 %collective-permute-start = (bf16[256,260]{1,0:T(8,128)(2,1)S(1)}, bf16[256,260]{1,0:T(8,128)(2,1)S(1)}, u32[]{:S(2)}, u32[]{:S(2)}) collective-permute-start(bf16[256,260]{1,0:T(8,128)(2,1)S(1)} %pad_maximum_fusion), channel_id=1, source_target_pairs={{0,8},{8,16},{16,24},{24,32},{32,40},{40,48},{48,56},{56,64},{64,7... | collective-permute-start | bytes 399368 | tf_op jit(solution)/shard_map/ppermute | solution.py:14
  21.0 0.8 slice-start
  21.0 0.9 slice-start.1
  22.0 24.0 %collective-permute-start.1 = (bf16[256,262]{1,0:T(8,128)(2,1)S(1)}, bf16[256,262]{1,0:T(8,128)(2,1)S(1)}, u32[]{:S(2)}, u32[]{:S(2)}) collective-permute-start(bf16[256,262]{1,0:T(8,128)(2,1)S(1)} %pad_maximum_fusion.1), channel_id=1, source_target_pairs={{8,0},{16,8},{24,16},{32,24},{40,32},{48,40},{56,48},{64,56},{72,6... | collective-permute-start | bytes 402440 | tf_op jit(solution)/shard_map/ppermute | solution.py:14
  25.2 16.6 %all-to-all-start.1 = ((f32[8,1,320]{2,1,0:T(1,128)}), f32[8,1,320]{2,1,0:T(1,128)S(1)}, u32[]{:S(2)}, u32[]{:S(2)}) async-start(f32[8,1,320]{2,1,0:T(1,128)} %reshape.166), calls=%async_computation.1 | async-start | bytes 24576 | tf_op jit(solution)/shard_map/all_to_all | solution.py:139
  43.7 3.6 %copy-start.18 = (f32[256]{0:T(256)}, f32[256]{0:T(256)S(1)}, u32[]{:S(2)}) copy-start(f32[256]{0:T(256)S(1)} %mul.262) | copy-start | bytes 3076
  43.9 3.4 %copy-start.20 = (f32[256]{0:T(256)}, f32[256]{0:T(256)S(1)}, u32[]{:S(2)}) copy-start(f32[256]{0:T(256)S(1)} %mul.265) | copy-start | bytes 3076
  44.1 3.2 %copy-start.22 = (f32[256]{0:T(256)}, f32[256]{0:T(256)S(1)}, u32[]{:S(2)}) copy-start(f32[256]{0:T(256)S(1)} %mul.268) | copy-start | bytes 3076
  44.3 3.0 %copy-start.24 = (f32[256]{0:T(256)}, f32[256]{0:T(256)S(1)}, u32[]{:S(2)}) copy-start(f32[256]{0:T(256)S(1)} %mul.271) | copy-start | bytes 3076
  44.5 2.8 %copy-start.26 = (f32[256]{0:T(256)}, f32[256]{0:T(256)S(1)}, u32[]{:S(2)}) copy-start(f32[256]{0:T(256)S(1)} %mul.274) | copy-start | bytes 3076
  45.9 4.9 %copy-start.13 = (bf16[256,2]{1,0:T(8,128)(2,1)}, bf16[256,2]{1,0:T(8,128)(2,1)S(1)}, u32[]{:S(2)}) copy-start(bf16[256,2]{1,0:T(8,128)(2,1)S(1)} %slice.340) | copy-start | bytes 3076
  46.0 0.7 copy-start.6
  46.0 0.7 copy-start.8
  46.0 1.0 copy-start
  58.2 0.7 copy-start.29
  58.8 2.4 %copy-start.9 = (bf16[256,129]{1,0:T(8,128)(2,1)S(1)}, bf16[256,129]{1,0:T(8,128)(2,1)}, u32[]{:S(2)}) copy-start(bf16[256,129]{1,0:T(8,128)(2,1)} %copy-done.8) | copy-start | bytes 198148
  61.2 0.9 copy-start.15
  61.6 0.9 copy-start.7
  62.5 0.9 copy-start.16
  62.9 0.9 copy-start.3
  63.1 0.9 copy-start.14
  63.4 1.6 %copy-start.11 = (f32[256,258]{1,0:T(8,128)S(1)}, f32[256,258]{1,0:T(8,128)}, u32[]{:S(2)}) copy-start(f32[256,258]{1,0:T(8,128)} %slice_convert_fusion) | copy-start | bytes 792580
  65.4 4.2 %copy-start.12 = (bf16[1,256,383]{2,1,0:T(8,128)(2,1)S(1)}, bf16[1,256,383]{2,1,0:T(8,128)(2,1)}, u32[]{:S(2)}) copy-start(bf16[1,256,383]{2,1,0:T(8,128)(2,1)} %slice_bitcast_fusion) | copy-start | bytes 588292
  66.2 15.5 %all-to-all-start.2 = ((f32[8,1,320]{2,1,0:T(1,128)}), f32[8,1,320]{2,1,0:T(1,128)S(1)}, u32[]{:S(2)}, u32[]{:S(2)}) async-start(f32[8,1,320]{2,1,0:T(1,128)} %reshape.168), calls=%async_computation.2 | async-start | bytes 24576 | tf_op jit(solution)/shard_map/all_to_all | solution.py:218
  69.6 0.9 copy-start.17
  70.7 7.3 %copy-start.25 = (f32[256]{0:T(256)S(1)}, f32[256]{0:T(256)}, u32[]{:S(2)}) copy-start(f32[256]{0:T(256)} %copy-done.24) | copy-start | bytes 3076
  70.7 7.3 %copy-start.27 = (f32[256]{0:T(256)S(1)}, f32[256]{0:T(256)}, u32[]{:S(2)}) copy-start(f32[256]{0:T(256)} %copy-done.26) | copy-start | bytes 3076
  78.0 0.7 copy-start.23
  78.6 1.0 copy-start.19
  78.6 1.0 copy-start.21
  79.6 1.0 copy-start.5
  79.6 1.1 %copy-start.10 = (f32[256,258]{1,0:T(8,128)S(1)}, f32[256,258]{1,0:T(8,128)}, u32[]{:S(2)}) copy-start(f32[256,258]{1,0:T(8,128)} %get-tuple-element.93) | copy-start | bytes 792580
  83.2 22.0 %all-to-all-start.3 = ((f32[64,1,72]{2,1,0:T(1,128)}), f32[64,1,72]{2,1,0:T(1,128)S(1)}, u32[]{:S(2)}, u32[]{:S(2)}) async-start(f32[64,1,72]{2,1,0:T(1,128)} %bitcast.22), calls=%async_computation.3 | async-start | bytes 65536 | tf_op jit(solution)/shard_map/all_to_all | solution.py:226

commit v4 on v3

--- a/solution.py
+++ b/solution.py
@@ -1,3 +1,4 @@
+import functools
 import math
 
 import jax
@@ -74,10 +75,14 @@
     )[0]
 
 
-def banded_kernel(ahead_ref, behind_ref, pw_ref, gw_ref, fo_ref, bo_ref):
+def banded_kernel(ahead_ref, behind_ref, pw_ref, gw_ref, fo_ref, bo_ref, fg_ref, *, here):
     rows = fo_ref.shape[2]
     lanes = ahead_ref.shape[1]
     dims = (((1,), (1,)), ((), ()))
+    flip = (
+        lax.broadcasted_iota(jnp.int32, (here, here), 0) + lax.broadcasted_iota(jnp.int32, (here, here), 1)
+        == here - 1
+    ).astype(jnp.bfloat16)
     for group in range(ahead_ref.shape[0]):
         for row_ref, data_ref, out_ref in ((ahead_ref, pw_ref, fo_ref), (behind_ref, gw_ref, bo_ref)):
             band = pltpu.roll(
@@ -86,9 +91,15 @@
             out_ref[group] = lax.dot_general(
                 data_ref[group], band, dims, preferred_element_type=jnp.float32
             )
-
-
-def both_convs(product, grad_mixed, filters_low):
+        gm_rev = jnp.dot(gw_ref[group][:, :here], flip, preferred_element_type=jnp.float32).astype(jnp.bfloat16)
+        cross = lax.dot_general(
+            gm_rev, pw_ref[group], (((0,), (0,)), ((), ())), preferred_element_type=jnp.float32
+        )
+        diag = pltpu.roll(cross, lanes - here + 1, 1, stride=1, stride_axis=0)
+        fg_ref[group : group + 1, :] = jnp.sum(diag, axis=0, keepdims=True)[:, : fg_ref.shape[1]]
+
+
+def both_convs(product, grad_mixed, filters_low, here):
     channels, win = product.shape
     groups, taps = filters_low.shape
     out_len = win - taps + 1
@@ -100,16 +111,17 @@
     pw = jnp.pad(product, ((0, 0), (0, lanes - win))).reshape(groups, channels // groups, lanes)
     gw = jnp.pad(grad_mixed, ((0, 0), (0, lanes - win))).reshape(groups, channels // groups, lanes)
     spec = pl.BlockSpec(memory_space=pltpu.VMEM)
-    fo, bo = pl.pallas_call(
-        banded_kernel,
-        out_shape=(jax.ShapeDtypeStruct((groups, channels // groups, rows), jnp.float32),) * 2,
+    fo, bo, fg = pl.pallas_call(
+        functools.partial(banded_kernel, here=here),
+        out_shape=(jax.ShapeDtypeStruct((groups, channels // groups, rows), jnp.float32),) * 2
+        + (jax.ShapeDtypeStruct((groups, taps), jnp.float32),),
         in_specs=[spec] * 4,
-        out_specs=(spec, spec),
+        out_specs=(spec, spec, spec),
         cost_estimate=pl.CostEstimate(
-            flops=4 * channels * lanes * rows, transcendentals=0, bytes_accessed=4 * channels * (lanes + 2 * rows)
+            flops=4 * channels * lanes * (rows + here), transcendentals=0, bytes_accessed=4 * channels * (lanes + 2 * rows)
         ),
     )(ahead, behind, pw, gw)
-    return fo.reshape(channels, rows)[:, :out_len], bo.reshape(channels, rows)[:, :out_len]
+    return fo.reshape(channels, rows)[:, :out_len], bo.reshape(channels, rows)[:, :out_len], fg
 
 
 def shards(outer_gate, inner_gate, value_stream, grad_output, filters, feature_taps, skip_gain):
@@ -177,7 +189,7 @@
     filters_low = filters_all.astype(jnp.bfloat16)
     product_here = product[:, reach_cols:].astype(jnp.float32)
     grad_mixed = (upstream * outer_feat).astype(jnp.bfloat16)
-    convolved, ahead = both_convs(product, grad_mixed, filters_low)
+    convolved, ahead, filter_diag = both_convs(product, grad_mixed, filters_low, block_len)
     mixed = convolved + skip_all[:, None] * product_here
     gated_out = (outer_feat[:, :block_len] * mixed[:, :block_len]).astype(jnp.bfloat16)
 
@@ -192,10 +204,7 @@
 
     grad_scale = 1.0 / math.sqrt(ctx_size * block_len)
     gm_here = grad_mixed[:, :block_len]
-    filter_rev = depthwise(product[:, : block_len + reach_cols], gm_here)
-    filter_part = grad_scale * jnp.sum(
-        filter_rev.reshape(groups, group_size, taps_count), axis=1
-    )[:, ::-1]
+    filter_part = grad_scale * filter_diag[:, ::-1]
     skip_part = grad_scale * jnp.sum(
         gm_here.astype(jnp.float32) * product_here[:, :block_len], axis=1
     )

time: 108 us -> 107 us (level)
  matrix products: 7.06 us -> 0 us
  waiting for transfers between devices: 13.8 us -> 19.5 us
  local copies, waits for them, and re-layouts: 24.1 us -> 20.3 us
  Pallas kernels: 4.59 us -> 7.8 us
  starting transfers between devices: 43.3 us -> 44.4 us
    conv_general_dilated x1 -> x0, matrix products: 7.06 us -> none  [depthwise(): lax.conv_general_dilated(values[None], kernel[:, None, :], window_strides...]
    all_to_all x1, waiting for transfers between devices: 0.01 us -> 5.6 us  [shards(): by_owner = lax.all_to_all(to_fsdp, 'fsdp', 0, 0, tiled=True)]
    pallas_call x1, Pallas kernels: 4.59 us -> 7.8 us  [both_convs(): pl.pallas_call(functools.partial(banded_kernel, here=here), out_shape=(ja...]
    unnamed x68 -> x52, local copies, waits for them, and re-layouts: 8.57 us -> 6.29 us
    broadcast_in_dim x4 -> x0, local copies, waits for them, and re-layouts: 2.13 us -> none  [the longest x2 1.29 us: depthwise(): values[None]]
  transfers between devices with their start and end apart: 6 -> 6, of which waited for: 3 -> 4; matrix products, arithmetic and copies ran while one was open for 18% -> 9% of each run, Pallas kernels for 0% -> 0%
where the time goes in v4:
time: 107 us
  starting transfers between devices  44.4 us (41%)
  local copies, waits for them, and re-layouts  20.3 us (19%)
  waiting for transfers between devices  19.5 us (18%)
  other arithmetic  13.7 us (13%)
  Pallas kernels  7.8 us (7%)
  between operations  1.2 us (1%)
    all_to_all x1, starting transfers between devices, shards(): reduced = jnp.sum(lax.all_to_all(send, 'ctx', 0, 0, tiled=True), axis=0)  13.8 us
    all_to_all x1, starting transfers between devices, shards(): lax.all_to_all(jnp.broadcast_to(row[None], (ctx_size, row.shape[0])), 'ct...  11.6 us
    all_to_all x1, starting transfers between devices, shards(): moved = lax.all_to_all(gathered[:, n_filt:], 'fsdp', 0, 0, tiled=True)  10 us
    all_to_all x1, waiting for transfers between devices, shards(): reduced = jnp.sum(lax.all_to_all(send, 'ctx', 0, 0, tiled=True), axis=0)  8.31 us
    pallas_call x1, Pallas kernels, both_convs(): pl.pallas_call(functools.partial(banded_kernel, here=here), out_shape=(ja...  7.8 us
    unnamed x52, local copies, waits for them, and re-layouts  6.29 us
    all_to_all x1, waiting for transfers between devices, shards(): by_owner = lax.all_to_all(to_fsdp, 'fsdp', 0, 0, tiled=True)  5.6 us
    ppermute x2, starting transfers between devices, passed_along(): return lax.ppermute(shard, axis, pairs)  5.59 us
  transfers between devices with their start and end apart: 6, of which 4 were waited for; matrix products, arithmetic and copies ran while one was open for 9% of the time, Pallas kernels for 0%

profile of v4, /device:TPU:1, one launch (start us, length us, event | category | flops | bytes accessed | tf_op | source)
XLA Modules:
  0.0 106.8 jit_solution(12350527301154567822)
XLA Ops:
  0.7 0.8 reshape.153
  1.6 0.7 pad_maximum_fusion.6
  2.4 0.6 broadcast_in_dim.2
  3.0 11.6 %all-to-all-start = ((f32[64,1,72]{2,1,0:T(1,128)}), f32[64,1,72]{2,1,0:T(1,128)S(1)}, u32[]{:S(2)}, u32[]{:S(2)}) async-start(f32[64,1,72]{2,1,0:T(1,128)} %broadcast_in_dim.2), calls=%async_computation | async-start | bytes 65536 | tf_op jit(solution)/shard_map/all_to_all | solution.py:139
  14.6 0.9 slice.268
  15.7 0.8 copy-done.3
  16.8 3.7 %collective-permute-start = (bf16[256,260]{1,0:T(8,128)(2,1)S(1)}, bf16[256,260]{1,0:T(8,128)(2,1)S(1)}, u32[]{:S(2)}, u32[]{:S(2)}) collective-permute-start(bf16[256,260]{1,0:T(8,128)(2,1)S(1)} %pad_maximum_fusion), channel_id=1, source_target_pairs={{0,8},{8,16},{16,24},{24,32},{32,40},{40,48},{48,56},{56,64},{64,7... | collective-permute-start | bytes 399368 | tf_op jit(solution)/shard_map/ppermute | solution.py:15
  20.5 0.8 slice-done
  21.5 1.9 %collective-permute-start.1 = (bf16[256,262]{1,0:T(8,128)(2,1)S(1)}, bf16[256,262]{1,0:T(8,128)(2,1)S(1)}, u32[]{:S(2)}, u32[]{:S(2)}) collective-permute-start(bf16[256,262]{1,0:T(8,128)(2,1)S(1)} %pad_maximum_fusion.1), channel_id=1, source_target_pairs={{8,0},{16,8},{24,16},{32,24},{40,32},{48,40},{56,48},{64,56},{72,6... | collective-permute-start | bytes 402440 | tf_op jit(solution)/shard_map/ppermute | solution.py:15
  23.4 0.4 all-to-all-done
  24.0 0.7 reshape.166
  24.7 10.0 %all-to-all-start.1 = ((f32[8,1,320]{2,1,0:T(1,128)}), f32[8,1,320]{2,1,0:T(1,128)S(1)}, u32[]{:S(2)}, u32[]{:S(2)}) async-start(f32[8,1,320]{2,1,0:T(1,128)} %reshape.166), calls=%async_computation.1 | async-start | bytes 24576 | tf_op jit(solution)/shard_map/all_to_all | solution.py:151
  35.0 0.6 pad.15.behind_ref
  35.6 0.6 pad.14.ahead_ref
  36.3 5.1 %all-to-all-done.1 = f32[8,1,320]{2,1,0:T(1,128)S(1)} async-done(((f32[8,1,320]{2,1,0:T(1,128)}), f32[8,1,320]{2,1,0:T(1,128)S(1)}, u32[]{:S(2)}, u32[]{:S(2)}) %all-to-all-start.1) | async-done | bytes 10272 | tf_op jit(solution)/shard_map/all_to_all | solution.py:151
  41.4 0.5 broadcast.16
  41.9 0.7 reduce.1
  44.7 0.7 mul.279
  45.9 0.8 copy-done.2
  47.0 0.9 multiply_convert_fusion.1
  47.9 0.9 slice_convert_fusion
  48.8 0.7 pad.16
  49.7 1.3 %multiply_convert_fusion = (bf16[256,385]{1,0:T(8,128)(2,1)S(1)}, f32[256,385]{1,0:T(8,128)}) fusion(bf16[256,129]{1,0:T(8,128)(2,1)S(1)} %get-tuple-element.79, bf16[256,256]{1,0:T(8,128)(2,1)S(1)} %copy-done.4, f32[256,387]{1,0:T(8,128)S(1)} %maximum_convert_fusion, f32[256]{0:T(256)S(1)} %mul.256, f32[256]{0:T(256)S(1)} %mul.253, f32[256]{0:T(256)S(1)} %mul.250), kind=kLoop, calls=%fused_computation.15 | loop fusion | flops 1084160 | bytes 1974272 | tf_op jit(solution)/shard_map/convert_element_type | solution.py:191
  50.9 0.7 pad.17
  51.7 7.8 %shard_map.126 = (f32[16,16,272]{2,1,0:T(8,128)}, f32[16,16,272]{2,1,0:T(8,128)}, f32[16,128]{1,0:T(8,128)}) custom-call(f32[16,512]{1,0:T(8,128)} %pad.14.ahead_ref, f32[16,512]{1,0:T(8,128)} %pad.15.behind_ref, bf16[16,16,512]{2,1,0:T(8,128)(2,1)} %bitcast.61, bf16[16,16,512]{2,1,0:T(8,128)(2,1)} %bitcast.62), custom_call_target="tpu_custom_call" | custom-call | flops 276824064 | bytes 1081344 | tf_op jit(solution)/shard_map/pallas_call | solution.py:114
  59.5 0.7 copy-done.21
  60.1 2.3 %fusion.34 = (f32[256,258]{1,0:T(8,128)S(1)}, bf16[256,258]{1,0:T(8,128)(2,1)S(1)}, f32[256,258]{1,0:T(8,128)S(1)}, bf16[256,258]{1,0:T(8,128)(2,1)S(1)}, f32[25...) fusion(f32[256,385]{1,0:T(8,128)S(1)} %get-tuple-element.75, ...), kind=kLoop, calls=%fused_computation.94 | loop fusion | flops 990720 | bytes 3039232 | tf_op jit(solution)/shard_map/convert_element_type | solution.py:203
  62.4 0.3 fusion.10
  62.7 0.3 fusion.13
  63.1 0.3 copy-done.17
  63.4 0.3 copy-done.15
  63.7 1.0 fusion.20
  64.7 0.3 fusion.16
  65.0 0.3 copy-done.20
  67.4 0.4 copy-done.11
  67.9 1.0 fusion.23
  69.5 0.7 reshape.168
  70.2 3.3 %all-to-all-start.2 = ((f32[8,1,320]{2,1,0:T(1,128)}), f32[8,1,320]{2,1,0:T(1,128)S(1)}, u32[]{:S(2)}, u32[]{:S(2)}) async-start(f32[8,1,320]{2,1,0:T(1,128)} %reshape.168), calls=%async_computation.2 | async-start | bytes 24576 | tf_op jit(solution)/shard_map/all_to_all | solution.py:227
  73.6 0.7 fusion.28
  74.5 5.6 %all-to-all-done.2 = f32[8,1,320]{2,1,0:T(1,128)S(1)} async-done(((f32[8,1,320]{2,1,0:T(1,128)}), f32[8,1,320]{2,1,0:T(1,128)S(1)}, u32[]{:S(2)}, u32[]{:S(2)}) %all-to-all-start.2) | async-done | bytes 10272 | tf_op jit(solution)/shard_map/all_to_all | solution.py:227
  80.1 0.7 reduce.2
  80.9 0.7 pad_maximum_fusion.5
  81.6 13.8 %all-to-all-start.3 = ((f32[64,1,72]{2,1,0:T(1,128)}), f32[64,1,72]{2,1,0:T(1,128)S(1)}, u32[]{:S(2)}, u32[]{:S(2)}) async-start(f32[64,1,72]{2,1,0:T(1,128)} %bitcast.19), calls=%async_computation.3 | async-start | bytes 65536 | tf_op jit(solution)/shard_map/all_to_all | solution.py:235
  95.3 1.0 fusion.26
  96.3 8.3 %all-to-all-done.3 = f32[64,1,72]{2,1,0:T(1,128)S(1)} async-done(((f32[64,1,72]{2,1,0:T(1,128)}), f32[64,1,72]{2,1,0:T(1,128)S(1)}, u32[]{:S(2)}, u32[]{:S(2)}) %all-to-all-start.3) | async-done | bytes 18464 | tf_op jit(solution)/shard_map/all_to_all | solution.py:235
  104.7 0.6 slice.332
  105.4 0.7 reshape.163
  106.1 0.6 copy.157
  (123 shorter events, 7.2 us)
Async XLA Ops:
  0.6 0.8 copy-start.22
  0.6 14.9 %copy-start.1 = (bf16[256,256]{1,0:T(8,128)(2,1)S(1)}, bf16[256,256]{1,0:T(8,128)(2,1)}, u32[]{:S(2)}) copy-start(bf16[256,256]{1,0:T(8,128)(2,1)} %param.8) | copy-start | bytes 393220
  3.0 20.8 %all-to-all-start = ((f32[64,1,72]{2,1,0:T(1,128)}), f32[64,1,72]{2,1,0:T(1,128)S(1)}, u32[]{:S(2)}, u32[]{:S(2)}) async-start(f32[64,1,72]{2,1,0:T(1,128)} %broadcast_in_dim.2), calls=%async_computation | async-start | bytes 65536 | tf_op jit(solution)/shard_map/all_to_all | solution.py:139
  15.6 0.9 copy-start.3
  16.6 3.9 %copy-start.4 = (bf16[256,256]{1,0:T(8,128)(2,1)S(1)}, bf16[256,256]{1,0:T(8,128)(2,1)}, u32[]{:S(2)}) copy-start(bf16[256,256]{1,0:T(8,128)(2,1)} %param.10) | copy-start | bytes 393220
  16.8 3.7 %copy-start = (bf16[256,256]{1,0:T(8,128)(2,1)S(1)}, bf16[256,256]{1,0:T(8,128)(2,1)}, u32[]{:S(2)}) copy-start(bf16[256,256]{1,0:T(8,128)(2,1)} %param.7) | copy-start | bytes 393220
  16.8 28.6 %collective-permute-start = (bf16[256,260]{1,0:T(8,128)(2,1)S(1)}, bf16[256,260]{1,0:T(8,128)(2,1)S(1)}, u32[]{:S(2)}, u32[]{:S(2)}) collective-permute-start(bf16[256,260]{1,0:T(8,128)(2,1)S(1)} %pad_maximum_fusion), channel_id=1, source_target_pairs={{0,8},{8,16},{16,24},{24,32},{32,40},{40,48},{48,56},{56,64},{64,7... | collective-permute-start | bytes 399368 | tf_op jit(solution)/shard_map/ppermute | solution.py:15
  20.5 0.8 slice-start
  20.5 0.9 slice-start.1
  21.5 24.1 %collective-permute-start.1 = (bf16[256,262]{1,0:T(8,128)(2,1)S(1)}, bf16[256,262]{1,0:T(8,128)(2,1)S(1)}, u32[]{:S(2)}, u32[]{:S(2)}) collective-permute-start(bf16[256,262]{1,0:T(8,128)(2,1)S(1)} %pad_maximum_fusion.1), channel_id=1, source_target_pairs={{8,0},{16,8},{24,16},{32,24},{40,32},{48,40},{56,48},{64,56},{72,6... | collective-permute-start | bytes 402440 | tf_op jit(solution)/shard_map/ppermute | solution.py:15
  24.7 16.6 %all-to-all-start.1 = ((f32[8,1,320]{2,1,0:T(1,128)}), f32[8,1,320]{2,1,0:T(1,128)S(1)}, u32[]{:S(2)}, u32[]{:S(2)}) async-start(f32[8,1,320]{2,1,0:T(1,128)} %reshape.166), calls=%async_computation.1 | async-start | bytes 24576 | tf_op jit(solution)/shard_map/all_to_all | solution.py:151
  43.3 3.7 %copy-start.14 = (f32[256]{0:T(256)}, f32[256]{0:T(256)S(1)}, u32[]{:S(2)}) copy-start(f32[256]{0:T(256)S(1)} %mul.274) | copy-start | bytes 3076
  43.5 3.5 %copy-start.16 = (f32[256]{0:T(256)}, f32[256]{0:T(256)S(1)}, u32[]{:S(2)}) copy-start(f32[256]{0:T(256)S(1)} %mul.271) | copy-start | bytes 3076
  43.7 3.3 %copy-start.18 = (f32[256]{0:T(256)}, f32[256]{0:T(256)S(1)}, u32[]{:S(2)}) copy-start(f32[256]{0:T(256)S(1)} %mul.268) | copy-start | bytes 3076
  44.1 2.9 %copy-start.10 = (f32[256]{0:T(256)}, f32[256]{0:T(256)S(1)}, u32[]{:S(2)}) copy-start(f32[256]{0:T(256)S(1)} %mul.262) | copy-start | bytes 3076
  44.3 2.7 %copy-start.12 = (f32[256]{0:T(256)}, f32[256]{0:T(256)S(1)}, u32[]{:S(2)}) copy-start(f32[256]{0:T(256)S(1)} %mul.259) | copy-start | bytes 3076
  45.4 4.1 %copy-start.8 = (bf16[256,2]{1,0:T(8,128)(2,1)}, bf16[256,2]{1,0:T(8,128)(2,1)S(1)}, u32[]{:S(2)}) copy-start(bf16[256,2]{1,0:T(8,128)(2,1)S(1)} %slice.336) | copy-start | bytes 3076
  45.8 0.9 copy-start.2
  59.5 0.7 copy-start.21
  60.1 2.3 %copy-start.9 = (bf16[256,2]{1,0:T(8,128)(2,1)S(1)}, bf16[256,2]{1,0:T(8,128)(2,1)}, u32[]{:S(2)}) copy-start(bf16[256,2]{1,0:T(8,128)(2,1)} %copy-done.8) | copy-start | bytes 3076
  62.7 0.7 copy-start.17
  62.7 0.7 copy-start.19
  63.1 0.6 copy-start.15
  64.7 0.7 copy-start.20
  66.8 0.7 copy-start.13
  67.2 0.7 copy-start.11
  67.9 1.1 %copy-start.7 = (f32[256,258]{1,0:T(8,128)S(1)}, f32[256,258]{1,0:T(8,128)}, u32[]{:S(2)}) copy-start(f32[256,258]{1,0:T(8,128)} %slice_convert_fusion) | copy-start | bytes 792580
  69.0 4.6 %copy-start.5 = (f32[256,385]{1,0:T(8,128)S(1)}, f32[256,385]{1,0:T(8,128)}, u32[]{:S(2)}) copy-start(f32[256,385]{1,0:T(8,128)} %get-tuple-element.72) | copy-start | bytes 1182724
  69.1 4.4 %copy-start.6 = (f32[256,258]{1,0:T(8,128)S(1)}, f32[256,258]{1,0:T(8,128)}, u32[]{:S(2)}) copy-start(f32[256,258]{1,0:T(8,128)} %get-tuple-element.95) | copy-start | bytes 792580
  70.2 9.9 %all-to-all-start.2 = ((f32[8,1,320]{2,1,0:T(1,128)}), f32[8,1,320]{2,1,0:T(1,128)S(1)}, u32[]{:S(2)}, u32[]{:S(2)}) async-start(f32[8,1,320]{2,1,0:T(1,128)} %reshape.168), calls=%async_computation.2 | async-start | bytes 24576 | tf_op jit(solution)/shard_map/all_to_all | solution.py:227
  81.6 23.1 %all-to-all-start.3 = ((f32[64,1,72]{2,1,0:T(1,128)}), f32[64,1,72]{2,1,0:T(1,128)S(1)}, u32[]{:S(2)}, u32[]{:S(2)}) async-start(f32[64,1,72]{2,1,0:T(1,128)} %bitcast.19), calls=%async_computation.3 | async-start | bytes 65536 | tf_op jit(solution)/shard_map/all_to_all | solution.py:235

commit v5 on v4

--- a/solution.py
+++ b/solution.py
@@ -77,7 +77,7 @@
 
 def banded_kernel(ahead_ref, behind_ref, pw_ref, gw_ref, fo_ref, bo_ref, fg_ref, *, here):
     rows = fo_ref.shape[2]
-    lanes = ahead_ref.shape[1]
+    lanes = ahead_ref.shape[2]
     dims = (((1,), (1,)), ((), ()))
     flip = (
         lax.broadcasted_iota(jnp.int32, (here, here), 0) + lax.broadcasted_iota(jnp.int32, (here, here), 1)
@@ -86,7 +86,7 @@
     for group in range(ahead_ref.shape[0]):
         for row_ref, data_ref, out_ref in ((ahead_ref, pw_ref, fo_ref), (behind_ref, gw_ref, bo_ref)):
             band = pltpu.roll(
-                jnp.broadcast_to(row_ref[group : group + 1, :], (rows, lanes)), 0, 1, stride=1, stride_axis=0
+                jnp.broadcast_to(row_ref[group], (rows, lanes)), 0, 1, stride=1, stride_axis=0
             ).astype(jnp.bfloat16)
             out_ref[group] = lax.dot_general(
                 data_ref[group], band, dims, preferred_element_type=jnp.float32
@@ -96,7 +96,7 @@
             gm_rev, pw_ref[group], (((0,), (0,)), ((), ())), preferred_element_type=jnp.float32
         )
         diag = pltpu.roll(cross, lanes - here + 1, 1, stride=1, stride_axis=0)
-        fg_ref[group : group + 1, :] = jnp.sum(diag, axis=0, keepdims=True)[:, : fg_ref.shape[1]]
+        fg_ref[group] = jnp.sum(diag, axis=0, keepdims=True)[:, : fg_ref.shape[2]]
 
 
 def both_convs(product, grad_mixed, filters_low, here):
@@ -106,22 +106,29 @@
     rows = -(-out_len // 16) * 16
     lanes = -(-max(win, rows + taps - 1) // 128) * 128
     as_rows = filters_low.astype(jnp.float32)
-    ahead = jnp.pad(as_rows[:, ::-1], ((0, 0), (0, lanes - taps)))
-    behind = jnp.pad(as_rows, ((0, 0), (0, lanes - taps)))
+    ahead = jnp.pad(as_rows[:, ::-1], ((0, 0), (0, lanes - taps))).reshape(groups, 1, lanes)
+    behind = jnp.pad(as_rows, ((0, 0), (0, lanes - taps))).reshape(groups, 1, lanes)
     pw = jnp.pad(product, ((0, 0), (0, lanes - win))).reshape(groups, channels // groups, lanes)
     gw = jnp.pad(grad_mixed, ((0, 0), (0, lanes - win))).reshape(groups, channels // groups, lanes)
-    spec = pl.BlockSpec(memory_space=pltpu.VMEM)
+    step = math.gcd(groups, 4)
+    size = channels // groups
+
+    def blocks(*tail):
+        return pl.BlockSpec((step,) + tail, lambda i: (i, 0, 0))
+
     fo, bo, fg = pl.pallas_call(
         functools.partial(banded_kernel, here=here),
-        out_shape=(jax.ShapeDtypeStruct((groups, channels // groups, rows), jnp.float32),) * 2
-        + (jax.ShapeDtypeStruct((groups, taps), jnp.float32),),
-        in_specs=[spec] * 4,
-        out_specs=(spec, spec, spec),
+        out_shape=(jax.ShapeDtypeStruct((groups, size, rows), jnp.float32),) * 2
+        + (jax.ShapeDtypeStruct((groups, 1, taps), jnp.float32),),
+        grid=(groups // step,),
+        in_specs=[blocks(1, lanes), blocks(1, lanes), blocks(size, lanes), blocks(size, lanes)],
+        out_specs=(blocks(size, rows), blocks(size, rows), blocks(1, taps)),
+        compiler_params=pltpu.CompilerParams(vmem_limit_bytes=8 * 1024 * 1024),
         cost_estimate=pl.CostEstimate(
             flops=4 * channels * lanes * (rows + here), transcendentals=0, bytes_accessed=4 * channels * (lanes + 2 * rows)
         ),
     )(ahead, behind, pw, gw)
-    return fo.reshape(channels, rows)[:, :out_len], bo.reshape(channels, rows)[:, :out_len], fg
+    return fo.reshape(channels, rows)[:, :out_len], bo.reshape(channels, rows)[:, :out_len], fg.reshape(groups, taps)
 
 
 def shards(outer_gate, inner_gate, value_stream, grad_output, filters, feature_taps, skip_gain):

time: 107 us -> 99 us (0.925)
  local copies, waits for them, and re-layouts: 20.3 us -> 14.8 us
  other arithmetic: 13.7 us -> 10.3 us
  waiting for transfers between devices: 19.5 us -> 20.6 us
    unnamed x52 -> x18, local copies, waits for them, and re-layouts: 6.29 us -> 3.9 us
    convert_element_type x1, other arithmetic: 2.25 us -> 0.38 us  [shards(): grad_value = carry_back(grad_value_feat.astype(jnp.float32), taps_all[2])]
    pad x2, local copies, waits for them, and re-layouts: 1.26 us -> 0.01 us  [the longest x1 0.01 us: both_convs(): jnp.pad(as_rows[:, ::-1], ((0, 0), (0, lanes - taps)))]
    all_to_all x1, waiting for transfers between devices: 5.11 us -> 6.27 us  [shards(): moved = lax.all_to_all(gathered[:, n_filt:], 'fsdp', 0, 0, tiled=True)]
  transfers between devices with their start and end apart: 6 -> 6, of which waited for: 4 -> 4; matrix products, arithmetic and copies ran while one was open for 9% -> 8% of each run, Pallas kernels for 0% -> 0%
where the time goes in v5:
time: 99 us; the launch traced here: 98.5 us
  starting transfers between devices  44.4 us (45%)
  waiting for transfers between devices  20.6 us (21%)
  local copies, waits for them, and re-layouts  14.8 us (15%)
  other arithmetic  10.3 us (10%)
  Pallas kernels  7.3 us (7%)
  between operations  1.12 us (1%)
    all_to_all x1, starting transfers between devices, shards(): reduced = jnp.sum(lax.all_to_all(send, 'ctx', 0, 0, tiled=True), axis=0)  13.8 us
    all_to_all x1, starting transfers between devices, shards(): lax.all_to_all(jnp.broadcast_to(row[None], (ctx_size, row.shape[0])), 'ct...  11.6 us
    all_to_all x1, starting transfers between devices, shards(): moved = lax.all_to_all(gathered[:, n_filt:], 'fsdp', 0, 0, tiled=True)  10 us
    all_to_all x1, waiting for transfers between devices, shards(): reduced = jnp.sum(lax.all_to_all(send, 'ctx', 0, 0, tiled=True), axis=0)  8.32 us
    pallas_call x1, Pallas kernels, both_convs(): pl.pallas_call(functools.partial(banded_kernel, here=here), out_shape=(ja...  7.3 us
    all_to_all x1, waiting for transfers between devices, shards(): moved = lax.all_to_all(gathered[:, n_filt:], 'fsdp', 0, 0, tiled=True)  6.27 us
    all_to_all x1, waiting for transfers between devices, shards(): by_owner = lax.all_to_all(to_fsdp, 'fsdp', 0, 0, tiled=True)  5.62 us
    ppermute x2, starting transfers between devices, passed_along(): return lax.ppermute(shard, axis, pairs)  5.59 us
  transfers between devices with their start and end apart: 6, of which 4 were waited for; matrix products, arithmetic and copies ran while one was open for 8% of the time, Pallas kernels for 0%

profile of v5, /device:TPU:1, one launch (start us, length us, event | category | flops | bytes accessed | tf_op | source)
XLA Modules:
  0.0 98.5 jit_solution(12584092688564384863)
XLA Ops:
  0.7 0.8 reshape.162
  1.6 0.7 pad_maximum_fusion.6
  2.4 0.6 broadcast_in_dim.2
  3.0 11.6 %all-to-all-start = ((f32[64,1,72]{2,1,0:T(1,128)}), f32[64,1,72]{2,1,0:T(1,128)S(1)}, u32[]{:S(2)}, u32[]{:S(2)}) async-start(f32[64,1,72]{2,1,0:T(1,128)} %broadcast_in_dim.2), calls=%async_computation | async-start | bytes 65536 | tf_op jit(solution)/shard_map/all_to_all | solution.py:146
  14.6 0.9 slice.268
  15.7 0.8 copy-done.3
  16.6 0.2 pad_maximum_fusion
  16.8 3.7 %collective-permute-start = (bf16[256,260]{1,0:T(8,128)(2,1)S(1)}, bf16[256,260]{1,0:T(8,128)(2,1)S(1)}, u32[]{:S(2)}, u32[]{:S(2)}) collective-permute-start(bf16[256,260]{1,0:T(8,128)(2,1)S(1)} %pad_maximum_fusion), channel_id=1, source_target_pairs={{0,8},{8,16},{16,24},{24,32},{32,40},{40,48},{48,56},{56,64},{64,7... | collective-permute-start | bytes 399368 | tf_op jit(solution)/shard_map/ppermute | solution.py:15
  20.5 0.8 slice-done
  21.3 0.1 pad_maximum_fusion.1
  21.5 1.9 %collective-permute-start.1 = (bf16[256,262]{1,0:T(8,128)(2,1)S(1)}, bf16[256,262]{1,0:T(8,128)(2,1)S(1)}, u32[]{:S(2)}, u32[]{:S(2)}) collective-permute-start(bf16[256,262]{1,0:T(8,128)(2,1)S(1)} %pad_maximum_fusion.1), channel_id=1, source_target_pairs={{8,0},{16,8},{24,16},{32,24},{40,32},{48,40},{56,48},{64,56},{72,6... | collective-permute-start | bytes 402440 | tf_op jit(solution)/shard_map/ppermute | solution.py:15
  23.4 0.4 all-to-all-done
  24.0 0.7 reshape.178
  24.7 10.0 %all-to-all-start.1 = ((f32[8,1,320]{2,1,0:T(1,128)}), f32[8,1,320]{2,1,0:T(1,128)S(1)}, u32[]{:S(2)}, u32[]{:S(2)}) async-start(f32[8,1,320]{2,1,0:T(1,128)} %reshape.178), calls=%async_computation.1 | async-start | bytes 24576 | tf_op jit(solution)/shard_map/all_to_all | solution.py:158
  35.1 6.3 %all-to-all-done.1 = f32[8,1,320]{2,1,0:T(1,128)S(1)} async-done(((f32[8,1,320]{2,1,0:T(1,128)}), f32[8,1,320]{2,1,0:T(1,128)S(1)}, u32[]{:S(2)}, u32[]{:S(2)}) %all-to-all-start.1) | async-done | bytes 10272 | tf_op jit(solution)/shard_map/all_to_all | solution.py:158
  41.4 0.5 broadcast.16
  41.9 0.7 reduce.1
  44.8 0.1 fusion.44
  45.3 0.8 copy-done.2
  46.1 0.3 maximum_convert_fusion.1
  46.4 0.9 multiply_convert_fusion.1
  47.3 0.1 slice_convert_fusion
  47.4 0.2 maximum_convert_fusion
  47.6 0.5 multiply_convert_fusion
  48.1 7.3 %shard_map.126 = (f32[16,16,272]{2,1,0:T(8,128)S(1)}, f32[16,16,272]{2,1,0:T(8,128)S(1)}, f32[16,1,128]{2,1,0:T(1,128)S(1)}) custom-call(f32[16,1,512]{2,1,0:T(1,128)S(1)} %reshape.165.ahead_ref, f32[16,1,512]{2,1,0:T(1,128)S(1)} %reshape.166.behind_ref, bf16[16,16,512]{2,1,0:T(8,128)(2,1)S(1)} %bitcast.58, bf16[16,16,512]{2,1,0:T(8,128)(2,1)S(1)} %bitcast.59), custom_call_target="tpu_custom_call" | custom-call | flops 276824064 | bytes 1081344 | tf_op jit(solution)/shard_map/pallas_call | solution.py:119
  55.4 0.4 fusion.34
  55.8 0.3 fusion.10
  56.1 0.4 fusion.13
  56.5 1.0 fusion.20
  57.5 0.3 fusion.16
  58.1 0.1 stack.47
  59.2 0.1 stack.44
  59.4 0.1 stack.42
  59.6 1.0 fusion.23
  60.7 0.1 fusion.18
  60.9 0.1 copy.154
  61.2 0.7 reshape.180
  61.9 3.3 %all-to-all-start.2 = ((f32[8,1,320]{2,1,0:T(1,128)}), f32[8,1,320]{2,1,0:T(1,128)S(1)}, u32[]{:S(2)}, u32[]{:S(2)}) async-start(f32[8,1,320]{2,1,0:T(1,128)} %reshape.180), calls=%async_computation.2 | async-start | bytes 24576 | tf_op jit(solution)/shard_map/all_to_all | solution.py:234
  65.3 0.7 fusion.28
  66.2 5.6 %all-to-all-done.2 = f32[8,1,320]{2,1,0:T(1,128)S(1)} async-done(((f32[8,1,320]{2,1,0:T(1,128)}), f32[8,1,320]{2,1,0:T(1,128)S(1)}, u32[]{:S(2)}, u32[]{:S(2)}) %all-to-all-start.2) | async-done | bytes 10272 | tf_op jit(solution)/shard_map/all_to_all | solution.py:234
  71.8 0.7 reduce.2
  72.6 0.7 pad_maximum_fusion.5
  73.3 13.8 %all-to-all-start.3 = ((f32[64,1,72]{2,1,0:T(1,128)}), f32[64,1,72]{2,1,0:T(1,128)S(1)}, u32[]{:S(2)}, u32[]{:S(2)}) async-start(f32[64,1,72]{2,1,0:T(1,128)} %bitcast.20), calls=%async_computation.3 | async-start | bytes 65536 | tf_op jit(solution)/shard_map/all_to_all | solution.py:242
  87.1 1.0 fusion.26
  88.0 8.3 %all-to-all-done.3 = f32[64,1,72]{2,1,0:T(1,128)S(1)} async-done(((f32[64,1,72]{2,1,0:T(1,128)}), f32[64,1,72]{2,1,0:T(1,128)S(1)}, u32[]{:S(2)}, u32[]{:S(2)}) %all-to-all-start.3) | async-done | bytes 18464 | tf_op jit(solution)/shard_map/all_to_all | solution.py:242
  96.4 0.6 slice.332
  97.1 0.7 reshape.175
  97.9 0.6 copy.158
  (91 shorter events, 5.7 us)
Async XLA Ops:
  0.6 0.8 copy-start.5
  0.6 14.9 %copy-start.1 = (bf16[256,256]{1,0:T(8,128)(2,1)S(1)}, bf16[256,256]{1,0:T(8,128)(2,1)}, u32[]{:S(2)}) copy-start(bf16[256,256]{1,0:T(8,128)(2,1)} %param.8) | copy-start | bytes 393220
  3.0 20.8 %all-to-all-start = ((f32[64,1,72]{2,1,0:T(1,128)}), f32[64,1,72]{2,1,0:T(1,128)S(1)}, u32[]{:S(2)}, u32[]{:S(2)}) async-start(f32[64,1,72]{2,1,0:T(1,128)} %broadcast_in_dim.2), calls=%async_computation | async-start | bytes 65536 | tf_op jit(solution)/shard_map/all_to_all | solution.py:146
  15.6 0.9 copy-start.3
  16.6 3.9 %copy-start.4 = (bf16[256,256]{1,0:T(8,128)(2,1)S(1)}, bf16[256,256]{1,0:T(8,128)(2,1)}, u32[]{:S(2)}) copy-start(bf16[256,256]{1,0:T(8,128)(2,1)} %param.10) | copy-start | bytes 393220
  16.8 3.7 %copy-start = (bf16[256,256]{1,0:T(8,128)(2,1)S(1)}, bf16[256,256]{1,0:T(8,128)(2,1)}, u32[]{:S(2)}) copy-start(bf16[256,256]{1,0:T(8,128)(2,1)} %param.7) | copy-start | bytes 393220
  16.8 28.0 %collective-permute-start = (bf16[256,260]{1,0:T(8,128)(2,1)S(1)}, bf16[256,260]{1,0:T(8,128)(2,1)S(1)}, u32[]{:S(2)}, u32[]{:S(2)}) collective-permute-start(bf16[256,260]{1,0:T(8,128)(2,1)S(1)} %pad_maximum_fusion), channel_id=1, source_target_pairs={{0,8},{8,16},{16,24},{24,32},{32,40},{40,48},{48,56},{56,64},{64,7... | collective-permute-start | bytes 399368 | tf_op jit(solution)/shard_map/ppermute | solution.py:15
  20.5 0.8 slice-start
  20.5 0.9 slice-start.1
  21.5 23.5 %collective-permute-start.1 = (bf16[256,262]{1,0:T(8,128)(2,1)S(1)}, bf16[256,262]{1,0:T(8,128)(2,1)S(1)}, u32[]{:S(2)}, u32[]{:S(2)}) collective-permute-start(bf16[256,262]{1,0:T(8,128)(2,1)S(1)} %pad_maximum_fusion.1), channel_id=1, source_target_pairs={{8,0},{16,8},{24,16},{32,24},{40,32},{48,40},{56,48},{64,56},{72,6... | collective-permute-start | bytes 402440 | tf_op jit(solution)/shard_map/ppermute | solution.py:15
  24.7 16.6 %all-to-all-start.1 = ((f32[8,1,320]{2,1,0:T(1,128)}), f32[8,1,320]{2,1,0:T(1,128)S(1)}, u32[]{:S(2)}, u32[]{:S(2)}) async-start(f32[8,1,320]{2,1,0:T(1,128)} %reshape.178), calls=%async_computation.1 | async-start | bytes 24576 | tf_op jit(solution)/shard_map/all_to_all | solution.py:158
  45.2 0.9 copy-start.2
  61.9 9.9 %all-to-all-start.2 = ((f32[8,1,320]{2,1,0:T(1,128)}), f32[8,1,320]{2,1,0:T(1,128)S(1)}, u32[]{:S(2)}, u32[]{:S(2)}) async-start(f32[8,1,320]{2,1,0:T(1,128)} %reshape.180), calls=%async_computation.2 | async-start | bytes 24576 | tf_op jit(solution)/shard_map/all_to_all | solution.py:234
  73.3 23.1 %all-to-all-start.3 = ((f32[64,1,72]{2,1,0:T(1,128)}), f32[64,1,72]{2,1,0:T(1,128)S(1)}, u32[]{:S(2)}, u32[]{:S(2)}) async-start(f32[64,1,72]{2,1,0:T(1,128)} %bitcast.20), calls=%async_computation.3 | async-start | bytes 65536 | tf_op jit(solution)/shard_map/all_to_all | solution.py:242

commit v6 on v5

--- a/solution.py
+++ b/solution.py
@@ -198,16 +198,11 @@
     grad_mixed = (upstream * outer_feat).astype(jnp.bfloat16)
     convolved, ahead, filter_diag = both_convs(product, grad_mixed, filters_low, block_len)
     mixed = convolved + skip_all[:, None] * product_here
-    gated_out = (outer_feat[:, :block_len] * mixed[:, :block_len]).astype(jnp.bfloat16)
 
     grad_outer_feat = (upstream[:, :out_len] * mixed).astype(jnp.bfloat16)
     grad_product = ahead + skip_all[:, None] * grad_mixed[:, :out_len].astype(jnp.float32)
     grad_inner_feat = (grad_product * value_feat[:, reach_cols:]).astype(jnp.bfloat16)
     grad_value_feat = (grad_product * inner_feat[:, reach_cols:]).astype(jnp.bfloat16)
-
-    grad_outer = carry_back(grad_outer_feat.astype(jnp.float32), taps_all[0])
-    grad_inner = carry_back(grad_inner_feat.astype(jnp.float32), taps_all[1])
-    grad_value = carry_back(grad_value_feat.astype(jnp.float32), taps_all[2])
 
     grad_scale = 1.0 / math.sqrt(ctx_size * block_len)
     gm_here = grad_mixed[:, :block_len]
@@ -232,6 +227,14 @@
     )
     to_fsdp = chunk_parts.reshape(per_block, fsdp_size, n_chunk).transpose(1, 0, 2).reshape(ctx_size, n_chunk)
     by_owner = lax.all_to_all(to_fsdp, "fsdp", 0, 0, tiled=True)
+    by_owner, outer_feat, mixed, grad_outer_feat, grad_inner_feat, grad_value_feat = lax.optimization_barrier(
+        (by_owner, outer_feat, mixed, grad_outer_feat, grad_inner_feat, grad_value_feat)
+    )
+    gated_out = (outer_feat[:, :block_len] * mixed[:, :block_len]).astype(jnp.bfloat16)
+    grad_outer = carry_back(grad_outer_feat.astype(jnp.float32), taps_all[0])
+    grad_inner = carry_back(grad_inner_feat.astype(jnp.float32), taps_all[1])
+    grad_value = carry_back(grad_value_feat.astype(jnp.float32), taps_all[2])
+
     send = jnp.concatenate(
         [
             filter_part.reshape(groups, ctx_size, taps_here).transpose(1, 0, 2).reshape(ctx_size, -1),

time: 99 us -> 97.1 us (0.981)
  waiting for transfers between devices: 20.6 us -> 18.6 us
    all_to_all x1, waiting for transfers between devices: 8.32 us -> 5.6 us  [shards(): reduced = jnp.sum(lax.all_to_all(send, 'ctx', 0, 0, tiled=True), axis=0)]
  transfers between devices with their start and end apart: 6 -> 6, of which waited for: 4 -> 4; matrix products, arithmetic and copies ran while one was open for 8% -> 10% of each run, Pallas kernels for 0% -> 0%
where the time goes in v6:
time: 97.1 us; the launch traced here: 96.6 us
  starting transfers between devices  44.4 us (46%)
  waiting for transfers between devices  18.6 us (19%)
  local copies, waits for them, and re-layouts  14.8 us (15%)
  other arithmetic  10.4 us (11%)
  Pallas kernels  7.29 us (8%)
  between operations  1.15 us (1%)
    all_to_all x1, starting transfers between devices, shards(): reduced = jnp.sum(lax.all_to_all(send, 'ctx', 0, 0, tiled=True), axis=0)  13.8 us
    all_to_all x1, starting transfers between devices, shards(): lax.all_to_all(jnp.broadcast_to(row[None], (ctx_size, row.shape[0])), 'ct...  11.6 us
    all_to_all x1, starting transfers between devices, shards(): moved = lax.all_to_all(gathered[:, n_filt:], 'fsdp', 0, 0, tiled=True)  10 us
    pallas_call x1, Pallas kernels, both_convs(): pl.pallas_call(functools.partial(banded_kernel, here=here), out_shape=(ja...  7.29 us
    all_to_all x1, waiting for transfers between devices, shards(): by_owner = lax.all_to_all(to_fsdp, 'fsdp', 0, 0, tiled=True)  6.3 us
    all_to_all x1, waiting for transfers between devices, shards(): moved = lax.all_to_all(gathered[:, n_filt:], 'fsdp', 0, 0, tiled=True)  6.27 us
    all_to_all x1, waiting for transfers between devices, shards(): reduced = jnp.sum(lax.all_to_all(send, 'ctx', 0, 0, tiled=True), axis=0)  5.6 us
    ppermute x2, starting transfers between devices, passed_along(): return lax.ppermute(shard, axis, pairs)  5.59 us
  transfers between devices with their start and end apart: 6, of which 4 were waited for; matrix products, arithmetic and copies ran while one was open for 10% of the time, Pallas kernels for 0%

profile of v6, /device:TPU:1, one launch (start us, length us, event | category | flops | bytes accessed | tf_op | source)
XLA Modules:
  0.0 96.6 jit_solution(5387369707959140121)
XLA Ops:
  0.7 0.8 reshape.162
  1.6 0.7 pad_maximum_fusion.6
  2.4 0.6 broadcast_in_dim.2
  3.0 11.6 %all-to-all-start = ((f32[64,1,72]{2,1,0:T(1,128)}), f32[64,1,72]{2,1,0:T(1,128)S(1)}, u32[]{:S(2)}, u32[]{:S(2)}) async-start(f32[64,1,72]{2,1,0:T(1,128)} %broadcast_in_dim.2), calls=%async_computation | async-start | bytes 65536 | tf_op jit(solution)/shard_map/all_to_all | solution.py:146
  14.6 0.9 slice.275
  15.7 0.8 copy-done.2
  16.6 0.2 pad_maximum_fusion.1
  16.8 3.7 %collective-permute-start.1 = (bf16[256,260]{1,0:T(8,128)(2,1)S(1)}, bf16[256,260]{1,0:T(8,128)(2,1)S(1)}, u32[]{:S(2)}, u32[]{:S(2)}) collective-permute-start(bf16[256,260]{1,0:T(8,128)(2,1)S(1)} %pad_maximum_fusion.1), channel_id=1, source_target_pairs={{0,8},{8,16},{16,24},{24,32},{32,40},{40,48},{48,56},{56,64},{64,7... | collective-permute-start | bytes 399368 | tf_op jit(solution)/shard_map/ppermute | solution.py:15
  20.5 0.8 slice-done
  21.3 0.1 pad_maximum_fusion
  21.5 1.9 %collective-permute-start = (bf16[256,262]{1,0:T(8,128)(2,1)S(1)}, bf16[256,262]{1,0:T(8,128)(2,1)S(1)}, u32[]{:S(2)}, u32[]{:S(2)}) collective-permute-start(bf16[256,262]{1,0:T(8,128)(2,1)S(1)} %pad_maximum_fusion), channel_id=1, source_target_pairs={{8,0},{16,8},{24,16},{32,24},{40,32},{48,40},{56,48},{64,56},{72,6... | collective-permute-start | bytes 402440 | tf_op jit(solution)/shard_map/ppermute | solution.py:15
  23.4 0.4 all-to-all-done
  24.0 0.7 reshape.178
  24.7 10.0 %all-to-all-start.1 = ((f32[8,1,320]{2,1,0:T(1,128)}), f32[8,1,320]{2,1,0:T(1,128)S(1)}, u32[]{:S(2)}, u32[]{:S(2)}) async-start(f32[8,1,320]{2,1,0:T(1,128)} %reshape.178), calls=%async_computation.1 | async-start | bytes 24576 | tf_op jit(solution)/shard_map/all_to_all | solution.py:158
  35.1 6.3 %all-to-all-done.1 = f32[8,1,320]{2,1,0:T(1,128)S(1)} async-done(((f32[8,1,320]{2,1,0:T(1,128)}), f32[8,1,320]{2,1,0:T(1,128)S(1)}, u32[]{:S(2)}, u32[]{:S(2)}) %all-to-all-start.1) | async-done | bytes 10272 | tf_op jit(solution)/shard_map/all_to_all | solution.py:158
  41.4 0.5 broadcast.16
  41.9 0.7 reduce.1
  44.8 0.1 fusion.37
  45.3 0.8 copy-done.1
  46.1 0.3 maximum_convert_fusion.1
  46.4 0.9 multiply_convert_fusion.1
  47.3 0.1 slice_convert_fusion
  47.4 0.2 maximum_convert_fusion.3
  47.6 0.5 multiply_convert_fusion
  48.1 7.3 %shard_map.126 = (f32[16,16,272]{2,1,0:T(8,128)S(1)}, f32[16,16,272]{2,1,0:T(8,128)S(1)}, f32[16,1,128]{2,1,0:T(1,128)S(1)}) custom-call(f32[16,1,512]{2,1,0:T(1,128)S(1)} %reshape.163.ahead_ref, f32[16,1,512]{2,1,0:T(1,128)S(1)} %reshape.164.behind_ref, bf16[16,16,512]{2,1,0:T(8,128)(2,1)S(1)} %bitcast.58, bf16[16,16,512]{2,1,0:T(8,128)(2,1)S(1)} %bitcast.59), custom_call_target="tpu_custom_call" | custom-call | flops 276824064 | bytes 1081344 | tf_op jit(solution)/shard_map/pallas_call | solution.py:119
  55.4 0.4 fusion.8
  55.8 0.4 fusion.13
  56.2 0.4 fusion.16
  56.5 0.3 fusion.10
  57.1 0.1 stack.51
  57.3 0.1 stack.43
  57.5 0.1 stack.48
  58.8 0.1 fusion.27
  59.0 0.1 copy.121
  59.3 0.7 reshape.180
  60.0 3.3 %all-to-all-start.2 = ((f32[8,1,320]{2,1,0:T(1,128)}), f32[8,1,320]{2,1,0:T(1,128)S(1)}, u32[]{:S(2)}, u32[]{:S(2)}) async-start(f32[8,1,320]{2,1,0:T(1,128)} %reshape.180), calls=%async_computation.2 | async-start | bytes 24576 | tf_op jit(solution)/shard_map/all_to_all | solution.py:229
  63.6 6.3 %all-to-all-done.2 = f32[8,1,320]{2,1,0:T(1,128)S(1)} async-done(((f32[8,1,320]{2,1,0:T(1,128)}), f32[8,1,320]{2,1,0:T(1,128)S(1)}, u32[]{:S(2)}, u32[]{:S(2)}) %all-to-all-start.2) | async-done | bytes 10272 | tf_op jit(solution)/shard_map/all_to_all | solution.py:229
  69.9 0.7 reduce.2
  70.7 0.7 pad_maximum_fusion.5
  71.4 13.8 %all-to-all-start.3 = ((f32[64,1,72]{2,1,0:T(1,128)}), f32[64,1,72]{2,1,0:T(1,128)S(1)}, u32[]{:S(2)}, u32[]{:S(2)}) async-start(f32[64,1,72]{2,1,0:T(1,128)} %bitcast.20), calls=%async_computation.3 | async-start | bytes 65536 | tf_op jit(solution)/shard_map/all_to_all | solution.py:245
  85.2 1.0 %fusion.25 = bf16[256,256]{1,0:T(8,128)(2,1)} fusion(f32[256,258]{1,0:T(8,128)S(1)} %convert_element_type.144, f32[256]{0:T(256)S(1)} %mul.275, f32[256]{0:T(256)S(1)} %mul.272, f32[256]{0:T(256)S(1)} %mul.269), kind=kLoop, calls=%fused_computation.57 | loop fusion | flops 393216 | bytes 920576 | tf_op jit(solution)/shard_map/convert_element_type | solution.py:251
  86.2 1.0 %fusion.22 = bf16[256,256]{1,0:T(8,128)(2,1)} fusion(f32[256,258]{1,0:T(8,128)S(1)} %convert_element_type.146, f32[256]{0:T(256)S(1)} %mul.256, f32[256]{0:T(256)S(1)} %mul.253, f32[256]{0:T(256)S(1)} %mul.250), kind=kLoop, calls=%fused_computation.51 | loop fusion | flops 393216 | bytes 920576 | tf_op jit(solution)/shard_map/convert_element_type | solution.py:252
  87.2 0.7 multiply_convert_fusion.2
  87.9 1.0 %fusion.19 = bf16[256,256]{1,0:T(8,128)(2,1)} fusion(f32[256,258]{1,0:T(8,128)S(1)} %convert_element_type.148, f32[256]{0:T(256)S(1)} %mul.265, f32[256]{0:T(256)S(1)} %mul.262, f32[256]{0:T(256)S(1)} %mul.259), kind=kLoop, calls=%fused_computation.45 | loop fusion | flops 393216 | bytes 920576 | tf_op jit(solution)/shard_map/convert_element_type | solution.py:253
  88.9 5.6 %all-to-all-done.3 = f32[64,1,72]{2,1,0:T(1,128)S(1)} async-done(((f32[64,1,72]{2,1,0:T(1,128)}), f32[64,1,72]{2,1,0:T(1,128)S(1)}, u32[]{:S(2)}, u32[]{:S(2)}) %all-to-all-start.3) | async-done | bytes 18464 | tf_op jit(solution)/shard_map/all_to_all | solution.py:245
  94.5 0.6 slice.332
  95.2 0.7 reshape.175
  96.0 0.6 copy.127
  (94 shorter events, 5.8 us)
Async XLA Ops:
  0.6 0.8 copy-start.5
  0.6 14.9 %copy-start = (bf16[256,256]{1,0:T(8,128)(2,1)S(1)}, bf16[256,256]{1,0:T(8,128)(2,1)}, u32[]{:S(2)}) copy-start(bf16[256,256]{1,0:T(8,128)(2,1)} %param.8) | copy-start | bytes 393220
  3.0 20.8 %all-to-all-start = ((f32[64,1,72]{2,1,0:T(1,128)}), f32[64,1,72]{2,1,0:T(1,128)S(1)}, u32[]{:S(2)}, u32[]{:S(2)}) async-start(f32[64,1,72]{2,1,0:T(1,128)} %broadcast_in_dim.2), calls=%async_computation | async-start | bytes 65536 | tf_op jit(solution)/shard_map/all_to_all | solution.py:146
  15.6 0.9 copy-start.2
  16.6 3.9 %copy-start.4 = (bf16[256,256]{1,0:T(8,128)(2,1)S(1)}, bf16[256,256]{1,0:T(8,128)(2,1)}, u32[]{:S(2)}) copy-start(bf16[256,256]{1,0:T(8,128)(2,1)} %param.10) | copy-start | bytes 393220
  16.8 3.7 %copy-start.3 = (bf16[256,256]{1,0:T(8,128)(2,1)S(1)}, bf16[256,256]{1,0:T(8,128)(2,1)}, u32[]{:S(2)}) copy-start(bf16[256,256]{1,0:T(8,128)(2,1)} %param.7) | copy-start | bytes 393220
  16.8 28.0 %collective-permute-start.1 = (bf16[256,260]{1,0:T(8,128)(2,1)S(1)}, bf16[256,260]{1,0:T(8,128)(2,1)S(1)}, u32[]{:S(2)}, u32[]{:S(2)}) collective-permute-start(bf16[256,260]{1,0:T(8,128)(2,1)S(1)} %pad_maximum_fusion.1), channel_id=1, source_target_pairs={{0,8},{8,16},{16,24},{24,32},{32,40},{40,48},{48,56},{56,64},{64,7... | collective-permute-start | bytes 399368 | tf_op jit(solution)/shard_map/ppermute | solution.py:15
  20.5 0.8 slice-start
  20.5 0.9 slice-start.1
  21.5 23.5 %collective-permute-start = (bf16[256,262]{1,0:T(8,128)(2,1)S(1)}, bf16[256,262]{1,0:T(8,128)(2,1)S(1)}, u32[]{:S(2)}, u32[]{:S(2)}) collective-permute-start(bf16[256,262]{1,0:T(8,128)(2,1)S(1)} %pad_maximum_fusion), channel_id=1, source_target_pairs={{8,0},{16,8},{24,16},{32,24},{40,32},{48,40},{56,48},{64,56},{72,6... | collective-permute-start | bytes 402440 | tf_op jit(solution)/shard_map/ppermute | solution.py:15
  24.7 16.6 %all-to-all-start.1 = ((f32[8,1,320]{2,1,0:T(1,128)}), f32[8,1,320]{2,1,0:T(1,128)S(1)}, u32[]{:S(2)}, u32[]{:S(2)}) async-start(f32[8,1,320]{2,1,0:T(1,128)} %reshape.178), calls=%async_computation.1 | async-start | bytes 24576 | tf_op jit(solution)/shard_map/all_to_all | solution.py:158
  45.2 0.9 copy-start.1
  60.0 9.9 %all-to-all-start.2 = ((f32[8,1,320]{2,1,0:T(1,128)}), f32[8,1,320]{2,1,0:T(1,128)S(1)}, u32[]{:S(2)}, u32[]{:S(2)}) async-start(f32[8,1,320]{2,1,0:T(1,128)} %reshape.180), calls=%async_computation.2 | async-start | bytes 24576 | tf_op jit(solution)/shard_map/all_to_all | solution.py:229
  71.4 23.1 %all-to-all-start.3 = ((f32[64,1,72]{2,1,0:T(1,128)}), f32[64,1,72]{2,1,0:T(1,128)S(1)}, u32[]{:S(2)}, u32[]{:S(2)}) async-start(f32[64,1,72]{2,1,0:T(1,128)} %bitcast.20), calls=%async_computation.3 | async-start | bytes 65536 | tf_op jit(solution)/shard_map/all_to_all | solution.py:245

commit v7 on v6

--- a/solution.py
+++ b/solution.py
@@ -142,7 +142,24 @@
     group_size = channels // groups
     chunk = feature_taps.shape[2]
 
+    rim = reach_cols + 2
+    prev_rim = passed_along(
+        jnp.concatenate(
+            [outer_gate[:, block_len - 2 :], inner_gate[:, block_len - rim :], value_stream[:, block_len - rim :]],
+            axis=1,
+        ),
+        "ctx",
+        1,
+    )
+    next_rim = passed_along(
+        jnp.concatenate(
+            [grad_output[:, :rim], outer_gate[:, :rim], inner_gate[:, :2], value_stream[:, :2]], axis=1
+        ),
+        "ctx",
+        -1,
+    )
     row = jnp.concatenate([filters.reshape(-1), feature_taps.reshape(-1), skip_gain])
+    row, prev_rim, next_rim = lax.optimization_barrier((row, prev_rim, next_rim))
     gathered = lax.all_to_all(
         jnp.broadcast_to(row[None], (ctx_size, row.shape[0])), "ctx", 0, 0, tiled=True
     )
@@ -164,22 +181,6 @@
     )
     skip_all = local[:, 9 * chunk :].reshape(channels)
 
-    rim = reach_cols + 2
-    prev_rim = passed_along(
-        jnp.concatenate(
-            [outer_gate[:, block_len - 2 :], inner_gate[:, block_len - rim :], value_stream[:, block_len - rim :]],
-            axis=1,
-        ),
-        "ctx",
-        1,
-    )
-    next_rim = passed_along(
-        jnp.concatenate(
-            [grad_output[:, :rim], outer_gate[:, :rim], inner_gate[:, :2], value_stream[:, :2]], axis=1
-        ),
-        "ctx",
-        -1,
-    )
     outer_ext = jnp.concatenate([prev_rim[:, :2], outer_gate, next_rim[:, rim : 2 * rim]], axis=1)
     inner_ext = jnp.concatenate(
         [prev_rim[:, 2 : 2 + rim], inner_gate, next_rim[:, 2 * rim : 2 * rim + 2]], axis=1

time: 97.1 us -> 106 us (1.092)
  waiting for transfers between devices: 18.6 us -> 26.6 us
  starting transfers between devices: 44.4 us -> 39.9 us
  local copies, waits for them, and re-layouts: 14.8 us -> 18.8 us
    all_to_all x1, waiting for transfers between devices: 0.44 us -> 7.97 us  [shards(): lax.all_to_all(jnp.broadcast_to(row[None], (ctx_size, row.shape[0])), 'ct...]
    all_to_all x1, starting transfers between devices: 13.8 us -> 7.21 us  [shards(): reduced = jnp.sum(lax.all_to_all(send, 'ctx', 0, 0, tiled=True), axis=0)]
    ppermute x2, starting transfers between devices: 5.59 us -> 10.8 us  [passed_along(): return lax.ppermute(shard, axis, pairs)]
    unnamed x18 -> x50, local copies, waits for them, and re-layouts: 3.9 us -> 8.12 us
    all_to_all x1, starting transfers between devices: 11.6 us -> 8.43 us  [shards(): lax.all_to_all(jnp.broadcast_to(row[None], (ctx_size, row.shape[0])), 'ct...]
    ppermute x2, waiting for transfers between devices: 0.01 us -> 1.68 us  [passed_along(): return lax.ppermute(shard, axis, pairs)]
    all_to_all x1, waiting for transfers between devices: 5.6 us -> 4.37 us  [shards(): reduced = jnp.sum(lax.all_to_all(send, 'ctx', 0, 0, tiled=True), axis=0)]
  transfers between devices with their start and end apart: 6 -> 6, of which waited for: 4 -> 5; matrix products, arithmetic and copies ran while one was open for 10% -> 5% of each run, Pallas kernels for 0% -> 0%
where the time goes in v7:
time: 106 us; the launch traced here: 105 us
  starting transfers between devices  39.9 us (38%)
  waiting for transfers between devices  26.6 us (25%)
  local copies, waits for them, and re-layouts  18.8 us (18%)
  other arithmetic  11.4 us (11%)
  Pallas kernels  7.3 us (7%)
  between operations  1.2 us (1%)
    ppermute x2, starting transfers between devices, passed_along(): return lax.ppermute(shard, axis, pairs)  10.8 us
    all_to_all x1, starting transfers between devices, shards(): moved = lax.all_to_all(gathered[:, n_filt:], 'fsdp', 0, 0, tiled=True)  10 us
    all_to_all x1, starting transfers between devices, shards(): lax.all_to_all(jnp.broadcast_to(row[None], (ctx_size, row.shape[0])), 'ct...  8.43 us
    unnamed x50, local copies, waits for them, and re-layouts  8.12 us
    all_to_all x1, waiting for transfers between devices, shards(): lax.all_to_all(jnp.broadcast_to(row[None], (ctx_size, row.shape[0])), 'ct...  7.97 us
    pallas_call x1, Pallas kernels, both_convs(): pl.pallas_call(functools.partial(banded_kernel, here=here), out_shape=(ja...  7.3 us
    all_to_all x1, starting transfers between devices, shards(): reduced = jnp.sum(lax.all_to_all(send, 'ctx', 0, 0, tiled=True), axis=0)  7.21 us
    all_to_all x1, waiting for transfers between devices, shards(): by_owner = lax.all_to_all(to_fsdp, 'fsdp', 0, 0, tiled=True)  6.3 us
  transfers between devices with their start and end apart: 6, of which 5 were waited for; matrix products, arithmetic and copies ran while one was open for 5% of the time, Pallas kernels for 0%

profile of v7, /device:TPU:1, one launch (start us, length us, event | category | flops | bytes accessed | tf_op | source)
XLA Modules:
  0.0 105.2 jit_solution(7857851388867728222)
XLA Ops:
  0.7 0.9 copy-done.2
  1.6 1.0 pad_maximum_fusion.1
  2.6 8.9 %collective-permute-start.1 = (bf16[256,262]{1,0:T(8,128)(2,1)S(1)}, bf16[256,262]{1,0:T(8,128)(2,1)S(1)}, u32[]{:S(2)}, u32[]{:S(2)}) collective-permute-start(bf16[256,262]{1,0:T(8,128)(2,1)S(1)} %pad_maximum_fusion.1), channel_id=1, source_target_pairs={{8,0},{16,8},{24,16},{32,24},{40,32},{48,40},{56,48},{64,56},{72,6... | collective-permute-start | bytes 402440 | tf_op jit(solution)/shard_map/ppermute | solution.py:15
  11.8 0.8 copy-done.1
  12.7 0.2 pad_maximum_fusion
  12.9 1.9 %collective-permute-start = (bf16[256,260]{1,0:T(8,128)(2,1)S(1)}, bf16[256,260]{1,0:T(8,128)(2,1)S(1)}, u32[]{:S(2)}, u32[]{:S(2)}) collective-permute-start(bf16[256,260]{1,0:T(8,128)(2,1)S(1)} %pad_maximum_fusion), channel_id=1, source_target_pairs={{0,8},{8,16},{16,24},{24,32},{32,40},{40,48},{48,56},{56,64},{64,7... | collective-permute-start | bytes 399368 | tf_op jit(solution)/shard_map/ppermute | solution.py:15
  15.1 0.6 copy-done.21
  15.7 1.7 %collective-permute-done = bf16[256,260]{1,0:T(8,128)(2,1)S(1)} collective-permute-done((bf16[256,260]{1,0:T(8,128)(2,1)S(1)}, bf16[256,260]{1,0:T(8,128)(2,1)S(1)}, u32[]{:S(2)}, u32[]{:S(2)}) %collective-permute-start) | collective-permute-done | bytes 133152 | tf_op jit(solution)/shard_map/ppermute | solution.py:15
  17.4 0.7 fusion.38
  18.1 0.2 fusion.36
  18.3 0.6 broadcast_in_dim.2
  19.0 8.4 %all-to-all-start = ((f32[64,1,72]{2,1,0:T(1,128)}), f32[64,1,72]{2,1,0:T(1,128)S(1)}, u32[]{:S(2)}, u32[]{:S(2)}) async-start(f32[64,1,72]{2,1,0:T(1,128)} %broadcast_in_dim.2), calls=%async_computation | async-start | bytes 65536 | tf_op jit(solution)/shard_map/all_to_all | solution.py:163
  27.8 0.7 copy-done.7
  28.6 8.0 %all-to-all-done = f32[64,1,72]{2,1,0:T(1,128)S(1)} async-done(((f32[64,1,72]{2,1,0:T(1,128)}), f32[64,1,72]{2,1,0:T(1,128)S(1)}, u32[]{:S(2)}, u32[]{:S(2)}) %all-to-all-start) | async-done | bytes 18464 | tf_op jit(solution)/shard_map/all_to_all | solution.py:163
  36.8 0.7 reshape.178
  37.5 10.0 %all-to-all-start.1 = ((f32[8,1,320]{2,1,0:T(1,128)}), f32[8,1,320]{2,1,0:T(1,128)S(1)}, u32[]{:S(2)}, u32[]{:S(2)}) async-start(f32[8,1,320]{2,1,0:T(1,128)} %reshape.178), calls=%async_computation.1 | async-start | bytes 24576 | tf_op jit(solution)/shard_map/all_to_all | solution.py:175
  47.9 6.3 %all-to-all-done.1 = f32[8,1,320]{2,1,0:T(1,128)S(1)} async-done(((f32[8,1,320]{2,1,0:T(1,128)}), f32[8,1,320]{2,1,0:T(1,128)S(1)}, u32[]{:S(2)}, u32[]{:S(2)}) %all-to-all-start.1) | async-done | bytes 10272 | tf_op jit(solution)/shard_map/all_to_all | solution.py:175
  54.1 0.5 broadcast.16
  54.6 0.7 reduce.1
  55.9 0.7 mul.275
  56.7 0.7 mul.272
  58.6 0.7 mul.279
  59.3 0.9 multiply_convert_fusion.1
  60.2 0.9 slice_convert_fusion
  61.1 0.9 copy-done.5
  61.9 0.5 multiply_convert_fusion
  62.5 7.3 %shard_map.126 = (f32[16,16,272]{2,1,0:T(8,128)S(1)}, f32[16,16,272]{2,1,0:T(8,128)S(1)}, f32[16,1,128]{2,1,0:T(1,128)S(1)}) custom-call(f32[16,1,512]{2,1,0:T(1,128)S(1)} %reshape.163.ahead_ref, f32[16,1,512]{2,1,0:T(1,128)S(1)} %reshape.164.behind_ref, bf16[16,16,512]{2,1,0:T(8,128)(2,1)S(1)} %bitcast.58, bf16[16,16,512]{2,1,0:T(8,128)(2,1)S(1)} %bitcast.59), custom_call_target="tpu_custom_call" | custom-call | flops 276824064 | bytes 1081344 | tf_op jit(solution)/shard_map/pallas_call | solution.py:119
  69.8 0.7 copy-done.19
  70.4 0.4 fusion.8
  70.9 0.3 fusion.13
  71.2 0.4 fusion.16
  71.6 0.3 fusion.10
  74.4 0.7 reshape.180
  75.1 3.3 %all-to-all-start.2 = ((f32[8,1,320]{2,1,0:T(1,128)}), f32[8,1,320]{2,1,0:T(1,128)S(1)}, u32[]{:S(2)}, u32[]{:S(2)}) async-start(f32[8,1,320]{2,1,0:T(1,128)} %reshape.180), calls=%async_computation.2 | async-start | bytes 24576 | tf_op jit(solution)/shard_map/all_to_all | solution.py:230
  78.7 6.3 %all-to-all-done.2 = f32[8,1,320]{2,1,0:T(1,128)S(1)} async-done(((f32[8,1,320]{2,1,0:T(1,128)}), f32[8,1,320]{2,1,0:T(1,128)S(1)}, u32[]{:S(2)}, u32[]{:S(2)}) %all-to-all-start.2) | async-done | bytes 10272 | tf_op jit(solution)/shard_map/all_to_all | solution.py:230
  85.0 0.7 reduce.2
  85.7 0.7 pad_maximum_fusion.5
  86.4 7.2 %all-to-all-start.3 = ((f32[64,1,72]{2,1,0:T(1,128)}), f32[64,1,72]{2,1,0:T(1,128)S(1)}, u32[]{:S(2)}, u32[]{:S(2)}) async-start(f32[64,1,72]{2,1,0:T(1,128)} %bitcast.20), calls=%async_computation.3 | async-start | bytes 65536 | tf_op jit(solution)/shard_map/all_to_all | solution.py:246
  93.7 0.6 copy-done.9
  94.3 1.0 fusion.25
  95.3 0.6 copy-done.13
  96.0 1.0 fusion.22
  97.0 0.7 multiply_convert_fusion.2
  97.7 1.0 fusion.19
  98.7 4.4 %all-to-all-done.3 = f32[64,1,72]{2,1,0:T(1,128)S(1)} async-done(((f32[64,1,72]{2,1,0:T(1,128)}), f32[64,1,72]{2,1,0:T(1,128)S(1)}, u32[]{:S(2)}, u32[]{:S(2)}) %all-to-all-start.3) | async-done | bytes 18464 | tf_op jit(solution)/shard_map/all_to_all | solution.py:246
  103.1 0.6 slice.332
  103.8 0.7 reshape.175
  104.5 0.6 copy.127
  (126 shorter events, 6.6 us)
Async XLA Ops:
  0.6 0.9 copy-start.2
  0.6 0.9 slice-start
  0.7 0.9 slice-start.1
  2.6 9.0 %copy-start = (bf16[256,256]{1,0:T(8,128)(2,1)S(1)}, bf16[256,256]{1,0:T(8,128)(2,1)}, u32[]{:S(2)}) copy-start(bf16[256,256]{1,0:T(8,128)(2,1)} %param.8) | copy-start | bytes 393220
  2.6 14.8 %collective-permute-start.1 = (bf16[256,262]{1,0:T(8,128)(2,1)S(1)}, bf16[256,262]{1,0:T(8,128)(2,1)S(1)}, u32[]{:S(2)}, u32[]{:S(2)}) collective-permute-start(bf16[256,262]{1,0:T(8,128)(2,1)S(1)} %pad_maximum_fusion.1), channel_id=1, source_target_pairs={{8,0},{16,8},{24,16},{32,24},{40,32},{48,40},{56,48},{64,56},{72,6... | collective-permute-start | bytes 402440 | tf_op jit(solution)/shard_map/ppermute | solution.py:15
  11.7 0.9 copy-start.1
  12.7 2.1 %copy-start.18 = (f32[3,3,4]{2,1,0:T(4,128)S(1)}, f32[3,3,4]{2,1,0:T(4,128)}, u32[]{:S(2)}) copy-start(f32[3,3,4]{2,1,0:T(4,128)} %param.12) | copy-start | bytes 436
  12.8 2.0 %copy-start.20 = (f32[16,2]{0,1:T(2,128)S(1)}, f32[16,2]{0,1:T(2,128)}, u32[]{:S(2)}) copy-start(f32[16,2]{0,1:T(2,128)} %param.11) | copy-start | bytes 388
  12.9 4.5 %collective-permute-start = (bf16[256,260]{1,0:T(8,128)(2,1)S(1)}, bf16[256,260]{1,0:T(8,128)(2,1)S(1)}, u32[]{:S(2)}, u32[]{:S(2)}) collective-permute-start(bf16[256,260]{1,0:T(8,128)(2,1)S(1)} %pad_maximum_fusion), channel_id=1, source_target_pairs={{0,8},{8,16},{16,24},{24,32},{32,40},{40,48},{48,56},{56,64},{64,7... | collective-permute-start | bytes 399368 | tf_op jit(solution)/shard_map/ppermute | solution.py:15
  15.0 0.7 copy-start.21
  18.1 9.3 %copy-start.3 = (bf16[256,256]{1,0:T(8,128)(2,1)S(1)}, bf16[256,256]{1,0:T(8,128)(2,1)}, u32[]{:S(2)}) copy-start(bf16[256,256]{1,0:T(8,128)(2,1)} %param.10) | copy-start | bytes 393220
  18.3 9.2 %copy-start.4 = (bf16[256,129]{1,0:T(8,128)(2,1)}, bf16[256,129]{1,0:T(8,128)(2,1)S(1)}, u32[]{:S(2)}) copy-start(bf16[256,129]{1,0:T(8,128)(2,1)S(1)} %get-tuple-element.85) | copy-start | bytes 198148
  19.0 17.7 %all-to-all-start = ((f32[64,1,72]{2,1,0:T(1,128)}), f32[64,1,72]{2,1,0:T(1,128)S(1)}, u32[]{:S(2)}, u32[]{:S(2)}) async-start(f32[64,1,72]{2,1,0:T(1,128)} %broadcast_in_dim.2), calls=%async_computation | async-start | bytes 65536 | tf_op jit(solution)/shard_map/all_to_all | solution.py:163
  27.7 0.8 copy-start.7
  37.5 16.6 %all-to-all-start.1 = ((f32[8,1,320]{2,1,0:T(1,128)}), f32[8,1,320]{2,1,0:T(1,128)S(1)}, u32[]{:S(2)}, u32[]{:S(2)}) async-start(f32[8,1,320]{2,1,0:T(1,128)} %reshape.178), calls=%async_computation.1 | async-start | bytes 24576 | tf_op jit(solution)/shard_map/all_to_all | solution.py:175
  58.2 1.1 %copy-start.12 = (f32[256]{0:T(256)}, f32[256]{0:T(256)S(1)}, u32[]{:S(2)}) copy-start(f32[256]{0:T(256)S(1)} %mul.256) | copy-start | bytes 3076
  58.4 0.9 copy-start.14
  58.6 0.7 copy-start.16
  61.0 0.9 copy-start.5
  61.0 0.9 copy-start.8
  61.0 0.9 copy-start.10
  69.8 0.7 copy-start.19
  72.1 1.8 %copy-start.6 = (f32[256,258]{1,0:T(8,128)S(1)}, f32[256,258]{1,0:T(8,128)}, u32[]{:S(2)}) copy-start(f32[256,258]{1,0:T(8,128)} %slice_convert_fusion) | copy-start | bytes 792580
  75.1 9.9 %all-to-all-start.2 = ((f32[8,1,320]{2,1,0:T(1,128)}), f32[8,1,320]{2,1,0:T(1,128)S(1)}, u32[]{:S(2)}, u32[]{:S(2)}) async-start(f32[8,1,320]{2,1,0:T(1,128)} %reshape.180), calls=%async_computation.2 | async-start | bytes 24576 | tf_op jit(solution)/shard_map/all_to_all | solution.py:230
  86.4 16.6 %all-to-all-start.3 = ((f32[64,1,72]{2,1,0:T(1,128)}), f32[64,1,72]{2,1,0:T(1,128)S(1)}, u32[]{:S(2)}, u32[]{:S(2)}) async-start(f32[64,1,72]{2,1,0:T(1,128)} %bitcast.20), calls=%async_computation.3 | async-start | bytes 65536 | tf_op jit(solution)/shard_map/all_to_all | solution.py:246
  93.6 0.7 copy-start.9
  93.6 0.7 copy-start.11
  95.3 0.7 copy-start.13
  95.3 0.7 copy-start.15
  95.3 0.7 copy-start.17

commit v8 on v6

--- a/solution.py
+++ b/solution.py
@@ -142,12 +142,14 @@
     group_size = channels // groups
     chunk = feature_taps.shape[2]
 
-    row = jnp.concatenate([filters.reshape(-1), feature_taps.reshape(-1), skip_gain])
+    pack = jnp.concatenate([feature_taps.reshape(-1), skip_gain])
+    n_chunk = pack.shape[0]
+    ring = lax.all_to_all(jnp.broadcast_to(pack[None], (fsdp_size, n_chunk)), "fsdp", 0, 0, tiled=True)
+    row = jnp.concatenate([filters.reshape(-1), ring.reshape(-1)])
     gathered = lax.all_to_all(
         jnp.broadcast_to(row[None], (ctx_size, row.shape[0])), "ctx", 0, 0, tiled=True
     )
     n_filt = groups * taps_here
-    n_chunk = row.shape[0] - n_filt
     per_block = ctx_size // fsdp_size
     filters_all = (
         gathered[:, :n_filt]
@@ -155,10 +157,9 @@
         .transpose(1, 0, 2)
         .reshape(groups, taps_count)
     )
-    moved = lax.all_to_all(gathered[:, n_filt:], "fsdp", 0, 0, tiled=True)
-    local = (
-        moved.reshape(fsdp_size, per_block, n_chunk).transpose(1, 0, 2).reshape(ctx_size, n_chunk)
-    )
+    local = lax.dynamic_slice_in_dim(
+        gathered[:, n_filt:], lax.axis_index("fsdp") * per_block, per_block, 0
+    ).reshape(ctx_size, n_chunk)
     taps_all = (
         local[:, : 9 * chunk].reshape(ctx_size, 3, 3, chunk).transpose(1, 2, 0, 3).reshape(3, 3, channels)
     )

time: 97.1 us -> 109 us (1.12)
  local copies, waits for them, and re-layouts: 14.8 us -> 27.9 us
  starting transfers between devices: 44.4 us -> 41.7 us
  other arithmetic: 10.4 us -> 12.8 us
  waiting for transfers between devices: 18.6 us -> 17.4 us
    all_to_all x1, starting transfers between devices: 13.8 us -> 5.79 us  [shards(): reduced = jnp.sum(lax.all_to_all(send, 'ctx', 0, 0, tiled=True), axis=0)]
    all_to_all x1, waiting for transfers between devices: 0.44 us -> 7.84 us  [shards(): lax.all_to_all(jnp.broadcast_to(row[None], (ctx_size, row.shape[0])), 'ct...]
    all_to_all x1, waiting for transfers between devices: 6.27 us -> 0.01 us  [shards(): lax.all_to_all(jnp.broadcast_to(pack[None], (fsdp_size, n_chunk)), 'fsdp'...]
    unnamed x18 -> x82, local copies, waits for them, and re-layouts: 3.9 us -> 9.9 us
    all_to_all x1, starting transfers between devices: 3.34 us -> 6.92 us  [shards(): by_owner = lax.all_to_all(to_fsdp, 'fsdp', 0, 0, tiled=True)]
    all_to_all x1, waiting for transfers between devices: 5.6 us -> 3.31 us  [shards(): reduced = jnp.sum(lax.all_to_all(send, 'ctx', 0, 0, tiled=True), axis=0)]
    mul x3, local copies, waits for them, and re-layouts: 0.32 us -> 1.5 us  [featurize(): result = tap_gains[0][:, None] * extended[:, 2:]]
    mul x3, local copies, waits for them, and re-layouts: 0.32 us -> 1.49 us  [featurize(): result = result + tap_gains[1][:, None] * extended[:, 1:out_len + 1]]
  transfers between devices with their start and end apart: 6 -> 6, of which waited for: 4 -> 3; matrix products, arithmetic and copies ran while one was open for 10% -> 8% of each run, Pallas kernels for 0% -> 0%
where the time goes in v8:
time: 109 us; the launch traced here: 108 us
  starting transfers between devices  41.7 us (38%)
  local copies, waits for them, and re-layouts  27.9 us (26%)
  waiting for transfers between devices  17.4 us (16%)
  other arithmetic  12.8 us (12%)
  Pallas kernels  7.3 us (7%)
  between operations  1.34 us (1%)
    all_to_all x1, starting transfers between devices, shards(): lax.all_to_all(jnp.broadcast_to(row[None], (ctx_size, row.shape[0])), 'ct...  12 us
    all_to_all x1, starting transfers between devices, shards(): lax.all_to_all(jnp.broadcast_to(pack[None], (fsdp_size, n_chunk)), 'fsdp'...  10.9 us
    unnamed x82, local copies, waits for them, and re-layouts  9.9 us
    all_to_all x1, waiting for transfers between devices, shards(): lax.all_to_all(jnp.broadcast_to(row[None], (ctx_size, row.shape[0])), 'ct...  7.84 us
    pallas_call x1, Pallas kernels, both_convs(): pl.pallas_call(functools.partial(banded_kernel, here=here), out_shape=(ja...  7.3 us
    all_to_all x1, starting transfers between devices, shards(): by_owner = lax.all_to_all(to_fsdp, 'fsdp', 0, 0, tiled=True)  6.92 us
    all_to_all x1, waiting for transfers between devices, shards(): by_owner = lax.all_to_all(to_fsdp, 'fsdp', 0, 0, tiled=True)  6.26 us
    ppermute x2, starting transfers between devices, passed_along(): return lax.ppermute(shard, axis, pairs)  6.1 us
  transfers between devices with their start and end apart: 6, of which 3 were waited for; matrix products, arithmetic and copies ran while one was open for 8% of the time, Pallas kernels for 0%

profile of v8, /device:TPU:1, one launch (start us, length us, event | category | flops | bytes accessed | tf_op | source)
XLA Modules:
  0.0 108.5 jit_solution(10126034853104985949)
XLA Ops:
  0.6 0.8 reshape.168
  1.5 0.6 broadcast_in_dim.4
  2.1 10.9 %all-to-all-start = ((f32[8,1,40]{2,1,0:T(1,128)}), f32[8,1,40]{2,1,0:T(1,128)S(1)}, u32[]{:S(2)}, u32[]{:S(2)}) async-start(f32[8,1,40]{2,1,0:T(1,128)} %broadcast_in_dim.4), calls=%async_computation | async-start | bytes 8192 | tf_op jit(solution)/shard_map/all_to_all | solution.py:147
  13.0 1.0 slice.276
  14.2 0.8 copy-done
  15.2 4.2 %collective-permute-start.1 = (bf16[256,260]{1,0:T(8,128)(2,1)S(1)}, bf16[256,260]{1,0:T(8,128)(2,1)S(1)}, u32[]{:S(2)}, u32[]{:S(2)}) collective-permute-start(bf16[256,260]{1,0:T(8,128)(2,1)S(1)} %pad_maximum_fusion.1), channel_id=1, source_target_pairs={{0,8},{8,16},{16,24},{24,32},{32,40},{40,48},{48,56},{56,64},{64,7... | collective-permute-start | bytes 399368 | tf_op jit(solution)/shard_map/ppermute | solution.py:15
  19.4 0.8 slice-done
  20.4 1.9 %collective-permute-start = (bf16[256,262]{1,0:T(8,128)(2,1)S(1)}, bf16[256,262]{1,0:T(8,128)(2,1)S(1)}, u32[]{:S(2)}, u32[]{:S(2)}) collective-permute-start(bf16[256,262]{1,0:T(8,128)(2,1)S(1)} %pad_maximum_fusion), channel_id=1, source_target_pairs={{8,0},{16,8},{24,16},{32,24},{40,32},{48,40},{56,48},{64,56},{72,6... | collective-permute-start | bytes 402440 | tf_op jit(solution)/shard_map/ppermute | solution.py:15
  22.4 0.7 copy-done.37
  23.7 0.7 reduce.4
  24.5 0.7 broadcast_in_dim.5
  25.2 12.0 %all-to-all-start.1 = ((f32[64,1,352]{2,1,0:T(1,128)}), f32[64,1,352]{2,1,0:T(1,128)}, u32[]{:S(2)}, u32[]{:S(2)}) async-start(f32[64,1,352]{2,1,0:T(1,128)} %broadcast_in_dim.5), calls=%async_computation.1 | async-start | bytes 196608 | tf_op jit(solution)/shard_map/all_to_all | solution.py:149
  37.7 0.6 copy-done.7
  38.6 0.7 copy-done.1
  39.6 7.8 %all-to-all-done.1 = f32[64,1,352]{2,1,0:T(1,128)} async-done(((f32[64,1,352]{2,1,0:T(1,128)}), f32[64,1,352]{2,1,0:T(1,128)}, u32[]{:S(2)}, u32[]{:S(2)}) %all-to-all-start.1) | async-done | bytes 90144 | tf_op jit(solution)/shard_map/all_to_all | solution.py:149
  47.4 1.0 copy.72
  48.7 0.7 slice.363
  49.6 0.6 fusion.39
  50.3 0.7 mul.254
  51.0 0.7 mul.257
  51.8 0.7 mul.260
  52.6 0.7 mul.263
  53.4 0.7 mul.266
  54.2 0.7 mul.269
  54.9 0.7 copy-done.23
  55.6 1.6 %multiply_convert_fusion.1 = (bf16[256,385]{1,0:T(8,128)(2,1)S(1)}, f32[256,385]{1,0:T(8,128)S(1)}, f32[256,385]{1,0:T(8,128)S(1)}) fusion(f32[256,387]{1,0:T(8,128)S(1)} %get-tuple-element.89, f32[256]{0:T(256)} %mul.269, f32[256]{0:T(256)S(1)} %copy-done.25, f32[256]{0:T(256)S(1)} %copy-done.23, f32[256,387]{1,0:T(8,128)S(1)} %get-tuple-element.88, ...), kind=kLoop, calls=%fused_computation.16 | loop fusion | flops 1182720 | bytes 3357184 | tf_op jit(solution)/shard_map/convert_element_type | solution.py:194
  57.2 0.9 slice_convert_fusion
  58.1 0.6 copy-done.36
  59.9 1.3 %multiply_convert_fusion = (bf16[256,385]{1,0:T(8,128)(2,1)S(1)}, f32[256,385]{1,0:T(8,128)}) fusion(bf16[256,129]{1,0:T(8,128)(2,1)S(1)} %copy-done.8, bf16[256,256]{1,0:T(8,128)(2,1)S(1)} %copy-done.6, f32[256,387]{1,0:T(8,128)S(1)} %maximum_convert_fusion.3, f32[256]{0:T(256)S(1)} %mul.279, f32[256]{0:T(256)S(1)} %mul.276, f32[256]{0:T(256)S(1)} %mul.273), kind=kLoop, calls=%fused_computation.15 | loop fusion | flops 1084160 | bytes 1974272 | tf_op jit(solution)/shard_map/convert_element_type | solution.py:199
  61.5 0.7 copy-done.18
  62.4 7.3 %shard_map.126 = (f32[16,16,272]{2,1,0:T(8,128)S(1)}, f32[16,16,272]{2,1,0:T(8,128)S(1)}, f32[16,1,128]{2,1,0:T(1,128)S(1)}) custom-call(f32[16,1,512]{2,1,0:T(1,128)S(1)} %reshape.170.ahead_ref, f32[16,1,512]{2,1,0:T(1,128)S(1)} %reshape.171.behind_ref, bf16[16,16,512]{2,1,0:T(8,128)(2,1)S(1)} %bitcast.53, bf16[16,16,512]{2,1,0:T(8,128)(2,1)S(1)} %bitcast.54), custom_call_target="tpu_custom_call" | custom-call | flops 276824064 | bytes 1081344 | tf_op jit(solution)/shard_map/pallas_call | solution.py:119
  69.7 1.1 %fusion.8 = (bf16[256,258]{1,0:T(8,128)(2,1)S(1)}, f32[256,258]{1,0:T(8,128)}, bf16[256,258]{1,0:T(8,128)(2,1)S(1)}, bf16[256,258]{1,0:T(8,128)(2,1)S(1)}) fusion(f32[256,385]{1,0:T(8,128)S(1)} %maximum_convert_fusion, bf16[256,385]{1,0:T(8,128)(2,1)S(1)} %get-tuple-element.66, f32[256]{0:T(256)S(1)} %mul.283, f32[256,272]{1,0:T(8,128)S(1)} %bitcast.51, ...), kind=kLoop, calls=%fused_computation.24 | loop fusion | flops 792576 | bytes 2246656 | tf_op jit(solution)/shard_map/convert_element_type | solution.py:203
  74.9 0.7 reshape.194
  75.6 6.9 %all-to-all-start.2 = ((f32[8,1,320]{2,1,0:T(1,128)}), f32[8,1,320]{2,1,0:T(1,128)S(1)}, u32[]{:S(2)}, u32[]{:S(2)}) async-start(f32[8,1,320]{2,1,0:T(1,128)} %reshape.194), calls=%async_computation.2 | async-start | bytes 24576 | tf_op jit(solution)/shard_map/all_to_all | solution.py:230
  82.9 6.3 %all-to-all-done.2 = f32[8,1,320]{2,1,0:T(1,128)S(1)} async-done(((f32[8,1,320]{2,1,0:T(1,128)}), f32[8,1,320]{2,1,0:T(1,128)S(1)}, u32[]{:S(2)}, u32[]{:S(2)}) %all-to-all-start.2) | async-done | bytes 10272 | tf_op jit(solution)/shard_map/all_to_all | solution.py:230
  89.7 0.7 reduce.5
  90.4 0.7 pad_maximum_fusion.5
  91.1 5.8 %all-to-all-start.3 = ((f32[64,1,72]{2,1,0:T(1,128)}), f32[64,1,72]{2,1,0:T(1,128)S(1)}, u32[]{:S(2)}, u32[]{:S(2)}) async-start(f32[64,1,72]{2,1,0:T(1,128)} %bitcast.17), calls=%async_computation.3 | async-start | bytes 65536 | tf_op jit(solution)/shard_map/all_to_all | solution.py:246
  97.0 0.6 copy-done.24
  97.6 1.0 fusion.19
  98.6 0.6 copy-done.20
  99.3 1.0 fusion.22
  100.3 1.0 copy-done.9
  101.3 0.7 multiply_convert_fusion.2
  102.0 1.0 fusion.25
  103.0 3.3 %all-to-all-done.3 = f32[64,1,72]{2,1,0:T(1,128)S(1)} async-done(((f32[64,1,72]{2,1,0:T(1,128)}), f32[64,1,72]{2,1,0:T(1,128)S(1)}, u32[]{:S(2)}, u32[]{:S(2)}) %all-to-all-start.3) | async-done | bytes 18464 | tf_op jit(solution)/shard_map/all_to_all | solution.py:246
  107.1 0.6 copy.102
  107.8 0.7 reshape.182
  (163 shorter events, 10.7 us)
Async XLA Ops:
  0.6 0.8 copy-start.38
  2.1 21.1 %all-to-all-start = ((f32[8,1,40]{2,1,0:T(1,128)}), f32[8,1,40]{2,1,0:T(1,128)S(1)}, u32[]{:S(2)}, u32[]{:S(2)}) async-start(f32[8,1,40]{2,1,0:T(1,128)} %broadcast_in_dim.4), calls=%async_computation | async-start | bytes 8192 | tf_op jit(solution)/shard_map/all_to_all | solution.py:147
  13.0 1.1 copy-start.3
  14.0 0.9 copy-start
  15.2 4.2 %copy-start.5 = (bf16[256,256]{1,0:T(8,128)(2,1)S(1)}, bf16[256,256]{1,0:T(8,128)(2,1)}, u32[]{:S(2)}) copy-start(bf16[256,256]{1,0:T(8,128)(2,1)} %param.10) | copy-start | bytes 393220
  15.2 22.1 %collective-permute-start.1 = (bf16[256,260]{1,0:T(8,128)(2,1)S(1)}, bf16[256,260]{1,0:T(8,128)(2,1)S(1)}, u32[]{:S(2)}, u32[]{:S(2)}) collective-permute-start(bf16[256,260]{1,0:T(8,128)(2,1)S(1)} %pad_maximum_fusion.1), channel_id=1, source_target_pairs={{0,8},{8,16},{16,24},{24,32},{32,40},{40,48},{48,56},{56,64},{64,7... | collective-permute-start | bytes 399368 | tf_op jit(solution)/shard_map/ppermute | solution.py:15
  19.4 0.8 slice-start
  19.4 0.9 slice-start.1
  20.4 17.1 %collective-permute-start = (bf16[256,262]{1,0:T(8,128)(2,1)S(1)}, bf16[256,262]{1,0:T(8,128)(2,1)S(1)}, u32[]{:S(2)}, u32[]{:S(2)}) collective-permute-start(bf16[256,262]{1,0:T(8,128)(2,1)S(1)} %pad_maximum_fusion), channel_id=1, source_target_pairs={{8,0},{16,8},{24,16},{32,24},{40,32},{48,40},{56,48},{64,56},{72,6... | collective-permute-start | bytes 402440 | tf_op jit(solution)/shard_map/ppermute | solution.py:15
  22.3 0.7 copy-start.37
  25.2 22.2 %all-to-all-start.1 = ((f32[64,1,352]{2,1,0:T(1,128)}), f32[64,1,352]{2,1,0:T(1,128)}, u32[]{:S(2)}, u32[]{:S(2)}) async-start(f32[64,1,352]{2,1,0:T(1,128)} %broadcast_in_dim.5), calls=%async_computation.1 | async-start | bytes 196608 | tf_op jit(solution)/shard_map/all_to_all | solution.py:149
  37.3 1.1 copy-start.16
  37.5 1.1 %copy-start.10 = (bf16[256,129]{1,0:T(8,128)(2,1)}, bf16[256,129]{1,0:T(8,128)(2,1)S(1)}, u32[]{:S(2)}) copy-start(bf16[256,129]{1,0:T(8,128)(2,1)S(1)} %get-tuple-element.74) | copy-start | bytes 198148
  37.5 1.1 %copy-start.12 = (bf16[256,129]{1,0:T(8,128)(2,1)}, bf16[256,129]{1,0:T(8,128)(2,1)S(1)}, u32[]{:S(2)}) copy-start(bf16[256,129]{1,0:T(8,128)(2,1)S(1)} %get-tuple-element.73) | copy-start | bytes 198148
  37.6 0.7 copy-start.7
  38.4 0.9 copy-start.1
  54.9 0.7 copy-start.23
  54.9 0.7 copy-start.25
  54.9 0.7 copy-start.19
  58.1 0.7 copy-start.36
  58.1 0.9 copy-start.35
  58.1 1.8 %copy-start.8 = (bf16[256,129]{1,0:T(8,128)(2,1)S(1)}, bf16[256,129]{1,0:T(8,128)(2,1)}, u32[]{:S(2)}) copy-start(bf16[256,129]{1,0:T(8,128)(2,1)} %copy-done.7) | copy-start | bytes 198148
  58.1 1.8 %copy-start.6 = (bf16[256,256]{1,0:T(8,128)(2,1)S(1)}, bf16[256,256]{1,0:T(8,128)(2,1)}, u32[]{:S(2)}) copy-start(bf16[256,256]{1,0:T(8,128)(2,1)} %param.10) | copy-start | bytes 393220
  59.0 0.9 copy-start.27
  59.0 0.7 copy-start.34
  59.2 0.7 copy-start.30
  59.9 1.3 %copy-start.32 = (f32[256]{0:T(256)}, f32[256]{0:T(256)S(1)}, u32[]{:S(2)}) copy-start(f32[256]{0:T(256)S(1)} %mul.279) | copy-start | bytes 3076
  61.5 0.8 copy-start.18
  69.7 1.1 %copy-start.17 = (bf16[256,2]{1,0:T(8,128)(2,1)S(1)}, bf16[256,2]{1,0:T(8,128)(2,1)}, u32[]{:S(2)}) copy-start(bf16[256,2]{1,0:T(8,128)(2,1)} %copy-done.16) | copy-start | bytes 3076
  70.8 0.9 copy-start.13
  71.2 0.9 copy-start.2
  72.1 0.9 copy-start.11
  72.4 0.9 copy-start.4
  73.4 1.1 copy-start.15
  75.6 13.5 %all-to-all-start.2 = ((f32[8,1,320]{2,1,0:T(1,128)}), f32[8,1,320]{2,1,0:T(1,128)S(1)}, u32[]{:S(2)}, u32[]{:S(2)}) async-start(f32[8,1,320]{2,1,0:T(1,128)} %reshape.194), calls=%async_computation.2 | async-start | bytes 24576 | tf_op jit(solution)/shard_map/all_to_all | solution.py:230
  91.1 15.2 %all-to-all-start.3 = ((f32[64,1,72]{2,1,0:T(1,128)}), f32[64,1,72]{2,1,0:T(1,128)S(1)}, u32[]{:S(2)}, u32[]{:S(2)}) async-start(f32[64,1,72]{2,1,0:T(1,128)} %bitcast.17), calls=%async_computation.3 | async-start | bytes 65536 | tf_op jit(solution)/shard_map/all_to_all | solution.py:246
  96.9 0.7 copy-start.24
  96.9 0.7 copy-start.26
  96.9 0.7 copy-start.29
  98.6 0.7 copy-start.20
  98.6 0.7 copy-start.21
  98.6 0.7 copy-start.22
  99.3 1.0 copy-start.14
  100.3 1.0 copy-start.9
  101.3 0.7 copy-start.28
  101.3 0.7 copy-start.31
  101.3 0.7 copy-start.33

commit v9 on v6

--- a/solution.py
+++ b/solution.py
@@ -226,12 +226,15 @@
         axis=1,
     )
     to_fsdp = chunk_parts.reshape(per_block, fsdp_size, n_chunk).transpose(1, 0, 2).reshape(ctx_size, n_chunk)
+    to_fsdp, outer_feat, mixed, grad_outer_feat = lax.optimization_barrier(
+        (to_fsdp, outer_feat, mixed, grad_outer_feat)
+    )
     by_owner = lax.all_to_all(to_fsdp, "fsdp", 0, 0, tiled=True)
-    by_owner, outer_feat, mixed, grad_outer_feat, grad_inner_feat, grad_value_feat = lax.optimization_barrier(
-        (by_owner, outer_feat, mixed, grad_outer_feat, grad_inner_feat, grad_value_feat)
-    )
     gated_out = (outer_feat[:, :block_len] * mixed[:, :block_len]).astype(jnp.bfloat16)
     grad_outer = carry_back(grad_outer_feat.astype(jnp.float32), taps_all[0])
+    by_owner, grad_inner_feat, grad_value_feat = lax.optimization_barrier(
+        (by_owner, grad_inner_feat, grad_value_feat)
+    )
     grad_inner = carry_back(grad_inner_feat.astype(jnp.float32), taps_all[1])
     grad_value = carry_back(grad_value_feat.astype(jnp.float32), taps_all[2])
 

time: 97.1 us -> 97.1 us (level)
    all_to_all x1, waiting for transfers between devices: 6.3 us -> 4.61 us  [shards(): by_owner = lax.all_to_all(to_fsdp, 'fsdp', 0, 0, tiled=True)]
    all_to_all x1, waiting for transfers between devices: 5.6 us -> 7.28 us  [shards(): reduced = jnp.sum(lax.all_to_all(send, 'ctx', 0, 0, tiled=True), axis=0)]
where the time goes in v9:
time: 97.1 us; the launch traced here: 96.6 us
  starting transfers between devices  44.4 us (46%)
  waiting for transfers between devices  18.6 us (19%)
  local copies, waits for them, and re-layouts  14.7 us (15%)
  other arithmetic  10.5 us (11%)
  Pallas kernels  7.3 us (8%)
  between operations  1.15 us (1%)
    all_to_all x1, starting transfers between devices, shards(): reduced = jnp.sum(lax.all_to_all(send, 'ctx', 0, 0, tiled=True), axis=0)  13.8 us
    all_to_all x1, starting transfers between devices, shards(): lax.all_to_all(jnp.broadcast_to(row[None], (ctx_size, row.shape[0])), 'ct...  11.6 us
    all_to_all x1, starting transfers between devices, shards(): moved = lax.all_to_all(gathered[:, n_filt:], 'fsdp', 0, 0, tiled=True)  10 us
    pallas_call x1, Pallas kernels, both_convs(): pl.pallas_call(functools.partial(banded_kernel, here=here), out_shape=(ja...  7.3 us
    all_to_all x1, waiting for transfers between devices, shards(): reduced = jnp.sum(lax.all_to_all(send, 'ctx', 0, 0, tiled=True), axis=0)  7.28 us
    all_to_all x1, waiting for transfers between devices, shards(): moved = lax.all_to_all(gathered[:, n_filt:], 'fsdp', 0, 0, tiled=True)  6.27 us
    ppermute x2, starting transfers between devices, passed_along(): return lax.ppermute(shard, axis, pairs)  5.59 us
    all_to_all x1, waiting for transfers between devices, shards(): by_owner = lax.all_to_all(to_fsdp, 'fsdp', 0, 0, tiled=True)  4.61 us
  transfers between devices with their start and end apart: 6, of which 4 were waited for; matrix products, arithmetic and copies ran while one was open for 10% of the time, Pallas kernels for 0%

profile of v9, /device:TPU:1, one launch (start us, length us, event | category | flops | bytes accessed | tf_op | source)
XLA Modules:
  0.0 96.6 jit_solution(3233366212287894651)
XLA Ops:
  0.7 0.8 reshape.163
  1.6 0.7 pad_maximum_fusion.6
  2.4 0.6 broadcast_in_dim.2
  3.0 11.6 %all-to-all-start = ((f32[64,1,72]{2,1,0:T(1,128)}), f32[64,1,72]{2,1,0:T(1,128)S(1)}, u32[]{:S(2)}, u32[]{:S(2)}) async-start(f32[64,1,72]{2,1,0:T(1,128)} %broadcast_in_dim.2), calls=%async_computation | async-start | bytes 65536 | tf_op jit(solution)/shard_map/all_to_all | solution.py:146
  14.6 0.9 slice.275
  15.7 0.8 copy-done.2
  16.6 0.2 pad_maximum_fusion.1
  16.8 3.7 %collective-permute-start.1 = (bf16[256,260]{1,0:T(8,128)(2,1)S(1)}, bf16[256,260]{1,0:T(8,128)(2,1)S(1)}, u32[]{:S(2)}, u32[]{:S(2)}) collective-permute-start(bf16[256,260]{1,0:T(8,128)(2,1)S(1)} %pad_maximum_fusion.1), channel_id=1, source_target_pairs={{0,8},{8,16},{16,24},{24,32},{32,40},{40,48},{48,56},{56,64},{64,7... | collective-permute-start | bytes 399368 | tf_op jit(solution)/shard_map/ppermute | solution.py:15
  20.5 0.8 slice-done
  21.3 0.1 pad_maximum_fusion
  21.5 1.9 %collective-permute-start = (bf16[256,262]{1,0:T(8,128)(2,1)S(1)}, bf16[256,262]{1,0:T(8,128)(2,1)S(1)}, u32[]{:S(2)}, u32[]{:S(2)}) collective-permute-start(bf16[256,262]{1,0:T(8,128)(2,1)S(1)} %pad_maximum_fusion), channel_id=1, source_target_pairs={{8,0},{16,8},{24,16},{32,24},{40,32},{48,40},{56,48},{64,56},{72,6... | collective-permute-start | bytes 402440 | tf_op jit(solution)/shard_map/ppermute | solution.py:15
  23.4 0.4 all-to-all-done
  24.0 0.7 reshape.180
  24.7 10.0 %all-to-all-start.1 = ((f32[8,1,320]{2,1,0:T(1,128)}), f32[8,1,320]{2,1,0:T(1,128)S(1)}, u32[]{:S(2)}, u32[]{:S(2)}) async-start(f32[8,1,320]{2,1,0:T(1,128)} %reshape.180), calls=%async_computation.1 | async-start | bytes 24576 | tf_op jit(solution)/shard_map/all_to_all | solution.py:158
  35.1 6.3 %all-to-all-done.1 = f32[8,1,320]{2,1,0:T(1,128)S(1)} async-done(((f32[8,1,320]{2,1,0:T(1,128)}), f32[8,1,320]{2,1,0:T(1,128)S(1)}, u32[]{:S(2)}, u32[]{:S(2)}) %all-to-all-start.1) | async-done | bytes 10272 | tf_op jit(solution)/shard_map/all_to_all | solution.py:158
  41.4 0.5 broadcast.16
  41.9 0.7 reduce.1
  44.8 0.1 fusion.37
  45.3 0.8 copy-done.1
  46.1 0.3 maximum_convert_fusion.1
  46.4 0.9 multiply_convert_fusion.1
  47.3 0.1 slice_convert_fusion
  47.4 0.2 maximum_convert_fusion.3
  47.6 0.5 multiply_convert_fusion
  48.1 7.3 %shard_map.126 = (f32[16,16,272]{2,1,0:T(8,128)S(1)}, f32[16,16,272]{2,1,0:T(8,128)S(1)}, f32[16,1,128]{2,1,0:T(1,128)S(1)}) custom-call(f32[16,1,512]{2,1,0:T(1,128)S(1)} %reshape.164.ahead_ref, f32[16,1,512]{2,1,0:T(1,128)S(1)} %reshape.165.behind_ref, bf16[16,16,512]{2,1,0:T(8,128)(2,1)S(1)} %bitcast.60, bf16[16,16,512]{2,1,0:T(8,128)(2,1)S(1)} %bitcast.61), custom_call_target="tpu_custom_call" | custom-call | flops 276824064 | bytes 1081344 | tf_op jit(solution)/shard_map/pallas_call | solution.py:119
  55.4 0.4 fusion.8
  55.8 0.4 fusion.13
  56.2 0.4 fusion.16
  56.5 0.3 fusion.10
  57.1 0.1 stack.51
  58.3 0.1 stack.44
  58.5 0.1 stack.42
  58.8 0.1 copy.88
  58.9 0.1 fusion.27
  59.3 0.7 reshape.182
  60.0 3.3 %all-to-all-start.2 = ((f32[8,1,320]{2,1,0:T(1,128)}), f32[8,1,320]{2,1,0:T(1,128)S(1)}, u32[]{:S(2)}, u32[]{:S(2)}) async-start(f32[8,1,320]{2,1,0:T(1,128)} %reshape.182), calls=%async_computation.2 | async-start | bytes 24576 | tf_op jit(solution)/shard_map/all_to_all | solution.py:232
  63.4 1.0 %fusion.25 = bf16[256,256]{1,0:T(8,128)(2,1)} fusion(f32[256,258]{1,0:T(8,128)S(1)} %convert_element_type.144, f32[256]{0:T(256)S(1)} %mul.275, f32[256]{0:T(256)S(1)} %mul.272, f32[256]{0:T(256)S(1)} %mul.269), kind=kLoop, calls=%fused_computation.57 | loop fusion | flops 393216 | bytes 920576 | tf_op jit(solution)/shard_map/convert_element_type | solution.py:254
  64.3 0.7 multiply_convert_fusion.2
  65.3 4.6 %all-to-all-done.2 = f32[8,1,320]{2,1,0:T(1,128)S(1)} async-done(((f32[8,1,320]{2,1,0:T(1,128)}), f32[8,1,320]{2,1,0:T(1,128)S(1)}, u32[]{:S(2)}, u32[]{:S(2)}) %all-to-all-start.2) | async-done | bytes 10272 | tf_op jit(solution)/shard_map/all_to_all | solution.py:232
  69.9 0.7 reduce.2
  70.7 0.7 pad_maximum_fusion.5
  71.3 13.8 %all-to-all-start.3 = ((f32[64,1,72]{2,1,0:T(1,128)}), f32[64,1,72]{2,1,0:T(1,128)S(1)}, u32[]{:S(2)}, u32[]{:S(2)}) async-start(f32[64,1,72]{2,1,0:T(1,128)} %bitcast.21), calls=%async_computation.3 | async-start | bytes 65536 | tf_op jit(solution)/shard_map/all_to_all | solution.py:248
  85.2 1.0 %fusion.22 = bf16[256,256]{1,0:T(8,128)(2,1)} fusion(f32[256,258]{1,0:T(8,128)S(1)} %convert_element_type.146, f32[256]{0:T(256)S(1)} %mul.256, f32[256]{0:T(256)S(1)} %mul.253, f32[256]{0:T(256)S(1)} %mul.250), kind=kLoop, calls=%fused_computation.51 | loop fusion | flops 393216 | bytes 920576 | tf_op jit(solution)/shard_map/convert_element_type | solution.py:255
  86.2 1.0 %fusion.19 = bf16[256,256]{1,0:T(8,128)(2,1)} fusion(f32[256,258]{1,0:T(8,128)S(1)} %convert_element_type.148, f32[256]{0:T(256)S(1)} %mul.265, f32[256]{0:T(256)S(1)} %mul.262, f32[256]{0:T(256)S(1)} %mul.259), kind=kLoop, calls=%fused_computation.45 | loop fusion | flops 393216 | bytes 920576 | tf_op jit(solution)/shard_map/convert_element_type | solution.py:256
  87.1 7.3 %all-to-all-done.3 = f32[64,1,72]{2,1,0:T(1,128)S(1)} async-done(((f32[64,1,72]{2,1,0:T(1,128)}), f32[64,1,72]{2,1,0:T(1,128)S(1)}, u32[]{:S(2)}, u32[]{:S(2)}) %all-to-all-start.3) | async-done | bytes 18464 | tf_op jit(solution)/shard_map/all_to_all | solution.py:248
  94.5 0.6 slice.332
  95.2 0.7 reshape.177
  95.9 0.6 copy.93
  (94 shorter events, 5.8 us)
Async XLA Ops:
  0.6 0.8 copy-start.5
  0.6 14.9 %copy-start = (bf16[256,256]{1,0:T(8,128)(2,1)S(1)}, bf16[256,256]{1,0:T(8,128)(2,1)}, u32[]{:S(2)}) copy-start(bf16[256,256]{1,0:T(8,128)(2,1)} %param.8) | copy-start | bytes 393220
  3.0 20.8 %all-to-all-start = ((f32[64,1,72]{2,1,0:T(1,128)}), f32[64,1,72]{2,1,0:T(1,128)S(1)}, u32[]{:S(2)}, u32[]{:S(2)}) async-start(f32[64,1,72]{2,1,0:T(1,128)} %broadcast_in_dim.2), calls=%async_computation | async-start | bytes 65536 | tf_op jit(solution)/shard_map/all_to_all | solution.py:146
  15.6 0.9 copy-start.2
  16.6 3.9 %copy-start.4 = (bf16[256,256]{1,0:T(8,128)(2,1)S(1)}, bf16[256,256]{1,0:T(8,128)(2,1)}, u32[]{:S(2)}) copy-start(bf16[256,256]{1,0:T(8,128)(2,1)} %param.10) | copy-start | bytes 393220
  16.8 3.7 %copy-start.3 = (bf16[256,256]{1,0:T(8,128)(2,1)S(1)}, bf16[256,256]{1,0:T(8,128)(2,1)}, u32[]{:S(2)}) copy-start(bf16[256,256]{1,0:T(8,128)(2,1)} %param.7) | copy-start | bytes 393220
  16.8 28.0 %collective-permute-start.1 = (bf16[256,260]{1,0:T(8,128)(2,1)S(1)}, bf16[256,260]{1,0:T(8,128)(2,1)S(1)}, u32[]{:S(2)}, u32[]{:S(2)}) collective-permute-start(bf16[256,260]{1,0:T(8,128)(2,1)S(1)} %pad_maximum_fusion.1), channel_id=1, source_target_pairs={{0,8},{8,16},{16,24},{24,32},{32,40},{40,48},{48,56},{56,64},{64,7... | collective-permute-start | bytes 399368 | tf_op jit(solution)/shard_map/ppermute | solution.py:15
  20.5 0.8 slice-start
  20.5 0.9 slice-start.1
  21.5 23.5 %collective-permute-start = (bf16[256,262]{1,0:T(8,128)(2,1)S(1)}, bf16[256,262]{1,0:T(8,128)(2,1)S(1)}, u32[]{:S(2)}, u32[]{:S(2)}) collective-permute-start(bf16[256,262]{1,0:T(8,128)(2,1)S(1)} %pad_maximum_fusion), channel_id=1, source_target_pairs={{8,0},{16,8},{24,16},{32,24},{40,32},{48,40},{56,48},{64,56},{72,6... | collective-permute-start | bytes 402440 | tf_op jit(solution)/shard_map/ppermute | solution.py:15
  24.7 16.6 %all-to-all-start.1 = ((f32[8,1,320]{2,1,0:T(1,128)}), f32[8,1,320]{2,1,0:T(1,128)S(1)}, u32[]{:S(2)}, u32[]{:S(2)}) async-start(f32[8,1,320]{2,1,0:T(1,128)} %reshape.180), calls=%async_computation.1 | async-start | bytes 24576 | tf_op jit(solution)/shard_map/all_to_all | solution.py:158
  45.2 0.9 copy-start.1
  60.0 9.9 %all-to-all-start.2 = ((f32[8,1,320]{2,1,0:T(1,128)}), f32[8,1,320]{2,1,0:T(1,128)S(1)}, u32[]{:S(2)}, u32[]{:S(2)}) async-start(f32[8,1,320]{2,1,0:T(1,128)} %reshape.182), calls=%async_computation.2 | async-start | bytes 24576 | tf_op jit(solution)/shard_map/all_to_all | solution.py:232
  71.3 23.1 %all-to-all-start.3 = ((f32[64,1,72]{2,1,0:T(1,128)}), f32[64,1,72]{2,1,0:T(1,128)S(1)}, u32[]{:S(2)}, u32[]{:S(2)}) async-start(f32[64,1,72]{2,1,0:T(1,128)} %bitcast.21), calls=%async_computation.3 | async-start | bytes 65536 | tf_op jit(solution)/shard_map/all_to_all | solution.py:248

commit v10 on v9

--- a/solution.py
+++ b/solution.py
@@ -155,15 +155,10 @@
         .transpose(1, 0, 2)
         .reshape(groups, taps_count)
     )
-    moved = lax.all_to_all(gathered[:, n_filt:], "fsdp", 0, 0, tiled=True)
-    local = (
-        moved.reshape(fsdp_size, per_block, n_chunk).transpose(1, 0, 2).reshape(ctx_size, n_chunk)
-    )
-    taps_all = (
-        local[:, : 9 * chunk].reshape(ctx_size, 3, 3, chunk).transpose(1, 2, 0, 3).reshape(3, 3, channels)
-    )
-    skip_all = local[:, 9 * chunk :].reshape(channels)
-
+    chunk_rows, outer_gate, inner_gate, value_stream, grad_output = lax.optimization_barrier(
+        (gathered[:, n_filt:], outer_gate, inner_gate, value_stream, grad_output)
+    )
+    moved = lax.all_to_all(chunk_rows, "fsdp", 0, 0, tiled=True)
     rim = reach_cols + 2
     prev_rim = passed_along(
         jnp.concatenate(
@@ -180,6 +175,14 @@
         "ctx",
         -1,
     )
+    local = (
+        moved.reshape(fsdp_size, per_block, n_chunk).transpose(1, 0, 2).reshape(ctx_size, n_chunk)
+    )
+    taps_all = (
+        local[:, : 9 * chunk].reshape(ctx_size, 3, 3, chunk).transpose(1, 2, 0, 3).reshape(3, 3, channels)
+    )
+    skip_all = local[:, 9 * chunk :].reshape(channels)
+
     outer_ext = jnp.concatenate([prev_rim[:, :2], outer_gate, next_rim[:, rim : 2 * rim]], axis=1)
     inner_ext = jnp.concatenate(
         [prev_rim[:, 2 : 2 + rim], inner_gate, next_rim[:, 2 * rim : 2 * rim + 2]], axis=1

time: 97.1 us -> 97.1 us (level)
  blocking collectives: 0 us -> 20.7 us
  starting transfers between devices: 44.4 us -> 30 us
  waiting for transfers between devices: 18.6 us -> 13.4 us
    all_to_all x0 -> x1, blocking collectives: none -> 20.7 us  [shards(): lax.all_to_all(jnp.broadcast_to(row[None], (ctx_size, row.shape[0])), 'ct...]
    all_to_all x2 -> x1, starting transfers between devices: 21.7 us -> 10 us  [shards(): moved = lax.all_to_all(chunk_rows, 'fsdp', 0, 0, tiled=True)]
    all_to_all x2 -> x1, waiting for transfers between devices: 6.7 us -> 0.03 us  [shards(): moved = lax.all_to_all(chunk_rows, 'fsdp', 0, 0, tiled=True)]
    all_to_all x1, starting transfers between devices: 13.8 us -> 8.07 us  [shards(): reduced = jnp.sum(lax.all_to_all(send, 'ctx', 0, 0, tiled=True), axis=0)]
    all_to_all x1, starting transfers between devices: 3.34 us -> 6.93 us  [shards(): by_owner = lax.all_to_all(to_fsdp, 'fsdp', 0, 0, tiled=True)]
    unnamed x18 -> x20, local copies, waits for them, and re-layouts: 3.89 us -> 5.96 us
    ppermute x2, waiting for transfers between devices: 0.01 us -> 1.41 us  [passed_along(): return lax.ppermute(shard, axis, pairs)]
  transfers between devices with their start and end apart: 6 -> 5, of which waited for: 4 -> 3; matrix products, arithmetic and copies ran while one was open for 10% -> 8% of each run, Pallas kernels for 0% -> 0%
where the time goes in v10:
time: 97.1 us; the launch traced here: 96.7 us
  starting transfers between devices  30 us (31%)
  blocking collectives  20.7 us (21%)
  local copies, waits for them, and re-layouts  14.4 us (15%)
  waiting for transfers between devices  13.4 us (14%)
  other arithmetic  9.72 us (10%)
  Pallas kernels  7.3 us (8%)
  between operations  1.12 us (1%)
    all_to_all x1, blocking collectives, shards(): lax.all_to_all(jnp.broadcast_to(row[None], (ctx_size, row.shape[0])), 'ct...  20.7 us
    all_to_all x1, starting transfers between devices, shards(): moved = lax.all_to_all(chunk_rows, 'fsdp', 0, 0, tiled=True)  10 us
    all_to_all x1, starting transfers between devices, shards(): reduced = jnp.sum(lax.all_to_all(send, 'ctx', 0, 0, tiled=True), axis=0)  8.07 us
    pallas_call x1, Pallas kernels, both_convs(): pl.pallas_call(functools.partial(banded_kernel, here=here), out_shape=(ja...  7.3 us
    all_to_all x1, waiting for transfers between devices, shards(): reduced = jnp.sum(lax.all_to_all(send, 'ctx', 0, 0, tiled=True), axis=0)  7.28 us
    all_to_all x1, starting transfers between devices, shards(): by_owner = lax.all_to_all(to_fsdp, 'fsdp', 0, 0, tiled=True)  6.93 us
    unnamed x20, local copies, waits for them, and re-layouts  5.96 us
    ppermute x2, starting transfers between devices, passed_along(): return lax.ppermute(shard, axis, pairs)  5.01 us
  transfers between devices with their start and end apart: 5, of which 3 were waited for; matrix products, arithmetic and copies ran while one was open for 8% of the time, Pallas kernels for 0%

profile of v10, /device:TPU:1, one launch (start us, length us, event | category | flops | bytes accessed | tf_op | source)
XLA Modules:
  0.0 96.7 jit_solution(5463932324101135183)
XLA Ops:
  0.6 0.8 reshape.163
  1.6 0.6 copy-done.6
  2.3 20.7 %all_to_all.39 = f32[64,1,72]{2,1,0:T(1,128)S(1)} all-to-all(f32[64,1,72]{2,1,0:T(1,128)S(1)} %broadcast_in_dim.2), channel_id=1, replica_groups=mesh['ctx'=64,'fsdp'=8] {'ctx'}, dimensions={0} | all-to-all | bytes 36864 | tf_op jit(solution)/shard_map/all_to_all | solution.py:146
  23.1 0.8 copy-done.2
  24.0 0.8 copy-done
  25.0 0.7 reshape.180
  25.7 10.0 %all-to-all-start.1 = ((f32[8,1,320]{2,1,0:T(1,128)}), f32[8,1,320]{2,1,0:T(1,128)S(1)}, u32[]{:S(2)}, u32[]{:S(2)}) async-start(f32[8,1,320]{2,1,0:T(1,128)} %reshape.180), calls=%async_computation.1 | async-start | bytes 24576 | tf_op jit(solution)/shard_map/all_to_all | solution.py:161
  36.0 0.8 copy-done.3
  36.9 0.2 pad_maximum_fusion.1
  37.1 3.1 %collective-permute-start.1 = (bf16[256,260]{1,0:T(8,128)(2,1)S(1)}, bf16[256,260]{1,0:T(8,128)(2,1)S(1)}, u32[]{:S(2)}, u32[]{:S(2)}) collective-permute-start(bf16[256,260]{1,0:T(8,128)(2,1)S(1)} %pad_maximum_fusion.1), channel_id=1, source_target_pairs={{0,8},{8,16},{16,24},{24,32},{32,40},{40,48},{48,56},{56,64},{64,7... | collective-permute-start | bytes 399368 | tf_op jit(solution)/shard_map/ppermute | solution.py:15
  40.2 0.1 pad_maximum_fusion
  40.4 1.9 %collective-permute-start = (bf16[256,262]{1,0:T(8,128)(2,1)S(1)}, bf16[256,262]{1,0:T(8,128)(2,1)S(1)}, u32[]{:S(2)}, u32[]{:S(2)}) collective-permute-start(bf16[256,262]{1,0:T(8,128)(2,1)S(1)} %pad_maximum_fusion), channel_id=1, source_target_pairs={{8,0},{16,8},{24,16},{32,24},{40,32},{48,40},{56,48},{64,56},{72,6... | collective-permute-start | bytes 402440 | tf_op jit(solution)/shard_map/ppermute | solution.py:15
  42.3 0.5 broadcast.16
  42.8 0.7 reduce.1
  45.8 0.1 fusion.37
  45.9 1.4 %collective-permute-done = bf16[256,262]{1,0:T(8,128)(2,1)S(1)} collective-permute-done((bf16[256,262]{1,0:T(8,128)(2,1)S(1)}, bf16[256,262]{1,0:T(8,128)(2,1)S(1)}, u32[]{:S(2)}, u32[]{:S(2)}) %collective-permute-start) | collective-permute-done | bytes 134176 | tf_op jit(solution)/shard_map/ppermute | solution.py:15
  47.6 0.1 maximum_convert_fusion.1
  47.8 0.7 copy-done.1
  48.5 0.1 maximum_convert_fusion.2
  48.7 0.9 multiply_convert_fusion.1
  49.6 0.1 slice_convert_fusion
  49.8 0.2 maximum_convert_fusion.3
  49.9 0.5 multiply_convert_fusion
  50.4 7.3 %shard_map.126 = (f32[16,16,272]{2,1,0:T(8,128)S(1)}, f32[16,16,272]{2,1,0:T(8,128)S(1)}, f32[16,1,128]{2,1,0:T(1,128)S(1)}) custom-call(f32[16,1,512]{2,1,0:T(1,128)S(1)} %reshape.164.ahead_ref, f32[16,1,512]{2,1,0:T(1,128)S(1)} %reshape.165.behind_ref, bf16[16,16,512]{2,1,0:T(8,128)(2,1)S(1)} %bitcast.60, bf16[16,16,512]{2,1,0:T(8,128)(2,1)S(1)} %bitcast.61), custom_call_target="tpu_custom_call" | custom-call | flops 276824064 | bytes 1081344 | tf_op jit(solution)/shard_map/pallas_call | solution.py:119
  57.7 0.4 fusion.8
  58.2 0.4 fusion.16
  58.8 0.6 fusion.10
  59.5 0.1 stack.52
  59.7 0.1 stack.50
  59.9 0.1 stack.44
  60.1 0.1 stack.42
  60.3 0.1 stack.46
  61.0 0.1 copy.88
  61.1 0.1 fusion.27
  61.5 0.7 reshape.182
  62.2 6.9 %all-to-all-start.2 = ((f32[8,1,320]{2,1,0:T(1,128)}), f32[8,1,320]{2,1,0:T(1,128)S(1)}, u32[]{:S(2)}, u32[]{:S(2)}) async-start(f32[8,1,320]{2,1,0:T(1,128)} %reshape.182), calls=%async_computation.2 | async-start | bytes 24576 | tf_op jit(solution)/shard_map/all_to_all | solution.py:235
  69.1 1.0 %fusion.25 = bf16[256,256]{1,0:T(8,128)(2,1)} fusion(f32[256,258]{1,0:T(8,128)S(1)} %convert_element_type.144, f32[256]{0:T(256)S(1)} %mul.275, f32[256]{0:T(256)S(1)} %mul.272, f32[256]{0:T(256)S(1)} %mul.269), kind=kLoop, calls=%fused_computation.57 | loop fusion | flops 393216 | bytes 920576 | tf_op jit(solution)/shard_map/convert_element_type | solution.py:257
  70.1 0.7 multiply_convert_fusion.2
  71.0 4.7 %all-to-all-done.2 = f32[8,1,320]{2,1,0:T(1,128)S(1)} async-done(((f32[8,1,320]{2,1,0:T(1,128)}), f32[8,1,320]{2,1,0:T(1,128)S(1)}, u32[]{:S(2)}, u32[]{:S(2)}) %all-to-all-start.2) | async-done | bytes 10272 | tf_op jit(solution)/shard_map/all_to_all | solution.py:235
  75.7 0.7 reduce.2
  76.5 0.7 pad_maximum_fusion.5
  77.1 8.1 %all-to-all-start.3 = ((f32[64,1,72]{2,1,0:T(1,128)}), f32[64,1,72]{2,1,0:T(1,128)S(1)}, u32[]{:S(2)}, u32[]{:S(2)}) async-start(f32[64,1,72]{2,1,0:T(1,128)} %bitcast.21), calls=%async_computation.3 | async-start | bytes 65536 | tf_op jit(solution)/shard_map/all_to_all | solution.py:251
  85.2 1.0 %fusion.22 = bf16[256,256]{1,0:T(8,128)(2,1)} fusion(f32[256,258]{1,0:T(8,128)S(1)} %convert_element_type.146, f32[256]{0:T(256)S(1)} %mul.256, f32[256]{0:T(256)S(1)} %mul.253, f32[256]{0:T(256)S(1)} %mul.250), kind=kLoop, calls=%fused_computation.51 | loop fusion | flops 393216 | bytes 920576 | tf_op jit(solution)/shard_map/convert_element_type | solution.py:258
  86.2 1.0 %fusion.19 = bf16[256,256]{1,0:T(8,128)(2,1)} fusion(f32[256,258]{1,0:T(8,128)S(1)} %convert_element_type.148, f32[256]{0:T(256)S(1)} %mul.265, f32[256]{0:T(256)S(1)} %mul.262, f32[256]{0:T(256)S(1)} %mul.259), kind=kLoop, calls=%fused_computation.45 | loop fusion | flops 393216 | bytes 920576 | tf_op jit(solution)/shard_map/convert_element_type | solution.py:259
  87.2 7.3 %all-to-all-done.3 = f32[64,1,72]{2,1,0:T(1,128)S(1)} async-done(((f32[64,1,72]{2,1,0:T(1,128)}), f32[64,1,72]{2,1,0:T(1,128)S(1)}, u32[]{:S(2)}, u32[]{:S(2)}) %all-to-all-start.3) | async-done | bytes 18464 | tf_op jit(solution)/shard_map/all_to_all | solution.py:251
  94.6 0.6 slice.332
  95.2 0.7 reshape.177
  96.0 0.6 copy.93
  (95 shorter events, 5.7 us)
Async XLA Ops:
  0.6 0.8 copy-start.5
  1.5 0.7 copy-start.6
  23.0 0.9 copy-start.2
  23.9 0.9 copy-start
  25.7 16.6 %all-to-all-start.1 = ((f32[8,1,320]{2,1,0:T(1,128)}), f32[8,1,320]{2,1,0:T(1,128)S(1)}, u32[]{:S(2)}, u32[]{:S(2)}) async-start(f32[8,1,320]{2,1,0:T(1,128)} %reshape.180), calls=%async_computation.1 | async-start | bytes 24576 | tf_op jit(solution)/shard_map/all_to_all | solution.py:161
  35.9 0.9 copy-start.3
  36.9 3.3 %slice-start = ((bf16[256,256]{1,0:T(8,128)(2,1)}), bf16[256,2]{1,0:T(8,128)(2,1)S(1)}, s32[]{:S(2)}) async-start(bf16[256,256]{1,0:T(8,128)(2,1)} %param.9), calls=%async_computation.4 | async-start | bytes 131072 | tf_op jit(solution)/shard_map/slice | solution.py:173
  36.9 3.3 %slice-start.1 = ((bf16[256,256]{1,0:T(8,128)(2,1)}), bf16[256,2]{1,0:T(8,128)(2,1)S(1)}, s32[]{:S(2)}) async-start(bf16[256,256]{1,0:T(8,128)(2,1)} %param.8), calls=%async_computation.5 | async-start | bytes 131072 | tf_op jit(solution)/shard_map/slice | solution.py:173
  36.9 3.3 %copy-start.4 = (bf16[256,256]{1,0:T(8,128)(2,1)S(1)}, bf16[256,256]{1,0:T(8,128)(2,1)}, u32[]{:S(2)}) copy-start(bf16[256,256]{1,0:T(8,128)(2,1)} %param.10) | copy-start | bytes 393220
  37.1 8.7 %collective-permute-start.1 = (bf16[256,260]{1,0:T(8,128)(2,1)S(1)}, bf16[256,260]{1,0:T(8,128)(2,1)S(1)}, u32[]{:S(2)}, u32[]{:S(2)}) collective-permute-start(bf16[256,260]{1,0:T(8,128)(2,1)S(1)} %pad_maximum_fusion.1), channel_id=1, source_target_pairs={{0,8},{8,16},{16,24},{24,32},{32,40},{40,48},{48,56},{56,64},{64,7... | collective-permute-start | bytes 399368 | tf_op jit(solution)/shard_map/ppermute | solution.py:15
  40.4 7.0 %collective-permute-start = (bf16[256,262]{1,0:T(8,128)(2,1)S(1)}, bf16[256,262]{1,0:T(8,128)(2,1)S(1)}, u32[]{:S(2)}, u32[]{:S(2)}) collective-permute-start(bf16[256,262]{1,0:T(8,128)(2,1)S(1)} %pad_maximum_fusion), channel_id=1, source_target_pairs={{8,0},{16,8},{24,16},{32,24},{40,32},{48,40},{56,48},{64,56},{72,6... | collective-permute-start | bytes 402440 | tf_op jit(solution)/shard_map/ppermute | solution.py:15
  47.6 0.9 copy-start.1
  62.2 13.5 %all-to-all-start.2 = ((f32[8,1,320]{2,1,0:T(1,128)}), f32[8,1,320]{2,1,0:T(1,128)S(1)}, u32[]{:S(2)}, u32[]{:S(2)}) async-start(f32[8,1,320]{2,1,0:T(1,128)} %reshape.182), calls=%async_computation.2 | async-start | bytes 24576 | tf_op jit(solution)/shard_map/all_to_all | solution.py:235
  77.1 17.4 %all-to-all-start.3 = ((f32[64,1,72]{2,1,0:T(1,128)}), f32[64,1,72]{2,1,0:T(1,128)S(1)}, u32[]{:S(2)}, u32[]{:S(2)}) async-start(f32[64,1,72]{2,1,0:T(1,128)} %bitcast.21), calls=%async_computation.3 | async-start | bytes 65536 | tf_op jit(solution)/shard_map/all_to_all | solution.py:251

commit v11 on v9

--- a/solution.py
+++ b/solution.py
@@ -245,10 +245,10 @@
         ],
         axis=1,
     )
-    reduced = jnp.sum(lax.all_to_all(send, "ctx", 0, 0, tiled=True), axis=0)
-    filter_share = reduced[:n_filt].reshape(groups, taps_here)
-    taps_share = reduced[n_filt : n_filt + 9 * chunk].reshape(3, 3, chunk)
-    skip_share = reduced[n_filt + 9 * chunk :]
+    arrived = lax.all_to_all(send, "ctx", 0, 0, tiled=True)
+    filter_share = jnp.sum(arrived[:, :n_filt], axis=0).reshape(groups, taps_here)
+    taps_share = jnp.sum(arrived[:, n_filt : n_filt + 9 * chunk], axis=0).reshape(3, 3, chunk)
+    skip_share = jnp.sum(arrived[:, n_filt + 9 * chunk :], axis=0)
     return (
         gated_out,
         grad_outer.astype(jnp.bfloat16),

time: 97.1 us -> 97.1 us (level)
  no operation moved by 1% of the time
where the time goes in v11:
time: 97.1 us; the launch traced here: 96.6 us
  starting transfers between devices  44.4 us (46%)
  waiting for transfers between devices  18.6 us (19%)
  local copies, waits for them, and re-layouts  14 us (14%)
  other arithmetic  11.1 us (11%)
  Pallas kernels  7.3 us (8%)
  between operations  1.15 us (1%)
    all_to_all x1, starting transfers between devices, shards(): arrived = lax.all_to_all(send, 'ctx', 0, 0, tiled=True)  13.8 us
    all_to_all x1, starting transfers between devices, shards(): lax.all_to_all(jnp.broadcast_to(row[None], (ctx_size, row.shape[0])), 'ct...  11.6 us
    all_to_all x1, starting transfers between devices, shards(): moved = lax.all_to_all(gathered[:, n_filt:], 'fsdp', 0, 0, tiled=True)  10 us
    pallas_call x1, Pallas kernels, both_convs(): pl.pallas_call(functools.partial(banded_kernel, here=here), out_shape=(ja...  7.3 us
    all_to_all x1, waiting for transfers between devices, shards(): arrived = lax.all_to_all(send, 'ctx', 0, 0, tiled=True)  7.28 us
    all_to_all x1, waiting for transfers between devices, shards(): moved = lax.all_to_all(gathered[:, n_filt:], 'fsdp', 0, 0, tiled=True)  6.27 us
    ppermute x2, starting transfers between devices, passed_along(): return lax.ppermute(shard, axis, pairs)  5.59 us
    all_to_all x1, waiting for transfers between devices, shards(): by_owner = lax.all_to_all(to_fsdp, 'fsdp', 0, 0, tiled=True)  4.61 us
  transfers between devices with their start and end apart: 6, of which 4 were waited for; matrix products, arithmetic and copies ran while one was open for 10% of the time, Pallas kernels for 0%

profile of v11, /device:TPU:1, one launch (start us, length us, event | category | flops | bytes accessed | tf_op | source)
XLA Modules:
  0.0 96.6 jit_solution(6555595022316140769)
XLA Ops:
  0.7 0.8 reshape.155
  1.6 0.7 pad_maximum_fusion.6
  2.4 0.6 broadcast_in_dim.2
  3.0 11.6 %all-to-all-start = ((f32[64,1,72]{2,1,0:T(1,128)}), f32[64,1,72]{2,1,0:T(1,128)S(1)}, u32[]{:S(2)}, u32[]{:S(2)}) async-start(f32[64,1,72]{2,1,0:T(1,128)} %broadcast_in_dim.2), calls=%async_computation | async-start | bytes 65536 | tf_op jit(solution)/shard_map/all_to_all | solution.py:146
  14.6 0.9 slice.267
  15.7 0.8 copy-done.2
  16.6 0.2 pad_maximum_fusion.1
  16.8 3.7 %collective-permute-start.1 = (bf16[256,260]{1,0:T(8,128)(2,1)S(1)}, bf16[256,260]{1,0:T(8,128)(2,1)S(1)}, u32[]{:S(2)}, u32[]{:S(2)}) collective-permute-start(bf16[256,260]{1,0:T(8,128)(2,1)S(1)} %pad_maximum_fusion.1), channel_id=1, source_target_pairs={{0,8},{8,16},{16,24},{24,32},{32,40},{40,48},{48,56},{56,64},{64,7... | collective-permute-start | bytes 399368 | tf_op jit(solution)/shard_map/ppermute | solution.py:15
  20.5 0.8 slice-done
  21.3 0.1 pad_maximum_fusion
  21.5 1.9 %collective-permute-start = (bf16[256,262]{1,0:T(8,128)(2,1)S(1)}, bf16[256,262]{1,0:T(8,128)(2,1)S(1)}, u32[]{:S(2)}, u32[]{:S(2)}) collective-permute-start(bf16[256,262]{1,0:T(8,128)(2,1)S(1)} %pad_maximum_fusion), channel_id=1, source_target_pairs={{8,0},{16,8},{24,16},{32,24},{40,32},{48,40},{56,48},{64,56},{72,6... | collective-permute-start | bytes 402440 | tf_op jit(solution)/shard_map/ppermute | solution.py:15
  23.4 0.4 all-to-all-done
  24.0 0.7 reshape.172
  24.7 10.0 %all-to-all-start.1 = ((f32[8,1,320]{2,1,0:T(1,128)}), f32[8,1,320]{2,1,0:T(1,128)S(1)}, u32[]{:S(2)}, u32[]{:S(2)}) async-start(f32[8,1,320]{2,1,0:T(1,128)} %reshape.172), calls=%async_computation.1 | async-start | bytes 24576 | tf_op jit(solution)/shard_map/all_to_all | solution.py:158
  35.1 6.3 %all-to-all-done.1 = f32[8,1,320]{2,1,0:T(1,128)S(1)} async-done(((f32[8,1,320]{2,1,0:T(1,128)}), f32[8,1,320]{2,1,0:T(1,128)S(1)}, u32[]{:S(2)}, u32[]{:S(2)}) %all-to-all-start.1) | async-done | bytes 10272 | tf_op jit(solution)/shard_map/all_to_all | solution.py:158
  41.4 0.5 broadcast.16
  41.9 0.7 reduce
  44.8 0.1 fusion.37
  45.3 0.8 copy-done.1
  46.1 0.3 maximum_convert_fusion.1
  46.4 0.9 multiply_convert_fusion.1
  47.3 0.1 slice_convert_fusion
  47.4 0.2 maximum_convert_fusion.3
  47.6 0.5 multiply_convert_fusion
  48.1 7.3 %shard_map.126 = (f32[16,16,272]{2,1,0:T(8,128)S(1)}, f32[16,16,272]{2,1,0:T(8,128)S(1)}, f32[16,1,128]{2,1,0:T(1,128)S(1)}) custom-call(f32[16,1,512]{2,1,0:T(1,128)S(1)} %reshape.156.ahead_ref, f32[16,1,512]{2,1,0:T(1,128)S(1)} %reshape.157.behind_ref, bf16[16,16,512]{2,1,0:T(8,128)(2,1)S(1)} %bitcast.60, bf16[16,16,512]{2,1,0:T(8,128)(2,1)S(1)} %bitcast.61), custom_call_target="tpu_custom_call" | custom-call | flops 276824064 | bytes 1081344 | tf_op jit(solution)/shard_map/pallas_call | solution.py:119
  55.4 0.4 fusion.8
  55.8 0.4 fusion.13
  56.2 0.4 fusion.16
  56.5 0.3 fusion.10
  57.1 0.1 stack.51
  58.3 0.1 stack.44
  58.5 0.1 stack.42
  58.8 0.1 copy.88
  58.9 0.1 fusion.27
  59.3 0.7 reshape.174
  60.0 3.3 %all-to-all-start.2 = ((f32[8,1,320]{2,1,0:T(1,128)}), f32[8,1,320]{2,1,0:T(1,128)S(1)}, u32[]{:S(2)}, u32[]{:S(2)}) async-start(f32[8,1,320]{2,1,0:T(1,128)} %reshape.174), calls=%async_computation.2 | async-start | bytes 24576 | tf_op jit(solution)/shard_map/all_to_all | solution.py:232
  63.4 1.0 %fusion.25 = bf16[256,256]{1,0:T(8,128)(2,1)} fusion(f32[256,258]{1,0:T(8,128)S(1)} %convert_element_type.144, f32[256]{0:T(256)S(1)} %mul.275, f32[256]{0:T(256)S(1)} %mul.272, f32[256]{0:T(256)S(1)} %mul.269), kind=kLoop, calls=%fused_computation.57 | loop fusion | flops 393216 | bytes 920576 | tf_op jit(solution)/shard_map/convert_element_type | solution.py:254
  64.3 0.7 multiply_convert_fusion.2
  65.3 4.6 %all-to-all-done.2 = f32[8,1,320]{2,1,0:T(1,128)S(1)} async-done(((f32[8,1,320]{2,1,0:T(1,128)}), f32[8,1,320]{2,1,0:T(1,128)S(1)}, u32[]{:S(2)}, u32[]{:S(2)}) %all-to-all-start.2) | async-done | bytes 10272 | tf_op jit(solution)/shard_map/all_to_all | solution.py:232
  69.9 0.7 reduce.1
  70.7 0.7 pad_maximum_fusion.5
  71.3 13.8 %all-to-all-start.3 = ((f32[64,1,72]{2,1,0:T(1,128)}), f32[64,1,72]{2,1,0:T(1,128)S(1)}, u32[]{:S(2)}, u32[]{:S(2)}) async-start(f32[64,1,72]{2,1,0:T(1,128)} %bitcast.21), calls=%async_computation.3 | async-start | bytes 65536 | tf_op jit(solution)/shard_map/all_to_all | solution.py:248
  85.2 1.0 %fusion.22 = bf16[256,256]{1,0:T(8,128)(2,1)} fusion(f32[256,258]{1,0:T(8,128)S(1)} %convert_element_type.146, f32[256]{0:T(256)S(1)} %mul.256, f32[256]{0:T(256)S(1)} %mul.253, f32[256]{0:T(256)S(1)} %mul.250), kind=kLoop, calls=%fused_computation.51 | loop fusion | flops 393216 | bytes 920576 | tf_op jit(solution)/shard_map/convert_element_type | solution.py:255
  86.2 1.0 %fusion.19 = bf16[256,256]{1,0:T(8,128)(2,1)} fusion(f32[256,258]{1,0:T(8,128)S(1)} %convert_element_type.148, f32[256]{0:T(256)S(1)} %mul.265, f32[256]{0:T(256)S(1)} %mul.262, f32[256]{0:T(256)S(1)} %mul.259), kind=kLoop, calls=%fused_computation.45 | loop fusion | flops 393216 | bytes 920576 | tf_op jit(solution)/shard_map/convert_element_type | solution.py:256
  87.1 7.3 %all-to-all-done.3 = f32[64,1,72]{2,1,0:T(1,128)S(1)} async-done(((f32[64,1,72]{2,1,0:T(1,128)}), f32[64,1,72]{2,1,0:T(1,128)S(1)}, u32[]{:S(2)}, u32[]{:S(2)}) %all-to-all-start.3) | async-done | bytes 18464 | tf_op jit(solution)/shard_map/all_to_all | solution.py:248
  94.4 0.6 slice_reduce_fusion
  95.1 0.7 reshape.169
  95.9 0.6 copy.93
  (94 shorter events, 5.8 us)
Async XLA Ops:
  0.6 0.8 copy-start.5
  0.6 14.9 %copy-start = (bf16[256,256]{1,0:T(8,128)(2,1)S(1)}, bf16[256,256]{1,0:T(8,128)(2,1)}, u32[]{:S(2)}) copy-start(bf16[256,256]{1,0:T(8,128)(2,1)} %param.8) | copy-start | bytes 393220
  3.0 20.8 %all-to-all-start = ((f32[64,1,72]{2,1,0:T(1,128)}), f32[64,1,72]{2,1,0:T(1,128)S(1)}, u32[]{:S(2)}, u32[]{:S(2)}) async-start(f32[64,1,72]{2,1,0:T(1,128)} %broadcast_in_dim.2), calls=%async_computation | async-start | bytes 65536 | tf_op jit(solution)/shard_map/all_to_all | solution.py:146
  15.6 0.9 copy-start.2
  16.6 3.9 %copy-start.4 = (bf16[256,256]{1,0:T(8,128)(2,1)S(1)}, bf16[256,256]{1,0:T(8,128)(2,1)}, u32[]{:S(2)}) copy-start(bf16[256,256]{1,0:T(8,128)(2,1)} %param.10) | copy-start | bytes 393220
  16.8 3.7 %copy-start.3 = (bf16[256,256]{1,0:T(8,128)(2,1)S(1)}, bf16[256,256]{1,0:T(8,128)(2,1)}, u32[]{:S(2)}) copy-start(bf16[256,256]{1,0:T(8,128)(2,1)} %param.7) | copy-start | bytes 393220
  16.8 28.0 %collective-permute-start.1 = (bf16[256,260]{1,0:T(8,128)(2,1)S(1)}, bf16[256,260]{1,0:T(8,128)(2,1)S(1)}, u32[]{:S(2)}, u32[]{:S(2)}) collective-permute-start(bf16[256,260]{1,0:T(8,128)(2,1)S(1)} %pad_maximum_fusion.1), channel_id=1, source_target_pairs={{0,8},{8,16},{16,24},{24,32},{32,40},{40,48},{48,56},{56,64},{64,7... | collective-permute-start | bytes 399368 | tf_op jit(solution)/shard_map/ppermute | solution.py:15
  20.5 0.8 slice-start
  20.5 0.9 slice-start.1
  21.5 23.5 %collective-permute-start = (bf16[256,262]{1,0:T(8,128)(2,1)S(1)}, bf16[256,262]{1,0:T(8,128)(2,1)S(1)}, u32[]{:S(2)}, u32[]{:S(2)}) collective-permute-start(bf16[256,262]{1,0:T(8,128)(2,1)S(1)} %pad_maximum_fusion), channel_id=1, source_target_pairs={{8,0},{16,8},{24,16},{32,24},{40,32},{48,40},{56,48},{64,56},{72,6... | collective-permute-start | bytes 402440 | tf_op jit(solution)/shard_map/ppermute | solution.py:15
  24.7 16.6 %all-to-all-start.1 = ((f32[8,1,320]{2,1,0:T(1,128)}), f32[8,1,320]{2,1,0:T(1,128)S(1)}, u32[]{:S(2)}, u32[]{:S(2)}) async-start(f32[8,1,320]{2,1,0:T(1,128)} %reshape.172), calls=%async_computation.1 | async-start | bytes 24576 | tf_op jit(solution)/shard_map/all_to_all | solution.py:158
  45.2 0.9 copy-start.1
  60.0 9.9 %all-to-all-start.2 = ((f32[8,1,320]{2,1,0:T(1,128)}), f32[8,1,320]{2,1,0:T(1,128)S(1)}, u32[]{:S(2)}, u32[]{:S(2)}) async-start(f32[8,1,320]{2,1,0:T(1,128)} %reshape.174), calls=%async_computation.2 | async-start | bytes 24576 | tf_op jit(solution)/shard_map/all_to_all | solution.py:232
  71.3 23.1 %all-to-all-start.3 = ((f32[64,1,72]{2,1,0:T(1,128)}), f32[64,1,72]{2,1,0:T(1,128)S(1)}, u32[]{:S(2)}, u32[]{:S(2)}) async-start(f32[64,1,72]{2,1,0:T(1,128)} %bitcast.21), calls=%async_computation.3 | async-start | bytes 65536 | tf_op jit(solution)/shard_map/all_to_all | solution.py:248

commit v12 on v9

--- a/solution.py
+++ b/solution.py
@@ -110,7 +110,7 @@
     behind = jnp.pad(as_rows, ((0, 0), (0, lanes - taps))).reshape(groups, 1, lanes)
     pw = jnp.pad(product, ((0, 0), (0, lanes - win))).reshape(groups, channels // groups, lanes)
     gw = jnp.pad(grad_mixed, ((0, 0), (0, lanes - win))).reshape(groups, channels // groups, lanes)
-    step = math.gcd(groups, 4)
+    step = math.gcd(groups, 8)
     size = channels // groups
 
     def blocks(*tail):

time: 97.1 us -> 96.6 us (level)
  no operation moved by 1% of the time
where the time goes in v12:
time: 96.6 us; the launch traced here: 96.1 us
  starting transfers between devices  44.4 us (46%)
  waiting for transfers between devices  18.6 us (19%)
  local copies, waits for them, and re-layouts  14.7 us (15%)
  other arithmetic  10.5 us (11%)
  Pallas kernels  6.79 us (7%)
  between operations  1.15 us (1%)
    all_to_all x1, starting transfers between devices, shards(): reduced = jnp.sum(lax.all_to_all(send, 'ctx', 0, 0, tiled=True), axis=0)  13.8 us
    all_to_all x1, starting transfers between devices, shards(): lax.all_to_all(jnp.broadcast_to(row[None], (ctx_size, row.shape[0])), 'ct...  11.6 us
    all_to_all x1, starting transfers between devices, shards(): moved = lax.all_to_all(gathered[:, n_filt:], 'fsdp', 0, 0, tiled=True)  10 us
    all_to_all x1, waiting for transfers between devices, shards(): reduced = jnp.sum(lax.all_to_all(send, 'ctx', 0, 0, tiled=True), axis=0)  7.28 us
    pallas_call x1, Pallas kernels, both_convs(): pl.pallas_call(functools.partial(banded_kernel, here=here), out_shape=(ja...  6.79 us
    all_to_all x1, waiting for transfers between devices, shards(): moved = lax.all_to_all(gathered[:, n_filt:], 'fsdp', 0, 0, tiled=True)  6.27 us
    ppermute x2, starting transfers between devices, passed_along(): return lax.ppermute(shard, axis, pairs)  5.59 us
    all_to_all x1, waiting for transfers between devices, shards(): by_owner = lax.all_to_all(to_fsdp, 'fsdp', 0, 0, tiled=True)  4.61 us
  transfers between devices with their start and end apart: 6, of which 4 were waited for; matrix products, arithmetic and copies ran while one was open for 10% of the time, Pallas kernels for 0%

profile of v12, /device:TPU:1, one launch (start us, length us, event | category | flops | bytes accessed | tf_op | source)
XLA Modules:
  0.0 96.1 jit_solution(8085774126877766699)
XLA Ops:
  0.7 0.8 reshape.163
  1.6 0.7 pad_maximum_fusion.6
  2.4 0.6 broadcast_in_dim.2
  3.0 11.6 %all-to-all-start = ((f32[64,1,72]{2,1,0:T(1,128)}), f32[64,1,72]{2,1,0:T(1,128)S(1)}, u32[]{:S(2)}, u32[]{:S(2)}) async-start(f32[64,1,72]{2,1,0:T(1,128)} %broadcast_in_dim.2), calls=%async_computation | async-start | bytes 65536 | tf_op jit(solution)/shard_map/all_to_all | solution.py:146
  14.6 0.9 slice.275
  15.7 0.8 copy-done.2
  16.6 0.2 pad_maximum_fusion.1
  16.8 3.7 %collective-permute-start.1 = (bf16[256,260]{1,0:T(8,128)(2,1)S(1)}, bf16[256,260]{1,0:T(8,128)(2,1)S(1)}, u32[]{:S(2)}, u32[]{:S(2)}) collective-permute-start(bf16[256,260]{1,0:T(8,128)(2,1)S(1)} %pad_maximum_fusion.1), channel_id=1, source_target_pairs={{0,8},{8,16},{16,24},{24,32},{32,40},{40,48},{48,56},{56,64},{64,7... | collective-permute-start | bytes 399368 | tf_op jit(solution)/shard_map/ppermute | solution.py:15
  20.5 0.8 slice-done
  21.3 0.1 pad_maximum_fusion
  21.5 1.9 %collective-permute-start = (bf16[256,262]{1,0:T(8,128)(2,1)S(1)}, bf16[256,262]{1,0:T(8,128)(2,1)S(1)}, u32[]{:S(2)}, u32[]{:S(2)}) collective-permute-start(bf16[256,262]{1,0:T(8,128)(2,1)S(1)} %pad_maximum_fusion), channel_id=1, source_target_pairs={{8,0},{16,8},{24,16},{32,24},{40,32},{48,40},{56,48},{64,56},{72,6... | collective-permute-start | bytes 402440 | tf_op jit(solution)/shard_map/ppermute | solution.py:15
  23.4 0.4 all-to-all-done
  24.0 0.7 reshape.180
  24.7 10.0 %all-to-all-start.1 = ((f32[8,1,320]{2,1,0:T(1,128)}), f32[8,1,320]{2,1,0:T(1,128)S(1)}, u32[]{:S(2)}, u32[]{:S(2)}) async-start(f32[8,1,320]{2,1,0:T(1,128)} %reshape.180), calls=%async_computation.1 | async-start | bytes 24576 | tf_op jit(solution)/shard_map/all_to_all | solution.py:158
  35.1 6.3 %all-to-all-done.1 = f32[8,1,320]{2,1,0:T(1,128)S(1)} async-done(((f32[8,1,320]{2,1,0:T(1,128)}), f32[8,1,320]{2,1,0:T(1,128)S(1)}, u32[]{:S(2)}, u32[]{:S(2)}) %all-to-all-start.1) | async-done | bytes 10272 | tf_op jit(solution)/shard_map/all_to_all | solution.py:158
  41.4 0.5 broadcast.16
  41.9 0.7 reduce.1
  44.8 0.1 fusion.37
  45.3 0.8 copy-done.1
  46.1 0.3 maximum_convert_fusion.1
  46.4 0.9 multiply_convert_fusion.1
  47.3 0.1 slice_convert_fusion
  47.4 0.2 maximum_convert_fusion.3
  47.6 0.5 multiply_convert_fusion
  48.1 6.8 %shard_map.126 = (f32[16,16,272]{2,1,0:T(8,128)S(1)}, f32[16,16,272]{2,1,0:T(8,128)S(1)}, f32[16,1,128]{2,1,0:T(1,128)S(1)}) custom-call(f32[16,1,512]{2,1,0:T(1,128)S(1)} %reshape.164.ahead_ref, f32[16,1,512]{2,1,0:T(1,128)S(1)} %reshape.165.behind_ref, bf16[16,16,512]{2,1,0:T(8,128)(2,1)S(1)} %bitcast.60, bf16[16,16,512]{2,1,0:T(8,128)(2,1)S(1)} %bitcast.61), custom_call_target="tpu_custom_call" | custom-call | flops 276824064 | bytes 1081344 | tf_op jit(solution)/shard_map/pallas_call | solution.py:119
  54.9 0.4 fusion.8
  55.3 0.4 fusion.13
  55.7 0.4 fusion.16
  56.0 0.3 fusion.10
  56.6 0.1 stack.51
  56.8 0.1 stack.43
  57.0 0.1 stack.48
  58.3 0.1 copy.88
  58.4 0.1 fusion.27
  58.8 0.7 reshape.182
  59.5 3.3 %all-to-all-start.2 = ((f32[8,1,320]{2,1,0:T(1,128)}), f32[8,1,320]{2,1,0:T(1,128)S(1)}, u32[]{:S(2)}, u32[]{:S(2)}) async-start(f32[8,1,320]{2,1,0:T(1,128)} %reshape.182), calls=%async_computation.2 | async-start | bytes 24576 | tf_op jit(solution)/shard_map/all_to_all | solution.py:232
  62.8 1.0 %fusion.25 = bf16[256,256]{1,0:T(8,128)(2,1)} fusion(f32[256,258]{1,0:T(8,128)S(1)} %convert_element_type.144, f32[256]{0:T(256)S(1)} %mul.275, f32[256]{0:T(256)S(1)} %mul.272, f32[256]{0:T(256)S(1)} %mul.269), kind=kLoop, calls=%fused_computation.57 | loop fusion | flops 393216 | bytes 920576 | tf_op jit(solution)/shard_map/convert_element_type | solution.py:254
  63.8 0.7 multiply_convert_fusion.2
  64.8 4.6 %all-to-all-done.2 = f32[8,1,320]{2,1,0:T(1,128)S(1)} async-done(((f32[8,1,320]{2,1,0:T(1,128)}), f32[8,1,320]{2,1,0:T(1,128)S(1)}, u32[]{:S(2)}, u32[]{:S(2)}) %all-to-all-start.2) | async-done | bytes 10272 | tf_op jit(solution)/shard_map/all_to_all | solution.py:232
  69.4 0.7 reduce.2
  70.1 0.7 pad_maximum_fusion.5
  70.8 13.8 %all-to-all-start.3 = ((f32[64,1,72]{2,1,0:T(1,128)}), f32[64,1,72]{2,1,0:T(1,128)S(1)}, u32[]{:S(2)}, u32[]{:S(2)}) async-start(f32[64,1,72]{2,1,0:T(1,128)} %bitcast.21), calls=%async_computation.3 | async-start | bytes 65536 | tf_op jit(solution)/shard_map/all_to_all | solution.py:248
  84.7 1.0 %fusion.22 = bf16[256,256]{1,0:T(8,128)(2,1)} fusion(f32[256,258]{1,0:T(8,128)S(1)} %convert_element_type.146, f32[256]{0:T(256)S(1)} %mul.256, f32[256]{0:T(256)S(1)} %mul.253, f32[256]{0:T(256)S(1)} %mul.250), kind=kLoop, calls=%fused_computation.51 | loop fusion | flops 393216 | bytes 920576 | tf_op jit(solution)/shard_map/convert_element_type | solution.py:255
  85.7 1.0 %fusion.19 = bf16[256,256]{1,0:T(8,128)(2,1)} fusion(f32[256,258]{1,0:T(8,128)S(1)} %convert_element_type.148, f32[256]{0:T(256)S(1)} %mul.265, f32[256]{0:T(256)S(1)} %mul.262, f32[256]{0:T(256)S(1)} %mul.259), kind=kLoop, calls=%fused_computation.45 | loop fusion | flops 393216 | bytes 920576 | tf_op jit(solution)/shard_map/convert_element_type | solution.py:256
  86.6 7.3 %all-to-all-done.3 = f32[64,1,72]{2,1,0:T(1,128)S(1)} async-done(((f32[64,1,72]{2,1,0:T(1,128)}), f32[64,1,72]{2,1,0:T(1,128)S(1)}, u32[]{:S(2)}, u32[]{:S(2)}) %all-to-all-start.3) | async-done | bytes 18464 | tf_op jit(solution)/shard_map/all_to_all | solution.py:248
  94.0 0.6 slice.332
  94.7 0.7 reshape.177
  95.4 0.6 copy.93
  (94 shorter events, 5.8 us)
Async XLA Ops:
  0.6 0.8 copy-start.5
  0.6 14.9 %copy-start = (bf16[256,256]{1,0:T(8,128)(2,1)S(1)}, bf16[256,256]{1,0:T(8,128)(2,1)}, u32[]{:S(2)}) copy-start(bf16[256,256]{1,0:T(8,128)(2,1)} %param.8) | copy-start | bytes 393220
  3.0 20.8 %all-to-all-start = ((f32[64,1,72]{2,1,0:T(1,128)}), f32[64,1,72]{2,1,0:T(1,128)S(1)}, u32[]{:S(2)}, u32[]{:S(2)}) async-start(f32[64,1,72]{2,1,0:T(1,128)} %broadcast_in_dim.2), calls=%async_computation | async-start | bytes 65536 | tf_op jit(solution)/shard_map/all_to_all | solution.py:146
  15.6 0.9 copy-start.2
  16.6 3.9 %copy-start.4 = (bf16[256,256]{1,0:T(8,128)(2,1)S(1)}, bf16[256,256]{1,0:T(8,128)(2,1)}, u32[]{:S(2)}) copy-start(bf16[256,256]{1,0:T(8,128)(2,1)} %param.10) | copy-start | bytes 393220
  16.8 3.7 %copy-start.3 = (bf16[256,256]{1,0:T(8,128)(2,1)S(1)}, bf16[256,256]{1,0:T(8,128)(2,1)}, u32[]{:S(2)}) copy-start(bf16[256,256]{1,0:T(8,128)(2,1)} %param.7) | copy-start | bytes 393220
  16.8 28.0 %collective-permute-start.1 = (bf16[256,260]{1,0:T(8,128)(2,1)S(1)}, bf16[256,260]{1,0:T(8,128)(2,1)S(1)}, u32[]{:S(2)}, u32[]{:S(2)}) collective-permute-start(bf16[256,260]{1,0:T(8,128)(2,1)S(1)} %pad_maximum_fusion.1), channel_id=1, source_target_pairs={{0,8},{8,16},{16,24},{24,32},{32,40},{40,48},{48,56},{56,64},{64,7... | collective-permute-start | bytes 399368 | tf_op jit(solution)/shard_map/ppermute | solution.py:15
  20.5 0.8 slice-start
  20.5 0.9 slice-start.1
  21.5 23.5 %collective-permute-start = (bf16[256,262]{1,0:T(8,128)(2,1)S(1)}, bf16[256,262]{1,0:T(8,128)(2,1)S(1)}, u32[]{:S(2)}, u32[]{:S(2)}) collective-permute-start(bf16[256,262]{1,0:T(8,128)(2,1)S(1)} %pad_maximum_fusion), channel_id=1, source_target_pairs={{8,0},{16,8},{24,16},{32,24},{40,32},{48,40},{56,48},{64,56},{72,6... | collective-permute-start | bytes 402440 | tf_op jit(solution)/shard_map/ppermute | solution.py:15
  24.7 16.6 %all-to-all-start.1 = ((f32[8,1,320]{2,1,0:T(1,128)}), f32[8,1,320]{2,1,0:T(1,128)S(1)}, u32[]{:S(2)}, u32[]{:S(2)}) async-start(f32[8,1,320]{2,1,0:T(1,128)} %reshape.180), calls=%async_computation.1 | async-start | bytes 24576 | tf_op jit(solution)/shard_map/all_to_all | solution.py:158
  45.2 0.9 copy-start.1
  59.5 9.9 %all-to-all-start.2 = ((f32[8,1,320]{2,1,0:T(1,128)}), f32[8,1,320]{2,1,0:T(1,128)S(1)}, u32[]{:S(2)}, u32[]{:S(2)}) async-start(f32[8,1,320]{2,1,0:T(1,128)} %reshape.182), calls=%async_computation.2 | async-start | bytes 24576 | tf_op jit(solution)/shard_map/all_to_all | solution.py:232
  70.8 23.1 %all-to-all-start.3 = ((f32[64,1,72]{2,1,0:T(1,128)}), f32[64,1,72]{2,1,0:T(1,128)S(1)}, u32[]{:S(2)}, u32[]{:S(2)}) async-start(f32[64,1,72]{2,1,0:T(1,128)} %bitcast.21), calls=%async_computation.3 | async-start | bytes 65536 | tf_op jit(solution)/shard_map/all_to_all | solution.py:248

commit v13 on v12

--- a/solution.py
+++ b/solution.py
@@ -110,7 +110,7 @@
     behind = jnp.pad(as_rows, ((0, 0), (0, lanes - taps))).reshape(groups, 1, lanes)
     pw = jnp.pad(product, ((0, 0), (0, lanes - win))).reshape(groups, channels // groups, lanes)
     gw = jnp.pad(grad_mixed, ((0, 0), (0, lanes - win))).reshape(groups, channels // groups, lanes)
-    step = math.gcd(groups, 8)
+    step = groups
     size = channels // groups
 
     def blocks(*tail):

time: 96.6 us -> 95.9 us (level)
  transfers between devices with their start and end apart: 6 -> 6, of which waited for: 4 -> 4; matrix products, arithmetic and copies ran while one was open for 10% -> 11% of each run, Pallas kernels for 0% -> 0%
where the time goes in v13:
time: 95.9 us; the launch traced here: 95.4 us
  starting transfers between devices  44.6 us (47%)
  waiting for transfers between devices  18.6 us (19%)
  local copies, waits for them, and re-layouts  14.7 us (15%)
  other arithmetic  10.5 us (11%)
  Pallas kernels  5.93 us (6%)
  between operations  1.14 us (1%)
    all_to_all x1, starting transfers between devices, shards(): reduced = jnp.sum(lax.all_to_all(send, 'ctx', 0, 0, tiled=True), axis=0)  13.8 us
    all_to_all x1, starting transfers between devices, shards(): lax.all_to_all(jnp.broadcast_to(row[None], (ctx_size, row.shape[0])), 'ct...  11.6 us
    all_to_all x1, starting transfers between devices, shards(): moved = lax.all_to_all(gathered[:, n_filt:], 'fsdp', 0, 0, tiled=True)  10 us
    all_to_all x1, waiting for transfers between devices, shards(): reduced = jnp.sum(lax.all_to_all(send, 'ctx', 0, 0, tiled=True), axis=0)  7.28 us
    all_to_all x1, waiting for transfers between devices, shards(): moved = lax.all_to_all(gathered[:, n_filt:], 'fsdp', 0, 0, tiled=True)  6.27 us
    pallas_call x1, Pallas kernels, both_convs(): pl.pallas_call(functools.partial(banded_kernel, here=here), out_shape=(ja...  5.93 us
    ppermute x2, starting transfers between devices, passed_along(): return lax.ppermute(shard, axis, pairs)  5.59 us
    all_to_all x1, waiting for transfers between devices, shards(): by_owner = lax.all_to_all(to_fsdp, 'fsdp', 0, 0, tiled=True)  4.61 us
  transfers between devices with their start and end apart: 6, of which 4 were waited for; matrix products, arithmetic and copies ran while one was open for 11% of the time, Pallas kernels for 0%

profile of v13, /device:TPU:1, one launch (start us, length us, event | category | flops | bytes accessed | tf_op | source)
XLA Modules:
  0.0 95.4 jit_solution(3359756117144630665)
XLA Ops:
  0.7 0.8 reshape.163
  1.6 0.7 pad_maximum_fusion.6
  2.4 0.6 broadcast_in_dim.2
  3.0 11.6 %all-to-all-start = ((f32[64,1,72]{2,1,0:T(1,128)}), f32[64,1,72]{2,1,0:T(1,128)S(1)}, u32[]{:S(2)}, u32[]{:S(2)}) async-start(f32[64,1,72]{2,1,0:T(1,128)} %broadcast_in_dim.2), calls=%async_computation | async-start | bytes 65536 | tf_op jit(solution)/shard_map/all_to_all | solution.py:146
  14.6 0.9 slice.275
  15.7 0.8 copy-done.2
  16.6 0.2 pad_maximum_fusion.1
  16.8 3.7 %collective-permute-start.1 = (bf16[256,260]{1,0:T(8,128)(2,1)S(1)}, bf16[256,260]{1,0:T(8,128)(2,1)S(1)}, u32[]{:S(2)}, u32[]{:S(2)}) collective-permute-start(bf16[256,260]{1,0:T(8,128)(2,1)S(1)} %pad_maximum_fusion.1), channel_id=1, source_target_pairs={{0,8},{8,16},{16,24},{24,32},{32,40},{40,48},{48,56},{56,64},{64,7... | collective-permute-start | bytes 399368 | tf_op jit(solution)/shard_map/ppermute | solution.py:15
  20.5 0.8 slice-done
  21.3 0.1 pad_maximum_fusion
  21.5 1.9 %collective-permute-start = (bf16[256,262]{1,0:T(8,128)(2,1)S(1)}, bf16[256,262]{1,0:T(8,128)(2,1)S(1)}, u32[]{:S(2)}, u32[]{:S(2)}) collective-permute-start(bf16[256,262]{1,0:T(8,128)(2,1)S(1)} %pad_maximum_fusion), channel_id=1, source_target_pairs={{8,0},{16,8},{24,16},{32,24},{40,32},{48,40},{56,48},{64,56},{72,6... | collective-permute-start | bytes 402440 | tf_op jit(solution)/shard_map/ppermute | solution.py:15
  23.4 0.4 all-to-all-done
  24.0 0.7 reshape.180
  24.7 10.0 %all-to-all-start.1 = ((f32[8,1,320]{2,1,0:T(1,128)}), f32[8,1,320]{2,1,0:T(1,128)S(1)}, u32[]{:S(2)}, u32[]{:S(2)}) async-start(f32[8,1,320]{2,1,0:T(1,128)} %reshape.180), calls=%async_computation.1 | async-start | bytes 24576 | tf_op jit(solution)/shard_map/all_to_all | solution.py:158
  35.1 6.3 %all-to-all-done.1 = f32[8,1,320]{2,1,0:T(1,128)S(1)} async-done(((f32[8,1,320]{2,1,0:T(1,128)}), f32[8,1,320]{2,1,0:T(1,128)S(1)}, u32[]{:S(2)}, u32[]{:S(2)}) %all-to-all-start.1) | async-done | bytes 10272 | tf_op jit(solution)/shard_map/all_to_all | solution.py:158
  41.4 0.5 broadcast.16
  41.9 0.7 reduce.1
  44.8 0.1 fusion.37
  45.3 0.8 copy-done.1
  46.1 0.3 maximum_convert_fusion.1
  46.4 0.9 multiply_convert_fusion.1
  47.3 0.1 slice_convert_fusion
  47.4 0.2 maximum_convert_fusion.3
  47.6 0.5 multiply_convert_fusion
  48.1 5.9 %shard_map.126 = (f32[16,16,272]{2,1,0:T(8,128)S(1)}, f32[16,16,272]{2,1,0:T(8,128)S(1)}, f32[16,1,128]{2,1,0:T(1,128)S(1)}) custom-call(f32[16,1,512]{2,1,0:T(1,128)S(1)} %reshape.164.ahead_ref, f32[16,1,512]{2,1,0:T(1,128)S(1)} %reshape.165.behind_ref, bf16[16,16,512]{2,1,0:T(8,128)(2,1)S(1)} %bitcast.60, bf16[16,16,512]{2,1,0:T(8,128)(2,1)S(1)} %bitcast.61), custom_call_target="tpu_custom_call" | custom-call | flops 276824064 | bytes 1081344 | tf_op jit(solution)/shard_map/pallas_call | solution.py:119
  54.0 0.4 fusion.8
  54.5 0.4 fusion.13
  54.8 0.4 fusion.16
  55.2 0.3 fusion.10
  55.8 0.1 stack.51
  56.0 0.1 stack.43
  56.2 0.1 stack.48
  57.4 0.1 copy.88
  57.6 0.1 fusion.27
  57.9 0.7 reshape.182
  58.6 3.5 %all-to-all-start.2 = ((f32[8,1,320]{2,1,0:T(1,128)}), f32[8,1,320]{2,1,0:T(1,128)S(1)}, u32[]{:S(2)}, u32[]{:S(2)}) async-start(f32[8,1,320]{2,1,0:T(1,128)} %reshape.182), calls=%async_computation.2 | async-start | bytes 24576 | tf_op jit(solution)/shard_map/all_to_all | solution.py:232
  62.2 1.0 %fusion.25 = bf16[256,256]{1,0:T(8,128)(2,1)} fusion(f32[256,258]{1,0:T(8,128)S(1)} %convert_element_type.144, f32[256]{0:T(256)S(1)} %mul.275, f32[256]{0:T(256)S(1)} %mul.272, f32[256]{0:T(256)S(1)} %mul.269), kind=kLoop, calls=%fused_computation.57 | loop fusion | flops 393216 | bytes 920576 | tf_op jit(solution)/shard_map/convert_element_type | solution.py:254
  63.1 0.7 multiply_convert_fusion.2
  64.1 4.6 %all-to-all-done.2 = f32[8,1,320]{2,1,0:T(1,128)S(1)} async-done(((f32[8,1,320]{2,1,0:T(1,128)}), f32[8,1,320]{2,1,0:T(1,128)S(1)}, u32[]{:S(2)}, u32[]{:S(2)}) %all-to-all-start.2) | async-done | bytes 10272 | tf_op jit(solution)/shard_map/all_to_all | solution.py:232
  68.7 0.7 reduce.2
  69.5 0.7 pad_maximum_fusion.5
  70.1 13.8 %all-to-all-start.3 = ((f32[64,1,72]{2,1,0:T(1,128)}), f32[64,1,72]{2,1,0:T(1,128)S(1)}, u32[]{:S(2)}, u32[]{:S(2)}) async-start(f32[64,1,72]{2,1,0:T(1,128)} %bitcast.21), calls=%async_computation.3 | async-start | bytes 65536 | tf_op jit(solution)/shard_map/all_to_all | solution.py:248
  84.0 1.0 %fusion.22 = bf16[256,256]{1,0:T(8,128)(2,1)} fusion(f32[256,258]{1,0:T(8,128)S(1)} %convert_element_type.146, f32[256]{0:T(256)S(1)} %mul.256, f32[256]{0:T(256)S(1)} %mul.253, f32[256]{0:T(256)S(1)} %mul.250), kind=kLoop, calls=%fused_computation.51 | loop fusion | flops 393216 | bytes 920576 | tf_op jit(solution)/shard_map/convert_element_type | solution.py:255
  85.0 1.0 %fusion.19 = bf16[256,256]{1,0:T(8,128)(2,1)} fusion(f32[256,258]{1,0:T(8,128)S(1)} %convert_element_type.148, f32[256]{0:T(256)S(1)} %mul.265, f32[256]{0:T(256)S(1)} %mul.262, f32[256]{0:T(256)S(1)} %mul.259), kind=kLoop, calls=%fused_computation.45 | loop fusion | flops 393216 | bytes 920576 | tf_op jit(solution)/shard_map/convert_element_type | solution.py:256
  85.9 7.3 %all-to-all-done.3 = f32[64,1,72]{2,1,0:T(1,128)S(1)} async-done(((f32[64,1,72]{2,1,0:T(1,128)}), f32[64,1,72]{2,1,0:T(1,128)S(1)}, u32[]{:S(2)}, u32[]{:S(2)}) %all-to-all-start.3) | async-done | bytes 18464 | tf_op jit(solution)/shard_map/all_to_all | solution.py:248
  93.3 0.6 slice.332
  94.0 0.7 reshape.177
  94.7 0.6 copy.93
  (94 shorter events, 5.8 us)
Async XLA Ops:
  0.6 0.8 copy-start.5
  0.6 14.9 %copy-start = (bf16[256,256]{1,0:T(8,128)(2,1)S(1)}, bf16[256,256]{1,0:T(8,128)(2,1)}, u32[]{:S(2)}) copy-start(bf16[256,256]{1,0:T(8,128)(2,1)} %param.8) | copy-start | bytes 393220
  3.0 20.8 %all-to-all-start = ((f32[64,1,72]{2,1,0:T(1,128)}), f32[64,1,72]{2,1,0:T(1,128)S(1)}, u32[]{:S(2)}, u32[]{:S(2)}) async-start(f32[64,1,72]{2,1,0:T(1,128)} %broadcast_in_dim.2), calls=%async_computation | async-start | bytes 65536 | tf_op jit(solution)/shard_map/all_to_all | solution.py:146
  15.6 0.9 copy-start.2
  16.6 3.9 %copy-start.4 = (bf16[256,256]{1,0:T(8,128)(2,1)S(1)}, bf16[256,256]{1,0:T(8,128)(2,1)}, u32[]{:S(2)}) copy-start(bf16[256,256]{1,0:T(8,128)(2,1)} %param.10) | copy-start | bytes 393220
  16.8 3.7 %copy-start.3 = (bf16[256,256]{1,0:T(8,128)(2,1)S(1)}, bf16[256,256]{1,0:T(8,128)(2,1)}, u32[]{:S(2)}) copy-start(bf16[256,256]{1,0:T(8,128)(2,1)} %param.7) | copy-start | bytes 393220
  16.8 28.0 %collective-permute-start.1 = (bf16[256,260]{1,0:T(8,128)(2,1)S(1)}, bf16[256,260]{1,0:T(8,128)(2,1)S(1)}, u32[]{:S(2)}, u32[]{:S(2)}) collective-permute-start(bf16[256,260]{1,0:T(8,128)(2,1)S(1)} %pad_maximum_fusion.1), channel_id=1, source_target_pairs={{0,8},{8,16},{16,24},{24,32},{32,40},{40,48},{48,56},{56,64},{64,7... | collective-permute-start | bytes 399368 | tf_op jit(solution)/shard_map/ppermute | solution.py:15
  20.5 0.8 slice-start
  20.5 0.9 slice-start.1
  21.5 23.5 %collective-permute-start = (bf16[256,262]{1,0:T(8,128)(2,1)S(1)}, bf16[256,262]{1,0:T(8,128)(2,1)S(1)}, u32[]{:S(2)}, u32[]{:S(2)}) collective-permute-start(bf16[256,262]{1,0:T(8,128)(2,1)S(1)} %pad_maximum_fusion), channel_id=1, source_target_pairs={{8,0},{16,8},{24,16},{32,24},{40,32},{48,40},{56,48},{64,56},{72,6... | collective-permute-start | bytes 402440 | tf_op jit(solution)/shard_map/ppermute | solution.py:15
  24.7 16.6 %all-to-all-start.1 = ((f32[8,1,320]{2,1,0:T(1,128)}), f32[8,1,320]{2,1,0:T(1,128)S(1)}, u32[]{:S(2)}, u32[]{:S(2)}) async-start(f32[8,1,320]{2,1,0:T(1,128)} %reshape.180), calls=%async_computation.1 | async-start | bytes 24576 | tf_op jit(solution)/shard_map/all_to_all | solution.py:158
  45.2 0.9 copy-start.1
  58.6 10.1 %all-to-all-start.2 = ((f32[8,1,320]{2,1,0:T(1,128)}), f32[8,1,320]{2,1,0:T(1,128)S(1)}, u32[]{:S(2)}, u32[]{:S(2)}) async-start(f32[8,1,320]{2,1,0:T(1,128)} %reshape.182), calls=%async_computation.2 | async-start | bytes 24576 | tf_op jit(solution)/shard_map/all_to_all | solution.py:232
  70.1 23.1 %all-to-all-start.3 = ((f32[64,1,72]{2,1,0:T(1,128)}), f32[64,1,72]{2,1,0:T(1,128)S(1)}, u32[]{:S(2)}, u32[]{:S(2)}) async-start(f32[64,1,72]{2,1,0:T(1,128)} %bitcast.21), calls=%async_computation.3 | async-start | bytes 65536 | tf_op jit(solution)/shard_map/all_to_all | solution.py:248
